TPU v7x, 512 devices: a whole 4x8x8 slice. The times are simulated.
512 devices in a mesh: tok: 128 (over z, y, core), rep: 4 (over x).
Axes of the slice: x: 4, y: 8, z: 8, core: 2. Of those that a mesh axis runs over, the one named last changes fastest.
Arguments:
- hidden: bfloat16 [12288, 1024], P(('tok', 'rep')), may hold values from -50 to 50
- norm_gain: bfloat16 [1024], replicated, may hold values from 0.5 to 1.5
- head_weight: bfloat16 [32128, 1024], P('tok'), may hold values from -3.75 to 3.75
- targets: int32 [12288], P(('tok', 'rep')), may hold values from 0 to 32127
- lengths: int32 [64], replicated, may hold values from 96 to 288, as said below
- padding_mask: int32 [12288], P(('tok', 'rep')), may hold values from 0 to 1, as said below
- owner_map: int32 [64], replicated, may hold values from 0 to 511, as said below
Outputs:
- logprob: float32 [12288], P(('tok', 'rep'))
- entropy: float32 [12288], P(('tok', 'rep'))
- request_table: float32 [512, 2, 2], P(('tok', 'rep'))
Inputs may be any that keep to these rules, and one draw needn't show every extreme that they name: `lengths`: lengths sum to 12288; the largest is exactly 288. `padding_mask`: the last token of every sequence is live. Each device's block of 24 tokens holds at most 18 live tokens, and the first block exactly 18. `owner_map`: each device owns at most 2 requests, and some device exactly 2.
All inputs are finite; a program needn't handle non-finite values.
Results may differ from a plain program's by a relative error of at most 0.015.
The roundings to bfloat16 on the way count: a program that leaves them out, or rounds other values in their place, can miss the bound.
Values may be sent and summed in bfloat16 or wider, within the bound.
No kernel may reach another device: no remote copies, remote signals or barrier semaphores. Data moves between devices by JAX's collectives and lax.ppermute only.
A program may use at most 64 MiB of HBM per device.

v0:
```python
import jax
import jax.numpy as jnp
from jax import lax
from jax.sharding import PartitionSpec as P

SLOTS = 2


EPSILON = 1e-06
NEG_FILL = -1e30
BLOCK_ROWS = 512


def combined_all(value, axis, join):
    pieces = jax.tree.map(lambda part: lax.all_gather(part, axis), value)
    head = jax.tree.map(lambda part: part[0], pieces)
    tail = jax.tree.map(lambda part: part[1:], pieces)
    total, _ = lax.scan(lambda total, share: (join(total, share), None), head, tail)
    return total


def slice_stats(piece_rows, piece_ids, head_weight, vocab_ids):

    def one_block(operands):
        block_rows, block_ids = operands
        logits = lax.dot_general(
            block_rows, head_weight, (((1,), (1,)), ((), ())), preferred_element_type=jnp.float32
        )
        row_top = jnp.max(logits, axis=1)
        weights = jnp.exp(logits - row_top[:, None])
        row_total = jnp.sum(weights, axis=1)
        moment = jnp.sum(weights * logits, axis=1)
        chosen = jnp.sum(jnp.where(vocab_ids[None, :] == block_ids[:, None], logits, 0.0), axis=1)
        return (row_top, row_total, moment, chosen)

    row_count = piece_rows.shape[0]
    padded = -(-row_count // BLOCK_ROWS) * BLOCK_ROWS
    blocks = padded // BLOCK_ROWS
    results = lax.map(
        one_block,
        (piece_rows.reshape(blocks, BLOCK_ROWS, -1), piece_ids.reshape(blocks, BLOCK_ROWS)),
    )
    return tuple((result_part.reshape(padded) for result_part in results))


def combine_rows(earlier, later):
    first_top, first_total, first_moment, first_chosen = earlier
    second_top, second_total, second_moment, second_chosen = later
    joint_top = jnp.maximum(first_top, second_top)
    first_scale = jnp.exp(first_top - joint_top)
    second_scale = jnp.exp(second_top - joint_top)
    return (
        joint_top,
        first_total * first_scale + second_total * second_scale,
        first_moment * first_scale + second_moment * second_scale,
        first_chosen + second_chosen,
    )


def shards(hidden, norm_gain, head_weight, targets, lengths, padding_mask, owner_map):
    rep_count = lax.axis_size("rep")
    tok_place = lax.axis_index("tok")
    rep_place = lax.axis_index("rep")
    local_rows = hidden.shape[0]
    slice_width = head_weight.shape[0]
    widened = hidden.astype(jnp.float32)
    mean_square = jnp.mean(widened * widened, axis=1)
    normed = (
        widened * lax.rsqrt(mean_square + EPSILON)[:, None] * norm_gain.astype(jnp.float32)[None, :]
    ).astype(jnp.bfloat16)
    state_norm = jnp.sqrt(mean_square)
    live_row = padding_mask == 1
    positions = jnp.arange(local_rows, dtype=jnp.int32)
    send_rows = normed[positions]
    send_targets = targets[positions]
    send_count = positions.shape[0]
    id_pair = jnp.stack([send_targets // 256, send_targets % 256], axis=1).astype(jnp.bfloat16)
    vocab_ids = tok_place * slice_width + jnp.arange(slice_width, dtype=jnp.int32)
    piece_rows = lax.all_gather(send_rows, "tok", axis=0, tiled=True)
    piece_pair = lax.all_gather(id_pair, "tok", axis=0, tiled=True)
    pair_float = piece_pair.astype(jnp.float32)
    piece_ids = (pair_float[:, 0] * 256.0 + pair_float[:, 1]).astype(jnp.int32)
    fresh_stats = slice_stats(piece_rows, piece_ids, head_weight, vocab_ids)
    partial_stats = tuple((update for update in fresh_stats))
    own_start = tok_place * send_count
    merged = combined_all(partial_stats, "tok", combine_rows)
    row_top, row_total, row_moment, row_chosen = (
        lax.dynamic_slice_in_dim(merged_part, own_start, send_count, 0) for merged_part in merged
    )
    log_total = jnp.log(row_total)
    packed_logprob = row_chosen - row_top - log_total
    packed_entropy = row_top + log_total - row_moment / row_total
    slot_index = jnp.minimum(positions, send_count - 1)
    logprob = jnp.where(live_row, packed_logprob[slot_index], 0.0)
    entropy = jnp.where(live_row, packed_entropy[slot_index], 0.0)
    token_top = row_top[slot_index]
    device_place = tok_place * rep_count + rep_place
    global_row = device_place * local_rows + positions
    seq_ends = jnp.cumsum(lengths)
    seq_count = lengths.shape[0]
    seq_ids = jnp.arange(seq_count, dtype=jnp.int32)
    sequence_of = jnp.sum((seq_ends[None, :] <= global_row[:, None]).astype(jnp.int32), axis=1)
    member = (sequence_of[:, None] == seq_ids[None, :]) & live_row[:, None]
    local_max = jnp.max(jnp.where(member, token_top[:, None], NEG_FILL), axis=0)
    local_norm = jnp.sum(
        jnp.where(global_row[:, None] == seq_ends[None, :] - 1, state_norm[:, None], 0.0), axis=0
    )
    request_max = lax.pmax(local_max, ("tok", "rep"))
    request_norm = lax.psum(local_norm, ("tok", "rep"))
    values = jnp.stack([request_max, request_norm], axis=1)
    owned_here = owner_map == device_place
    earlier_same = (owner_map[None, :] == owner_map[:, None]) & (
        seq_ids[None, :] < seq_ids[:, None]
    )
    slot_rank = jnp.sum(earlier_same.astype(jnp.int32), axis=1)
    slot_match = owned_here[:, None] & (
        slot_rank[:, None] == jnp.arange(SLOTS, dtype=jnp.int32)[None, :]
    )
    request_table = jnp.sum(jnp.where(slot_match[:, :, None], values[:, None, :], 0.0), axis=0)
    return (logprob, entropy, request_table[None])


def solution(mesh):
    return jax.shard_map(
        shards,
        mesh=mesh,
        in_specs=(
            P(("tok", "rep"), None),
            P(),
            P("tok", None),
            P(("tok", "rep")),
            P(),
            P(("tok", "rep")),
            P(),
        ),
        out_specs=(P(("tok", "rep")), P(("tok", "rep")), P(("tok", "rep"), None, None)),
        check_vma=False,
    )
```

profile of v0, /device:TPU:1, one launch (start us, length us, event | category | flops | bytes accessed | tf_op | source)
XLA Modules:
  0.0 804.8 jit_solution(18125102377911654415)
XLA Ops:
  9.8 1.2 gather_fusion
  11.9 51.9 %all-gather.1 = bf16[128,24,2]{1,2,0:T(2,128)(2,1)S(1)} all-gather(bf16[1,24,2]{1,2,0:T(2,128)(2,1)S(1)} %maximum_bitcast_fusion), channel_id=1, replica_groups=mesh['tok'=128,'rep'=4] {'tok'}, dimensions={0}, use_global_device_ids=true | all-gather | bytes 12384 | tf_op jit(solution)/shard_map/all_gather | solution.py:80
  64.2 39.4 %all-gather.12.cloned.1.call-done = bf16[3072,1024]{1,0:T(8,128)(2,1)} async-done(((bf16[24,1024]{1,0:T(8,128)(2,1)}), bf16[3072,1024]{1,0:T(8,128)(2,1)}) %all-gather.12.cloned.1.call-update) | async-done | bytes 6291472 | tf_op jit(solution)/shard_map/all_gather | solution.py:79
  103.6 13.4 %while.34 = (s32[]{:T(128)}, f32[6,512]{1,0:T(8,128)S(1)}, f32[6,512]{1,0:T(8,128)S(1)}, f32[6,512]{1,0:T(8,128)S(1)}, f32[6,512]{1,0:T(8,128)S(1)}, /*index=5*/...) while((s32[]{:T(128)}, f32[6,512]{1,0:T(8,128)S(1)}, ...), condition=%wide.region_6.7_spmd.clone, body=%wide.region_1.6_spmd.clone.sunk | while | flops 264218880 | bytes 2625641 | solution.py:39
  103.6 1.7 fusion.21
  105.9 1.7 fusion.21
  108.1 1.7 fusion.21
  110.3 1.7 fusion.21
  112.5 1.7 fusion.21
  114.8 1.7 fusion.21
  120.2 96.8 %psum.7 = f32[64,1]{0,1:T(1,128)S(1)} all-reduce(f32[64,1]{0,1:T(1,128)S(1)} %bitcast.103), channel_id=1, replica_groups=mesh['tok'=128,'rep'=4] {'tok','rep'}, use_global_device_ids=true, to_apply=%region_15.16 | all-reduce | flops 64 | bytes 512 | tf_op jit(solution)/shard_map/psum | solution.py:109
  217.4 1.4 slice-done
  219.1 60.9 %all-gather.16.cloned.1.call-done = f32[128,1,3072]{2,1,0:T(1,128)} async-done(((f32[1,1,3072]{2,1,0:T(1,128)}), f32[128,1,3072]{2,1,0:T(1,128)}) %all-gather.16.cloned.1.call-update) | async-done | bytes 1572880 | tf_op jit(solution)/shard_map/all_gather | solution.py:15
  280.0 1.4 slice-done.2
  281.4 1.4 copy.41
  282.9 79.8 %all-gather.18.cloned.1.call-done = f32[128,1,3072]{2,1,0:T(1,128)} async-done(((f32[1,1,3072]{2,1,0:T(1,128)}), f32[128,1,3072]{2,1,0:T(1,128)}) %all-gather.18.cloned.1.call-update) | async-done | bytes 1572880 | tf_op jit(solution)/shard_map/all_gather | solution.py:15
  362.6 1.4 slice-done.4
  364.0 1.5 copy.40
  365.5 79.7 %all-gather.20.cloned.1.call-done = f32[128,1,3072]{2,1,0:T(1,128)} async-done(((f32[1,1,3072]{2,1,0:T(1,128)}), f32[128,1,3072]{2,1,0:T(1,128)}) %all-gather.20.cloned.1.call-update) | async-done | bytes 1572880 | tf_op jit(solution)/shard_map/all_gather | solution.py:15
  445.2 1.4 slice-done.6
  446.6 1.5 copy.39
  448.1 250.6 %while.33 = (s32[]{:T(128)}, f32[3072]{0:T(1024)S(1)}, f32[3072]{0:T(1024)S(1)}, f32[3072]{0:T(1024)S(1)}, f32[3072]{0:T(1024)S(1)}, /*index=5*/f32[127,3072]{1,...) while((s32[]{:T(128)}, f32[3072]{0:T(1024)S(1)}, ...), condition=%wide.region_8.9_spmd, body=%wide.region_7.8_spmd.sunk | while | flops 36866 | bytes 307317 | solution.py:18
  451.0 1.0 constant_dynamic-slice_fusion.8
  470.7 1.0 constant_dynamic-slice_fusion.8
  488.5 1.0 constant_dynamic-slice_fusion.8
  508.2 1.0 constant_dynamic-slice_fusion.8
  526.0 1.0 constant_dynamic-slice_fusion.8
  545.7 1.0 constant_dynamic-slice_fusion.8
  563.4 1.0 constant_dynamic-slice_fusion.8
  583.2 1.0 constant_dynamic-slice_fusion.8
  600.9 1.0 constant_dynamic-slice_fusion.8
  701.0 96.0 %pmax.7 = f32[64,1]{0,1:T(1,128)S(1)} all-reduce(f32[64,1]{0,1:T(1,128)S(1)} %bitcast.102), channel_id=1, replica_groups=mesh['tok'=128,'rep'=4] {'tok','rep'}, use_global_device_ids=true, to_apply=%region_13.14 | all-reduce | flops 64 | bytes 512 | tf_op jit(solution)/shard_map/pmax | solution.py:108
  (873 shorter events, 249.3 us)
Async XLA Ops:
  7.2 4.0 copy-start
  7.2 96.4 %copy-start.1 = (bf16[251,1024]{1,0:T(8,128)(2,1)S(1)}, bf16[251,1024]{1,0:T(8,128)(2,1)}, u32[]{:S(2)}) copy-start(bf16[251,1024]{1,0:T(8,128)(2,1)} %param.13) | copy-start | bytes 1542148
  7.2 96.4 %all-gather.12.cloned.1.call-start = ((), (), s32[]{:S(2)}) async-start(), calls=%async_computation | async-start | bytes 6340608 | tf_op jit(solution)/shard_map/all_gather | solution.py:79
  11.0 206.4 %all-gather.14.cloned.1.call-start = ((), (), s32[]{:S(2)}) async-start(), calls=%async_computation.1 | async-start | bytes 1585152 | tf_op jit(solution)/shard_map/all_gather | solution.py:15
  103.6 16.1 %copy-start.2 = (s32[64]{0:T(128)S(1)}, s32[64]{0:T(128)}, u32[]{:S(2)}) copy-start(s32[64]{0:T(128)} %param.15) | copy-start | bytes 772
  103.6 113.6 %copy-start.4 = (s32[64]{0:T(128)S(1)}, s32[64]{0:T(128)}, u32[]{:S(2)}) copy-start(s32[64]{0:T(128)} %param.17) | copy-start | bytes 772
  103.6 113.8 %copy-start.3 = (s32[24]{0:T(128)S(1)}, s32[24]{0:T(128)}, u32[]{:S(2)}) copy-start(s32[24]{0:T(128)} %param.16) | copy-start | bytes 292
  117.6 162.4 %all-gather.16.cloned.1.call-start = ((), (), s32[]{:S(2)}) async-start(), calls=%async_computation.2 | async-start | bytes 1585152 | tf_op jit(solution)/shard_map/all_gather | solution.py:15
  118.4 244.2 %all-gather.18.cloned.1.call-start = ((), (), s32[]{:S(2)}) async-start(), calls=%async_computation.3 | async-start | bytes 1585152 | tf_op jit(solution)/shard_map/all_gather | solution.py:15
  119.0 326.1 %all-gather.20.cloned.1.call-start = ((), (), s32[]{:S(2)}) async-start(), calls=%async_computation.4 | async-start | bytes 1585152 | tf_op jit(solution)/shard_map/all_gather | solution.py:15
  217.4 1.4 slice-start
  280.0 1.4 slice-start.2
  362.6 1.4 slice-start.4
  445.2 1.4 slice-start.6
  446.6 1.5 slice-start.1
  446.6 1.5 slice-start.3
  446.6 1.5 slice-start.5
  446.6 1.5 slice-start.7
Sparse Core Ops, SparseCore 0:
  11.2 92.3 all-gather.11
  117.7 79.5 all-gather.13
  200.5 79.4 all-gather.15
  283.1 79.4 all-gather.17
  365.7 79.4 all-gather.19
where the time goes:
time: 813 us; the launch traced here: 805 us
  waiting for transfers between devices  260 us (32%)
  local copies, waits for them, and re-layouts  258 us (32%)
  blocking collectives  245 us (30%)
  between operations  14 us (2%)
  other arithmetic  10.4 us (1%)
  matrix products  10.3 us (1%)
    dynamic_slice x254, local copies, waits for them, and re-layouts, combined_all(): lax.scan(lambda total, share: (join(total, share), None), head, tail)  239 us
    all_gather x4, waiting for transfers between devices, combined_all(): pieces = jax.tree.map(lambda part: lax.all_gather(part, axis), value)  220 us
    psum x1, blocking collectives, shards(): request_norm = lax.psum(local_norm, ('tok', 'rep'))  96.8 us
    pmax x1, blocking collectives, shards(): request_max = lax.pmax(local_max, ('tok', 'rep'))  96 us
    all_gather x1, blocking collectives, shards(): piece_pair = lax.all_gather(id_pair, 'tok', axis=0, tiled=True)  51.9 us
    all_gather x1, waiting for transfers between devices, shards(): piece_rows = lax.all_gather(send_rows, 'tok', axis=0, tiled=True)  39.4 us
  transfers between devices with their start and end apart: 5, of which 4 were waited for; matrix products, arithmetic and copies ran while one was open for 1% of the time, Pallas kernels for 0%

commit v1 on v0

v1 whole, which is shorter than its diff:
```python
import jax
import jax.numpy as jnp
from jax import lax
from jax.sharding import PartitionSpec as P

SLOTS = 2


EPSILON = 1e-06
NEG_FILL = -1e30


def slice_stats(rows, ids, head_weight, vocab_ids):
    logits = lax.dot_general(
        rows, head_weight, (((2,), (1,)), ((), ())), preferred_element_type=jnp.float32
    )
    row_top = jnp.max(logits, axis=2)
    weights = jnp.exp(logits - row_top[:, :, None])
    row_total = jnp.sum(weights, axis=2)
    moment = jnp.sum(weights * logits, axis=2)
    chosen = jnp.sum(jnp.where(vocab_ids[None, None, :] == ids[:, :, None], logits, 0.0), axis=2)
    return row_top, row_total, moment, chosen


def shards(hidden, norm_gain, head_weight, targets, lengths, padding_mask, owner_map):
    tok_count = lax.axis_size("tok")
    rep_count = lax.axis_size("rep")
    tok_place = lax.axis_index("tok")
    rep_place = lax.axis_index("rep")
    local_rows, width = hidden.shape
    slice_width = head_weight.shape[0]
    seq_count = lengths.shape[0]

    widened = hidden.astype(jnp.float32)
    mean_square = jnp.mean(widened * widened, axis=1)
    normed = (
        widened * lax.rsqrt(mean_square + EPSILON)[:, None] * norm_gain.astype(jnp.float32)[None, :]
    ).astype(jnp.bfloat16)
    state_norm = jnp.sqrt(mean_square)
    live_row = padding_mask == 1

    meta = jnp.zeros((width,), jnp.float32)
    meta = meta.at[0:local_rows].set((targets // 256).astype(jnp.float32))
    meta = meta.at[local_rows:2 * local_rows].set((targets % 256).astype(jnp.float32))
    meta = meta.at[2 * local_rows:3 * local_rows].set(live_row.astype(jnp.float32))
    packet = jnp.concatenate([normed, meta.astype(jnp.bfloat16)[None, :]], axis=0)
    gathered = lax.all_gather(packet, "tok", axis=0)

    meta_all = gathered[:, local_rows, :].astype(jnp.float32)
    piece_ids = (meta_all[:, 0:local_rows] * 256.0 + meta_all[:, local_rows:2 * local_rows]).astype(jnp.int32)
    piece_live = meta_all[:, 2 * local_rows:3 * local_rows] > 0.5
    vocab_ids = tok_place * slice_width + jnp.arange(slice_width, dtype=jnp.int32)
    ids_full = jnp.concatenate([piece_ids, jnp.zeros((tok_count, 1), jnp.int32)], axis=1)
    top_p, total_p, moment_p, chosen_p = (
        part[:, :local_rows] for part in slice_stats(gathered, ids_full, head_weight, vocab_ids)
    )

    seq_ends = jnp.cumsum(lengths)
    seq_ids = jnp.arange(seq_count, dtype=jnp.int32)
    block_of = jnp.arange(tok_count, dtype=jnp.int32) * rep_count + rep_place
    piece_rows = block_of[:, None] * local_rows + jnp.arange(local_rows, dtype=jnp.int32)[None, :]
    piece_seq = jnp.sum((seq_ends[None, None, :] <= piece_rows[:, :, None]).astype(jnp.int32), axis=2)
    member = (piece_seq[:, :, None] == seq_ids[None, None, :]) & piece_live[:, :, None]
    part_max = jnp.max(jnp.where(member, top_p[:, :, None], NEG_FILL), axis=(0, 1))
    device_place = tok_place * rep_count + rep_place
    own_rows = device_place * local_rows + jnp.arange(local_rows, dtype=jnp.int32)
    part_norm = jnp.sum(
        jnp.where(own_rows[:, None] == seq_ends[None, :] - 1, state_norm[:, None], 0.0), axis=0
    )

    earlier_same = (owner_map[None, :] == owner_map[:, None]) & (seq_ids[None, :] < seq_ids[:, None])
    slot_rank = jnp.sum(earlier_same.astype(jnp.int32), axis=1)
    device_ids = jnp.arange(tok_count * rep_count, dtype=jnp.int32)
    slot_hot = (owner_map[:, None, None] == device_ids[None, :, None]) & (
        slot_rank[:, None, None] == jnp.arange(SLOTS, dtype=jnp.int32)[None, None, :]
    )
    req_max = jnp.max(jnp.where(slot_hot, part_max[:, None, None], NEG_FILL), axis=0)
    req_norm = jnp.sum(jnp.where(slot_hot, part_norm[:, None, None], 0.0), axis=0)
    req = jnp.stack([req_max, req_norm], axis=2).reshape(tok_count, rep_count * SLOTS * 2)

    stats = jnp.stack([top_p, total_p, moment_p, chosen_p], axis=2).reshape(tok_count, local_rows * 4)
    outgoing = jnp.concatenate([stats, req], axis=1)
    incoming = lax.all_to_all(outgoing, "tok", 0, 0, tiled=True)

    in_stats = incoming[:, : local_rows * 4].reshape(tok_count, local_rows, 4)
    tops = in_stats[:, :, 0]
    row_top = jnp.max(tops, axis=0)
    scale = jnp.exp(tops - row_top[None, :])
    row_total = jnp.sum(in_stats[:, :, 1] * scale, axis=0)
    row_moment = jnp.sum(in_stats[:, :, 2] * scale, axis=0)
    row_chosen = jnp.sum(in_stats[:, :, 3], axis=0)
    log_total = jnp.log(row_total)
    logprob = jnp.where(live_row, row_chosen - row_top - log_total, 0.0)
    entropy = jnp.where(live_row, row_top + log_total - row_moment / row_total, 0.0)

    in_req = incoming[:, local_rows * 4:].reshape(tok_count, rep_count, SLOTS, 2)
    rep_max = jnp.max(in_req[..., 0], axis=0)
    rep_norm = jnp.sum(in_req[..., 1], axis=0)
    rep_pair = jnp.stack([rep_max, rep_norm], axis=2)
    got = lax.all_to_all(rep_pair, "rep", 0, 0, tiled=True)
    final_max = jnp.max(got[..., 0], axis=0)
    final_norm = jnp.sum(got[..., 1], axis=0)
    has_slot = jnp.any(slot_hot[:, device_place, :], axis=0)
    request_table = jnp.where(
        has_slot[:, None], jnp.stack([final_max, final_norm], axis=1), 0.0
    )
    return (logprob, entropy, request_table[None])


def solution(mesh):
    return jax.shard_map(
        shards,
        mesh=mesh,
        in_specs=(
            P(("tok", "rep"), None),
            P(),
            P("tok", None),
            P(("tok", "rep")),
            P(),
            P(("tok", "rep")),
            P(),
        ),
        out_specs=(P(("tok", "rep")), P(("tok", "rep")), P(("tok", "rep"), None, None)),
        check_vma=False,
    )
```

time: 813 us -> 163 us (0.20); the launches traced: 805 us -> 163 us
  local copies, waits for them, and re-layouts: 258 us -> 6.5 us
  blocking collectives: 245 us -> 0 us
  waiting for transfers between devices: 260 us -> 105 us
  starting transfers between devices: 0.21 us -> 13.3 us
    dynamic_slice x260 -> x0, local copies, waits for them, and re-layouts: 239 us -> none  [the longest x254 239 us: combined_all(): lax.scan(lambda total, share: (join(total, share), None), head, tail)]
    all_gather x5 -> x1, waiting for transfers between devices: 260 us -> 91.2 us  [shards(): gathered = lax.all_gather(packet, 'tok', axis=0)]
    psum x1 -> x0, blocking collectives: 96.8 us -> none  [shards(): request_norm = lax.psum(local_norm, ('tok', 'rep'))]
    pmax x1 -> x0, blocking collectives: 96 us -> none  [shards(): request_max = lax.pmax(local_max, ('tok', 'rep'))]
    all_gather x1 -> x0, blocking collectives: 51.9 us -> none  [shards(): piece_pair = lax.all_gather(id_pair, 'tok', axis=0, tiled=True)]
    all_to_all x0 -> x2, waiting for transfers between devices: none -> 14.2 us  [the longest x1 11.1 us: shards(): incoming = lax.all_to_all(outgoing, 'tok', 0, 0, tiled=True)]
    all_to_all x0 -> x2, starting transfers between devices: none -> 13.2 us  [the longest x1 9.27 us: shards(): incoming = lax.all_to_all(outgoing, 'tok', 0, 0, tiled=True)]
  transfers between devices with their start and end apart: 5 -> 3, of which waited for: 4 -> 3; matrix products, arithmetic and copies ran while one was open for 1% -> 3% of each run, Pallas kernels for 0% -> 0%
where the time goes in v1:
time: 163 us
  waiting for transfers between devices  105 us (64%)
  between operations  14.3 us (9%)
  starting transfers between devices  13.3 us (8%)
  other arithmetic  12.5 us (8%)
  matrix products  11 us (7%)
  local copies, waits for them, and re-layouts  6.5 us (4%)
    all_gather x1, waiting for transfers between devices, shards(): gathered = lax.all_gather(packet, 'tok', axis=0)  91.2 us
    all_to_all x1, waiting for transfers between devices, shards(): incoming = lax.all_to_all(outgoing, 'tok', 0, 0, tiled=True)  11.1 us
    dot_general x1, matrix products, slice_stats(): lax.dot_general(rows, head_weight, (((2,), (1,)), ((), ())), preferred_el...  11 us
    all_to_all x1, starting transfers between devices, shards(): incoming = lax.all_to_all(outgoing, 'tok', 0, 0, tiled=True)  9.27 us
    all_to_all x1, starting transfers between devices, shards(): got = lax.all_to_all(rep_pair, 'rep', 0, 0, tiled=True)  3.97 us
  transfers between devices with their start and end apart: 3, of which 3 were waited for; matrix products, arithmetic and copies ran while one was open for 3% of the time, Pallas kernels for 0%

profile of v1, /device:TPU:1, one launch (start us, length us, event | category | flops | bytes accessed | tf_op | source)
XLA Modules:
  0.0 163.0 jit_solution(6672535148514706981)
XLA Ops:
  7.2 1.0 fusion.5
  8.2 0.7 convert_element_type.37
  8.9 0.7 fusion.12
  9.6 0.7 fusion.11
  10.3 0.7 constant_dynamic-update-slice_fusion
  11.1 0.9 fusion.7
  11.9 0.6 maximum_bitcast_fusion
  12.6 0.7 copy.53
  13.6 0.9 convert_reduce_fusion.1
  14.6 0.2 convert_reduce_fusion
  14.8 0.7 iota_compare_fusion.1
  15.6 91.2 %all-gather.4.cloned.1.call-done = bf16[128,25,1024]{2,1,0:T(8,128)(2,1)} async-done(((bf16[1,25,1024]{2,1,0:T(8,128)(2,1)}), bf16[128,25,1024]{2,1,0:T(8,128)(2,1)}) %all-gather.4.cloned.1.call-update) | async-done | bytes 6553616 | tf_op jit(solution)/shard_map/all_gather | solution.py:47
  106.8 2.0 %slice.110 = bf16[128,1,1024]{2,1,0:T(2,128)(2,1)S(1)} slice(bf16[128,25,1024]{2,1,0:T(8,128)(2,1)} %all-gather.4.cloned.1.call-done), slice={[0:128], [24:25], [0:1024]} | slice | bytes 524288 | tf_op jit(solution)/shard_map/slice | solution.py:49
  108.8 0.4 copy.65
  109.3 11.0 %fusion.14 = (f32[128,25]{0,1:T(8,128)S(1)}, f32[128,25,251]{2,0,1:T(8,128)S(1)}) fusion(bf16[251,1024]{1,0:T(8,128)(2,1)S(1)} %copy-done, bf16[128,25,1024]{2,1,0:T(8,128)(2,1)} %all-gather.4.cloned.1.call-done), kind=kOutput, calls=%fused_computation.65 | convolution fusion | flops 1645753600 | bytes 10293248 | tf_op jit(solution)/shard_map/dot_general | solution.py:14
  120.3 2.9 %fusion.2 = (f32[128,25]{0,1:T(8,128)S(1)}, f32[128,25]{0,1:T(8,128)S(1)}, f32[128,25]{0,1:T(8,128)S(1)}) fusion(f32[128,25,251]{2,0,1:T(8,128)S(1)} %get-tuple-element.74, f32[128,25]{0,1:T(8,128)S(1)} %get-tuple-element.73, s32[128,25]{0,1:T(8,128)S(1)} %concatenate.23, s32[251]{0:T(256)S(1)} %iota_add_fusion.1), kind=kLoop, calls=%fused_computation.5 | loop fusion | flops 5612800 | bytes 3277804 | tf_op jit(solution)/shard_map/reduce_sum | solution.py:19
  123.2 0.3 select_reduce_fusion.1
  123.5 0.1 select_reduce_fusion.3
  123.7 0.3 copy.54
  124.0 0.7 reshape.260
  124.8 0.7 copy.56
  125.5 9.3 %all-to-all-start = ((f32[128,1,112]{2,1,0:T(1,128)}), f32[128,1,112]{2,1,0:T(1,128)S(1)}, u32[]{:S(2)}, u32[]{:S(2)}) async-start(f32[128,1,112]{2,1,0:T(1,128)} %copy.56), calls=%async_computation | async-start | bytes 131072 | tf_op jit(solution)/shard_map/all_to_all | solution.py:83
  134.9 0.2 dynamic-slice_reduce_fusion
  135.1 11.1 %all-to-all-done = f32[128,1,112]{2,1,0:T(1,128)S(1)} async-done(((f32[128,1,112]{2,1,0:T(1,128)}), f32[128,1,112]{2,1,0:T(1,128)S(1)}, u32[]{:S(2)}, u32[]{:S(2)}) %all-to-all-start) | async-done | bytes 57376 | tf_op jit(solution)/shard_map/all_to_all | solution.py:83
  146.3 0.1 slice_reduce_fusion.2
  146.6 0.7 copy.62
  147.3 4.0 %all-to-all-start.1 = ((f32[4,2,2]{1,2,0:T(2,128)}), f32[4,2,2]{1,2,0:T(2,128)S(1)}, u32[]{:S(2)}, u32[]{:S(2)}) async-start(f32[4,2,2]{1,2,0:T(2,128)} %copy.62), calls=%async_computation.1 | async-start | bytes 8192 | tf_op jit(solution)/shard_map/all_to_all | solution.py:100
  151.3 0.3 fusion.13
  151.7 0.2 multiply_reduce_fusion.1
  151.8 0.5 subtract_select_fusion
  152.4 3.0 %all-to-all-done.1 = f32[4,2,2]{1,2,0:T(2,128)S(1)} async-done(((f32[4,2,2]{1,2,0:T(2,128)}), f32[4,2,2]{1,2,0:T(2,128)S(1)}, u32[]{:S(2)}, u32[]{:S(2)}) %all-to-all-start.1) | async-done | bytes 96 | tf_op jit(solution)/shard_map/all_to_all | solution.py:100
  155.5 0.6 copy.63
  (41 shorter events, 1.2 us)
Async XLA Ops:
  7.2 102.1 %copy-start = (bf16[251,1024]{1,0:T(8,128)(2,1)S(1)}, bf16[251,1024]{1,0:T(8,128)(2,1)}, u32[]{:S(2)}) copy-start(bf16[251,1024]{1,0:T(8,128)(2,1)} %param.15) | copy-start | bytes 1542148
  7.2 99.6 %all-gather.4.cloned.1.call-start = ((), (), s32[]{:S(2)}) async-start(), calls=%async_computation.2 | async-start | bytes 8454144 | tf_op jit(solution)/shard_map/all_gather | solution.py:47
  120.3 31.5 %copy-start.1 = (s32[24]{0:T(128)S(1)}, s32[24]{0:T(128)}, u32[]{:S(2)}) copy-start(s32[24]{0:T(128)} %param.18) | copy-start | bytes 292
  125.5 20.7 %all-to-all-start = ((f32[128,1,112]{2,1,0:T(1,128)}), f32[128,1,112]{2,1,0:T(1,128)S(1)}, u32[]{:S(2)}, u32[]{:S(2)}) async-start(f32[128,1,112]{2,1,0:T(1,128)} %copy.56), calls=%async_computation | async-start | bytes 131072 | tf_op jit(solution)/shard_map/all_to_all | solution.py:83
  147.3 8.1 %all-to-all-start.1 = ((f32[4,2,2]{1,2,0:T(2,128)}), f32[4,2,2]{1,2,0:T(2,128)S(1)}, u32[]{:S(2)}, u32[]{:S(2)}) async-start(f32[4,2,2]{1,2,0:T(2,128)} %copy.62), calls=%async_computation.1 | async-start | bytes 8192 | tf_op jit(solution)/shard_map/all_to_all | solution.py:100
Sparse Core Ops, SparseCore 0:
  12.7 94.0 all-gather.3

commit v2 on v1

v2 whole, which is shorter than its diff:
```python
import jax
import jax.numpy as jnp
import numpy as np
from jax import lax
from jax.sharding import Mesh
from jax.sharding import PartitionSpec as P

SLOTS = 2


EPSILON = 1e-06
NEG_FILL = -1e30
AXES = ("z", "y", "c", "x")
PLANE = ("z", "y")
CHIP = ("c", "x")


def slice_stats(rows, ids, vocab, vocab_ids):
    logits = lax.dot_general(
        rows, vocab, (((rows.ndim - 1,), (1,)), ((), ())), preferred_element_type=jnp.float32
    )
    row_top = jnp.max(logits, axis=-1)
    weights = jnp.exp(logits - row_top[..., None])
    row_total = jnp.sum(weights, axis=-1)
    moment = jnp.sum(weights * logits, axis=-1)
    chosen = jnp.sum(jnp.where(vocab_ids == ids[..., None], logits, 0.0), axis=-1)
    return row_top, row_total, moment, chosen


def gather_by_sum(block, axis):
    count = lax.axis_size(axis)
    place = lax.axis_index(axis)
    buffer = jnp.zeros((count,) + block.shape, block.dtype)
    buffer = lax.dynamic_update_slice(buffer, block[None], (place,) + (0,) * block.ndim)
    return lax.psum(buffer, axis)


def shards(hidden, norm_gain, head_weight, targets, lengths, padding_mask, owner_map):
    nz, ny, nc, nx = (lax.axis_size(a) for a in AXES)
    z, y, c, x = (lax.axis_index(a) for a in AXES)
    plane_count = nz * ny
    chip_count = nc * nx
    local_rows, width = hidden.shape
    slice_width = head_weight.shape[0]
    seq_count = lengths.shape[0]
    tok_place = (z * ny + y) * nc + c
    device_place = tok_place * nx + x

    widened = hidden.astype(jnp.float32)
    mean_square = jnp.mean(widened * widened, axis=1)
    normed = (
        widened * lax.rsqrt(mean_square + EPSILON)[:, None] * norm_gain.astype(jnp.float32)[None, :]
    ).astype(jnp.bfloat16)
    state_norm = jnp.sqrt(mean_square)
    live_row = padding_mask == 1

    other_head = lax.ppermute(head_weight, "c", [(i, (i + 1) % nc) for i in range(nc)])
    other_place = (z * ny + y) * nc + (c + nc - 1) % nc
    vocab = jnp.concatenate([head_weight, other_head], axis=0)
    vocab_ids = jnp.concatenate(
        [
            tok_place * slice_width + jnp.arange(slice_width, dtype=jnp.int32),
            other_place * slice_width + jnp.arange(slice_width, dtype=jnp.int32),
        ]
    )

    meta = jnp.zeros((width,), jnp.float32)
    meta = meta.at[0:local_rows].set((targets // 256).astype(jnp.float32))
    meta = meta.at[local_rows:2 * local_rows].set((targets % 256).astype(jnp.float32))
    meta = meta.at[2 * local_rows:3 * local_rows].set(live_row.astype(jnp.float32))
    packet = jnp.concatenate([normed, meta.astype(jnp.bfloat16)[None, :]], axis=0)
    gathered = gather_by_sum(gather_by_sum(packet, "y"), "z")
    gathered = gathered.reshape(plane_count, local_rows + 1, width)

    meta_all = gathered[:, local_rows, :].astype(jnp.float32)
    piece_ids = (meta_all[:, 0:local_rows] * 256.0 + meta_all[:, local_rows:2 * local_rows]).astype(jnp.int32)
    piece_live = meta_all[:, 2 * local_rows:3 * local_rows] > 0.5
    ids_full = jnp.concatenate([piece_ids, jnp.zeros((plane_count, 1), jnp.int32)], axis=1)
    top_p, total_p, moment_p, chosen_p = (
        part[:, :local_rows] for part in slice_stats(gathered, ids_full, vocab, vocab_ids)
    )

    seq_ends = jnp.cumsum(lengths)
    seq_ids = jnp.arange(seq_count, dtype=jnp.int32)
    block_of = (jnp.arange(plane_count, dtype=jnp.int32) * nc + c) * nx + x
    piece_rows = block_of[:, None] * local_rows + jnp.arange(local_rows, dtype=jnp.int32)[None, :]
    piece_seq = jnp.sum((seq_ends[None, None, :] <= piece_rows[:, :, None]).astype(jnp.int32), axis=2)
    member = (piece_seq[:, :, None] == seq_ids[None, None, :]) & piece_live[:, :, None]
    part_max = jnp.max(jnp.where(member, top_p[:, :, None], NEG_FILL), axis=(0, 1))
    own_rows = device_place * local_rows + jnp.arange(local_rows, dtype=jnp.int32)
    part_norm = jnp.sum(
        jnp.where(own_rows[:, None] == seq_ends[None, :] - 1, state_norm[:, None], 0.0), axis=0
    )

    earlier_same = (owner_map[None, :] == owner_map[:, None]) & (seq_ids[None, :] < seq_ids[:, None])
    slot_rank = jnp.sum(earlier_same.astype(jnp.int32), axis=1)
    device_ids = jnp.arange(plane_count * chip_count, dtype=jnp.int32)
    slot_hot = (owner_map[:, None, None] == device_ids[None, :, None]) & (
        slot_rank[:, None, None] == jnp.arange(SLOTS, dtype=jnp.int32)[None, None, :]
    )
    req_max = jnp.max(jnp.where(slot_hot, part_max[:, None, None], NEG_FILL), axis=0)
    req_norm = jnp.sum(jnp.where(slot_hot, part_norm[:, None, None], 0.0), axis=0)
    req = jnp.stack([req_max, req_norm], axis=2).reshape(plane_count, chip_count * SLOTS * 2)

    stats = jnp.stack([top_p, total_p, moment_p, chosen_p], axis=2).reshape(plane_count, local_rows * 4)
    outgoing = jnp.concatenate([stats, req], axis=1)
    incoming = lax.all_to_all(outgoing, PLANE, 0, 0, tiled=True)

    in_stats = incoming[:, : local_rows * 4].reshape(plane_count, local_rows, 4)
    tops = in_stats[:, :, 0]
    row_top = jnp.max(tops, axis=0)
    scale = jnp.exp(tops - row_top[None, :])
    row_total = jnp.sum(in_stats[:, :, 1] * scale, axis=0)
    row_moment = jnp.sum(in_stats[:, :, 2] * scale, axis=0)
    row_chosen = jnp.sum(in_stats[:, :, 3], axis=0)
    log_total = jnp.log(row_total)
    logprob = jnp.where(live_row, row_chosen - row_top - log_total, 0.0)
    entropy = jnp.where(live_row, row_top + log_total - row_moment / row_total, 0.0)

    in_req = incoming[:, local_rows * 4:].reshape(plane_count, chip_count, SLOTS, 2)
    chip_max = jnp.max(in_req[..., 0], axis=0)
    chip_norm = jnp.sum(in_req[..., 1], axis=0)
    chip_pair = jnp.stack([chip_max, chip_norm], axis=2)
    got = lax.all_to_all(chip_pair, CHIP, 0, 0, tiled=True)
    final_max = jnp.max(got[..., 0], axis=0)
    final_norm = jnp.sum(got[..., 1], axis=0)
    has_slot = jnp.any(slot_hot[:, device_place, :], axis=0)
    request_table = jnp.where(
        has_slot[:, None], jnp.stack([final_max, final_norm], axis=1), 0.0
    )
    return (logprob, entropy, request_table[None])


def solution(mesh):
    tok_count, rep_count = mesh.devices.shape
    cores = 2
    side = int(round((tok_count // cores) ** 0.5))
    fine = Mesh(np.asarray(mesh.devices).reshape(side, tok_count // cores // side, cores, rep_count), AXES)
    tokens = P(AXES)
    return jax.shard_map(
        shards,
        mesh=fine,
        in_specs=(
            P(AXES, None),
            P(),
            P(("z", "y", "c"), None),
            tokens,
            P(),
            tokens,
            P(),
        ),
        out_specs=(tokens, tokens, P(AXES, None, None)),
        check_vma=False,
    )
```

time: 163 us -> 253 us (1.55)
  waiting for transfers between devices: 105 us -> 187 us
  starting transfers between devices: 13.3 us -> 23.7 us
  matrix products: 11 us -> 4.21 us
  local copies, waits for them, and re-layouts: 6.5 us -> 11.1 us
    psum x0 -> x2, waiting for transfers between devices: none -> 172 us  [gather_by_sum(): return lax.psum(buffer, axis)]
    all_gather x1 -> x0, waiting for transfers between devices: 91.2 us -> none  [shards(): gathered = lax.all_gather(packet, 'tok', axis=0)]
    ppermute x0 -> x1, starting transfers between devices: none -> 7.37 us  [shards(): lax.ppermute(head_weight, 'c', [(i, (i + 1) % nc) for i in range(nc)])]
    dot_general x1, matrix products: 11 us -> 4.21 us  [slice_stats(): lax.dot_general(rows, vocab, (((rows.ndim - 1,), (1,)), ((), ())), prefer...]
    all_to_all x2, starting transfers between devices: 13.2 us -> 16.2 us  [the longest x1 9.85 us: shards(): incoming = lax.all_to_all(outgoing, PLANE, 0, 0, tiled=True)]
    unnamed x6 -> x14, local copies, waits for them, and re-layouts: 1.11 us -> 3.78 us
  transfers between devices with their start and end apart: 3 -> 5, of which waited for: 3 -> 4; matrix products, arithmetic and copies ran while one was open for 3% -> 2% of each run, Pallas kernels for 0% -> 0%
where the time goes in v2:
time: 253 us
  waiting for transfers between devices  187 us (74%)
  starting transfers between devices  23.7 us (9%)
  between operations  14.4 us (6%)
  other arithmetic  12.4 us (5%)
  local copies, waits for them, and re-layouts  11.1 us (4%)
  matrix products  4.21 us (2%)
    psum x2, waiting for transfers between devices, gather_by_sum(): return lax.psum(buffer, axis)  172 us
    all_to_all x1, waiting for transfers between devices, shards(): incoming = lax.all_to_all(outgoing, PLANE, 0, 0, tiled=True)  10.5 us
    all_to_all x1, starting transfers between devices, shards(): incoming = lax.all_to_all(outgoing, PLANE, 0, 0, tiled=True)  9.85 us
    ppermute x1, starting transfers between devices, shards(): lax.ppermute(head_weight, 'c', [(i, (i + 1) % nc) for i in range(nc)])  7.37 us
    all_to_all x1, starting transfers between devices, shards(): got = lax.all_to_all(chip_pair, CHIP, 0, 0, tiled=True)  6.39 us
  transfers between devices with their start and end apart: 5, of which 4 were waited for; matrix products, arithmetic and copies ran while one was open for 2% of the time, Pallas kernels for 0%

profile of v2, /device:TPU:1, one launch (start us, length us, event | category | flops | bytes accessed | tf_op | source)
XLA Modules:
  0.0 252.8 jit_solution(15617818416284887751)
XLA Ops:
  7.2 0.7 fusion.13
  7.9 0.7 fusion.12
  8.6 0.7 constant_dynamic-update-slice_fusion
  9.4 0.7 convert_element_type.37
  10.1 0.9 fusion.6
  11.0 0.9 fusion.8
  12.0 2.1 dynamic_update_slice.8
  14.1 0.7 copy-done.1
  15.0 79.2 %all-reduce.5.cloned.1.call-done = bf16[1,8,25,1024]{3,1,0,2:T(8,128)(2,1)} async-done(((bf16[1,8,25,1024]{3,1,0,2:T(8,128)(2,1)}), bf16[1,8,25,1024]{3,1,0,2:T(8,128)(2,1)}) %all-reduce.5.cloned.1.call-update) | async-done | bytes 409616 | tf_op jit(solution)/shard_map/psum | solution.py:35
  94.2 0.4 broadcast_in_dim.109
  94.6 0.6 copy-done.2
  95.2 1.7 copy-done
  97.0 7.4 %collective-permute-start = (bf16[251,1024]{1,0:T(8,128)(2,1)}, bf16[251,1024]{1,0:T(8,128)(2,1)}, u32[]{:S(2)}, u32[]{:S(2)}) collective-permute-start(bf16[251,1024]{1,0:T(8,128)(2,1)} %param.15), channel_id=1, source_target_pairs={{0,4},{4,0},{1,5},{5,1},{2,6},{6,2},{3,7},{7,3},{8,12},{12,8},{9,1... | collective-permute-start | bytes 1542152 | tf_op jit(solution)/shard_map/ppermute | solution.py:57
  105.2 1.4 convert_reduce_fusion
  106.7 93.2 %all-reduce.7.cloned.1.call-done = bf16[64,25,1024]{2,0,1:T(8,128)(2,1)} async-done(((bf16[64,25,1024]{2,0,1:T(8,128)(2,1)}), bf16[64,25,1024]{2,0,1:T(8,128)(2,1)}) %all-reduce.7.cloned.1.call-update) | async-done | bytes 3276816 | tf_op jit(solution)/shard_map/psum | solution.py:35
  199.9 0.9 fusion.5
  201.0 4.2 %fusion.16 = (f32[64,25]{0,1:T(8,128)S(1)}, f32[64,25,502]{2,0,1:T(8,128)S(1)}) fusion(bf16[64,25,1024]{2,0,1:T(8,128)(2,1)} %all-reduce.7.cloned.1.call-done, bf16[251,1024]{1,0:T(8,128)(2,1)} %collective-permute-done, bf16[251,1024]{1,0:T(8,128)(2,1)} %param.15), kind=kOutput, calls=%fused_computation.71 | convolution fusion | flops 1647811328 | bytes 7524096 | tf_op jit(solution)/shard_map/dot_general | solution.py:19
  205.3 0.9 select_reduce_fusion.1
  206.3 1.0 copy.42
  207.4 1.7 reshape.263
  209.3 1.9 fusion
  211.3 0.7 copy.44
  211.9 9.8 %all-to-all-start = ((f32[64,1,128]{2,1,0:T(1,128)}), f32[64,1,128]{2,1,0:T(1,128)S(1)}, u32[]{:S(2)}, u32[]{:S(2)}) async-start(f32[64,1,128]{2,1,0:T(1,128)} %copy.44), calls=%async_computation | async-start | bytes 65536 | tf_op jit(solution)/shard_map/all_to_all | solution.py:107
  221.9 0.2 dynamic-slice_reduce_fusion
  222.1 10.5 %all-to-all-done = f32[64,1,128]{2,1,0:T(1,128)S(1)} async-done(((f32[64,1,128]{2,1,0:T(1,128)}), f32[64,1,128]{2,1,0:T(1,128)S(1)}, u32[]{:S(2)}, u32[]{:S(2)}) %all-to-all-start) | async-done | bytes 32800 | tf_op jit(solution)/shard_map/all_to_all | solution.py:107
  232.7 0.3 fusion.15
  233.3 0.7 copy.50
  234.0 6.4 %all-to-all-start.1 = ((f32[8,2,2]{1,2,0:T(2,128)}), f32[8,2,2]{1,2,0:T(2,128)S(1)}, u32[]{:S(2)}, u32[]{:S(2)}) async-start(f32[8,2,2]{1,2,0:T(2,128)} %copy.50), calls=%async_computation.1 | async-start | bytes 16384 | tf_op jit(solution)/shard_map/all_to_all | solution.py:124
  240.5 0.2 multiply_reduce_fusion.1
  240.7 0.5 subtract_select_fusion
  241.2 4.0 %all-to-all-done.1 = f32[8,2,2]{1,2,0:T(2,128)S(1)} async-done(((f32[8,2,2]{1,2,0:T(2,128)}), f32[8,2,2]{1,2,0:T(2,128)S(1)}, u32[]{:S(2)}, u32[]{:S(2)}) %all-to-all-start.1) | async-done | bytes 160 | tf_op jit(solution)/shard_map/all_to_all | solution.py:124
  245.3 0.7 copy.51
  (60 shorter events, 2.4 us)
Async XLA Ops:
  7.2 87.0 %all-reduce.5.cloned.1.call-start = ((), (), s32[]{:S(2)}) async-start(), calls=%async_computation.2 | async-start | bytes 819200 | tf_op jit(solution)/shard_map/psum | solution.py:35
  14.1 0.8 copy-start.1
  14.9 185.0 %all-reduce.7.cloned.1.call-start = ((), (), s32[]{:S(2)}) async-start(), calls=%async_computation.3 | async-start | bytes 6553600 | tf_op jit(solution)/shard_map/psum | solution.py:35
  15.0 89.4 %copy-start.3 = (s32[64]{0:T(128)S(1)}, s32[64]{0:T(128)}, u32[]{:S(2)}) copy-start(s32[64]{0:T(128)} %param.17) | copy-start | bytes 772
  15.0 89.9 %copy-start.4 = (s32[64]{0:T(128)S(1)}, s32[64]{0:T(128)}, u32[]{:S(2)}) copy-start(s32[64]{0:T(128)} %param.19) | copy-start | bytes 772
  94.2 1.0 copy-start.2
  95.2 1.7 copy-start
  97.0 104.0 %collective-permute-start = (bf16[251,1024]{1,0:T(8,128)(2,1)}, bf16[251,1024]{1,0:T(8,128)(2,1)}, u32[]{:S(2)}, u32[]{:S(2)}) collective-permute-start(bf16[251,1024]{1,0:T(8,128)(2,1)} %param.15), channel_id=1, source_target_pairs={{0,4},{4,0},{1,5},{5,1},{2,6},{6,2},{3,7},{7,3},{8,12},{12,8},{9,1... | collective-permute-start | bytes 1542152 | tf_op jit(solution)/shard_map/ppermute | solution.py:57
  205.2 35.5 %copy-start.5 = (s32[24]{0:T(128)S(1)}, s32[24]{0:T(128)}, u32[]{:S(2)}) copy-start(s32[24]{0:T(128)} %param.18) | copy-start | bytes 292
  211.9 20.7 %all-to-all-start = ((f32[64,1,128]{2,1,0:T(1,128)}), f32[64,1,128]{2,1,0:T(1,128)S(1)}, u32[]{:S(2)}, u32[]{:S(2)}) async-start(f32[64,1,128]{2,1,0:T(1,128)} %copy.44), calls=%async_computation | async-start | bytes 65536 | tf_op jit(solution)/shard_map/all_to_all | solution.py:107
  234.0 11.3 %all-to-all-start.1 = ((f32[8,2,2]{1,2,0:T(2,128)}), f32[8,2,2]{1,2,0:T(2,128)S(1)}, u32[]{:S(2)}, u32[]{:S(2)}) async-start(f32[8,2,2]{1,2,0:T(2,128)} %copy.50), calls=%async_computation.1 | async-start | bytes 16384 | tf_op jit(solution)/shard_map/all_to_all | solution.py:124
Sparse Core Ops, SparseCore 0:
  15.0 79.1 all-reduce.4
  97.1 102.7 all-reduce.6

commit v3 on v1

--- a/solution.py
+++ b/solution.py
@@ -12,13 +12,13 @@
 
 def slice_stats(rows, ids, head_weight, vocab_ids):
     logits = lax.dot_general(
-        rows, head_weight, (((2,), (1,)), ((), ())), preferred_element_type=jnp.float32
+        head_weight, rows, (((1,), (1,)), ((), ())), preferred_element_type=jnp.float32
     )
-    row_top = jnp.max(logits, axis=2)
-    weights = jnp.exp(logits - row_top[:, :, None])
-    row_total = jnp.sum(weights, axis=2)
-    moment = jnp.sum(weights * logits, axis=2)
-    chosen = jnp.sum(jnp.where(vocab_ids[None, None, :] == ids[:, :, None], logits, 0.0), axis=2)
+    row_top = jnp.max(logits, axis=0)
+    weights = jnp.exp(logits - row_top[None, :])
+    row_total = jnp.sum(weights, axis=0)
+    moment = jnp.sum(weights * logits, axis=0)
+    chosen = jnp.sum(jnp.where(vocab_ids[:, None] == ids[None, :], logits, 0.0), axis=0)
     return row_top, row_total, moment, chosen
 
 
@@ -39,20 +39,30 @@
     state_norm = jnp.sqrt(mean_square)
     live_row = padding_mask == 1
 
-    meta = jnp.zeros((width,), jnp.float32)
-    meta = meta.at[0:local_rows].set((targets // 256).astype(jnp.float32))
-    meta = meta.at[local_rows:2 * local_rows].set((targets % 256).astype(jnp.float32))
-    meta = meta.at[2 * local_rows:3 * local_rows].set(live_row.astype(jnp.float32))
-    packet = jnp.concatenate([normed, meta.astype(jnp.bfloat16)[None, :]], axis=0)
+    pad_rows = 8
+    meta = jnp.concatenate(
+        [
+            (targets // 256).astype(jnp.float32),
+            (targets % 256).astype(jnp.float32),
+            live_row.astype(jnp.float32),
+            jnp.zeros((width - 3 * local_rows,), jnp.float32),
+        ]
+    )
+    meta_rows = jnp.concatenate([meta[None, :], jnp.zeros((pad_rows - 1, width), jnp.float32)], axis=0)
+    packet = jnp.concatenate([normed, meta_rows.astype(jnp.bfloat16)], axis=0)
+    block_rows = local_rows + pad_rows
     gathered = lax.all_gather(packet, "tok", axis=0)
 
     meta_all = gathered[:, local_rows, :].astype(jnp.float32)
     piece_ids = (meta_all[:, 0:local_rows] * 256.0 + meta_all[:, local_rows:2 * local_rows]).astype(jnp.int32)
     piece_live = meta_all[:, 2 * local_rows:3 * local_rows] > 0.5
     vocab_ids = tok_place * slice_width + jnp.arange(slice_width, dtype=jnp.int32)
-    ids_full = jnp.concatenate([piece_ids, jnp.zeros((tok_count, 1), jnp.int32)], axis=1)
+    ids_full = jnp.concatenate([piece_ids, jnp.zeros((tok_count, pad_rows), jnp.int32)], axis=1)
+    flat_stats = slice_stats(
+        gathered.reshape(tok_count * block_rows, width), ids_full.reshape(-1), head_weight, vocab_ids
+    )
     top_p, total_p, moment_p, chosen_p = (
-        part[:, :local_rows] for part in slice_stats(gathered, ids_full, head_weight, vocab_ids)
+        part.reshape(tok_count, block_rows)[:, :local_rows] for part in flat_stats
     )
 
     seq_ends = jnp.cumsum(lengths)

time: 163 us -> 161 us (0.988)
  matrix products: 11 us -> 7.73 us
    dot_general x1, matrix products: 11 us -> 7.73 us  [slice_stats(): lax.dot_general(head_weight, rows, (((1,), (1,)), ((), ())), preferred_el...]
where the time goes in v3:
time: 161 us; the launch traced here: 160 us
  waiting for transfers between devices  106 us (66%)
  between operations  14.3 us (9%)
  starting transfers between devices  13.3 us (8%)
  other arithmetic  12.3 us (8%)
  matrix products  7.73 us (5%)
  local copies, waits for them, and re-layouts  7.19 us (4%)
    all_gather x1, waiting for transfers between devices, shards(): gathered = lax.all_gather(packet, 'tok', axis=0)  91.2 us
    all_to_all x1, waiting for transfers between devices, shards(): incoming = lax.all_to_all(outgoing, 'tok', 0, 0, tiled=True)  11.1 us
    all_to_all x1, starting transfers between devices, shards(): incoming = lax.all_to_all(outgoing, 'tok', 0, 0, tiled=True)  9.27 us
    dot_general x1, matrix products, slice_stats(): lax.dot_general(head_weight, rows, (((1,), (1,)), ((), ())), preferred_el...  7.73 us
    all_to_all x1, starting transfers between devices, shards(): got = lax.all_to_all(rep_pair, 'rep', 0, 0, tiled=True)  3.97 us
    reduce_sum x1, other arithmetic, slice_stats(): row_total = jnp.sum(weights, axis=0)  3.51 us
    all_to_all x1, waiting for transfers between devices, shards(): got = lax.all_to_all(rep_pair, 'rep', 0, 0, tiled=True)  3.3 us
  transfers between devices with their start and end apart: 3, of which 3 were waited for; matrix products, arithmetic and copies ran while one was open for 3% of the time, Pallas kernels for 0%

profile of v3, /device:TPU:1, one launch (start us, length us, event | category | flops | bytes accessed | tf_op | source)
XLA Modules:
  0.0 160.5 jit_solution(2897731051746635699)
XLA Ops:
  7.2 1.0 fusion.6
  8.2 0.7 convert_convert_fusion
  8.9 0.7 convert_convert_fusion.1
  9.6 0.7 convert_element_type.35
  10.3 0.9 fusion.8
  11.2 0.6 fusion.9
  11.9 0.7 copy.69
  12.9 0.9 convert_reduce_fusion.1
  13.9 0.2 convert_reduce_fusion
  14.1 0.7 iota_compare_fusion.2
  14.8 91.2 %all-gather.3.cloned.1.call-done = bf16[4096,1024]{1,0:T(8,128)(2,1)} async-done(((bf16[32,1024]{1,0:T(8,128)(2,1)}), bf16[4096,1024]{1,0:T(8,128)(2,1)}) %all-gather.3.cloned.1.call-update) | async-done | bytes 8388624 | tf_op jit(solution)/shard_map/all_gather | solution.py:54
  106.1 2.0 %slice.75 = bf16[128,1,1024]{2,1,0:T(2,128)(2,1)S(1)} slice(bf16[128,32,1024]{2,1,0:T(8,128)(2,1)} %bitcast.54), slice={[0:128], [24:25], [0:1024]} | slice | bytes 524288 | tf_op jit(solution)/shard_map/slice | solution.py:56
  108.0 0.4 copy.82
  108.7 7.7 %fusion.15 = (f32[4096]{0:T(1024)S(1)}, f32[4096,251]{0,1:T(8,128)}) fusion(bf16[4096,1024]{1,0:T(8,128)(2,1)} %all-gather.3.cloned.1.call-done, bf16[251,1024]{1,0:T(8,128)(2,1)S(1)} %copy-done), kind=kOutput, calls=%fused_computation.72 | convolution fusion | flops 2106564608 | bytes 13031424 | tf_op jit(solution)/shard_map/dot_general | solution.py:14
  116.6 3.5 %fusion.1 = (f32[4096]{0:T(1024)S(1)}, f32[4096]{0:T(1024)S(1)}, f32[4096]{0:T(1024)S(1)}) fusion(f32[4096,251]{0,1:T(8,128)} %get-tuple-element.45, f32[4096]{0:T(1024)S(1)} %get-tuple-element.44, s32[4096]{0:T(1024)S(1)} %eq.97, s32[251]{0:T(256)S(1)} %iota_add_fusion.1), kind=kLoop, calls=%fused_computation.4 | loop fusion | flops 7184384 | bytes 4195308 | tf_op jit(solution)/shard_map/reduce_sum | solution.py:19
  120.5 0.3 select_reduce_fusion
  120.9 0.1 select_reduce_fusion.2
  121.0 0.3 copy.71
  121.3 0.7 reshape.220
  122.0 0.7 copy.73
  122.8 9.3 %all-to-all-start = ((f32[128,1,112]{2,1,0:T(1,128)}), f32[128,1,112]{2,1,0:T(1,128)S(1)}, u32[]{:S(2)}, u32[]{:S(2)}) async-start(f32[128,1,112]{2,1,0:T(1,128)} %copy.73), calls=%async_computation | async-start | bytes 131072 | tf_op jit(solution)/shard_map/all_to_all | solution.py:93
  132.1 0.2 dynamic-slice_reduce_fusion
  132.4 11.1 %all-to-all-done = f32[128,1,112]{2,1,0:T(1,128)S(1)} async-done(((f32[128,1,112]{2,1,0:T(1,128)}), f32[128,1,112]{2,1,0:T(1,128)S(1)}, u32[]{:S(2)}, u32[]{:S(2)}) %all-to-all-start) | async-done | bytes 57376 | tf_op jit(solution)/shard_map/all_to_all | solution.py:93
  143.6 0.3 fusion.14
  143.9 0.1 slice_reduce_fusion.2
  144.2 0.7 copy.79
  144.8 4.0 %all-to-all-start.1 = ((f32[4,2,2]{1,2,0:T(2,128)}), f32[4,2,2]{1,2,0:T(2,128)S(1)}, u32[]{:S(2)}, u32[]{:S(2)}) async-start(f32[4,2,2]{1,2,0:T(2,128)} %copy.79), calls=%async_computation.1 | async-start | bytes 8192 | tf_op jit(solution)/shard_map/all_to_all | solution.py:110
  148.8 0.1 reduce_max.57
  148.9 0.2 multiply_reduce_fusion
  149.1 0.5 subtract_select_fusion
  149.7 3.3 %all-to-all-done.1 = f32[4,2,2]{1,2,0:T(2,128)S(1)} async-done(((f32[4,2,2]{1,2,0:T(2,128)}), f32[4,2,2]{1,2,0:T(2,128)S(1)}, u32[]{:S(2)}, u32[]{:S(2)}) %all-to-all-start.1) | async-done | bytes 96 | tf_op jit(solution)/shard_map/all_to_all | solution.py:110
  153.0 0.6 copy.80
  (47 shorter events, 1.7 us)
Async XLA Ops:
  7.2 101.6 %copy-start = (bf16[251,1024]{1,0:T(8,128)(2,1)S(1)}, bf16[251,1024]{1,0:T(8,128)(2,1)}, u32[]{:S(2)}) copy-start(bf16[251,1024]{1,0:T(8,128)(2,1)} %param.9) | copy-start | bytes 1542148
  7.2 98.9 %all-gather.3.cloned.1.call-start = ((), (), s32[]{:S(2)}) async-start(), calls=%async_computation.2 | async-start | bytes 8454144 | tf_op jit(solution)/shard_map/all_gather | solution.py:54
  116.5 32.6 %copy-start.1 = (s32[24]{0:T(128)S(1)}, s32[24]{0:T(128)}, u32[]{:S(2)}) copy-start(s32[24]{0:T(128)} %param.12) | copy-start | bytes 292
  122.8 20.7 %all-to-all-start = ((f32[128,1,112]{2,1,0:T(1,128)}), f32[128,1,112]{2,1,0:T(1,128)S(1)}, u32[]{:S(2)}, u32[]{:S(2)}) async-start(f32[128,1,112]{2,1,0:T(1,128)} %copy.73), calls=%async_computation | async-start | bytes 131072 | tf_op jit(solution)/shard_map/all_to_all | solution.py:93
  144.8 8.1 %all-to-all-start.1 = ((f32[4,2,2]{1,2,0:T(2,128)}), f32[4,2,2]{1,2,0:T(2,128)S(1)}, u32[]{:S(2)}, u32[]{:S(2)}) async-start(f32[4,2,2]{1,2,0:T(2,128)} %copy.79), calls=%async_computation.1 | async-start | bytes 8192 | tf_op jit(solution)/shard_map/all_to_all | solution.py:110
Sparse Core Ops, SparseCore 0:
  12.0 94.0 all-gather.2

commit v4 on v3

--- a/solution.py
+++ b/solution.py
@@ -1,6 +1,8 @@
 import jax
 import jax.numpy as jnp
 from jax import lax
+from jax.experimental import pallas as pl
+from jax.experimental.pallas import tpu as pltpu
 from jax.sharding import PartitionSpec as P
 
 SLOTS = 2
@@ -10,16 +12,54 @@
 NEG_FILL = -1e30
 
 
+TILE = 512
+VOCAB_PAD = 256
+
+
+def stats_kernel(head_ref, vocab_ref, ids_ref, rows_ref, out_ref):
+    logits = lax.dot_general(
+        head_ref[...], rows_ref[...], (((1,), (1,)), ((), ())), preferred_element_type=jnp.float32
+    )
+    real = vocab_ref[...] >= 0
+    logits = jnp.where(real, logits, -jnp.inf)
+    row_top = jnp.max(logits, axis=0, keepdims=True)
+    weights = jnp.where(real, jnp.exp(logits - row_top), 0.0)
+    row_total = jnp.sum(weights, axis=0, keepdims=True)
+    moment = jnp.sum(jnp.where(real, weights * logits, 0.0), axis=0, keepdims=True)
+    chosen = jnp.sum(jnp.where(vocab_ref[...] == ids_ref[...], logits, 0.0), axis=0, keepdims=True)
+    out_ref[...] = jnp.concatenate(
+        [row_top, row_total, moment, chosen, jnp.zeros((4, row_top.shape[1]), jnp.float32)], axis=0
+    )
+
+
 def slice_stats(rows, ids, head_weight, vocab_ids):
-    logits = lax.dot_general(
-        head_weight, rows, (((1,), (1,)), ((), ())), preferred_element_type=jnp.float32
+    count, width = rows.shape
+    tile = TILE if count % TILE == 0 else count
+    slice_width = head_weight.shape[0]
+    head = jnp.concatenate(
+        [head_weight, jnp.zeros((VOCAB_PAD - slice_width, width), head_weight.dtype)], axis=0
     )
-    row_top = jnp.max(logits, axis=0)
-    weights = jnp.exp(logits - row_top[None, :])
-    row_total = jnp.sum(weights, axis=0)
-    moment = jnp.sum(weights * logits, axis=0)
-    chosen = jnp.sum(jnp.where(vocab_ids[:, None] == ids[None, :], logits, 0.0), axis=0)
-    return row_top, row_total, moment, chosen
+    vocab = jnp.concatenate(
+        [vocab_ids, jnp.full((VOCAB_PAD - slice_width,), -1, jnp.int32)]
+    )[:, None]
+    out = pl.pallas_call(
+        stats_kernel,
+        grid=(count // tile,),
+        in_specs=[
+            pl.BlockSpec((VOCAB_PAD, width), lambda i: (0, 0)),
+            pl.BlockSpec((VOCAB_PAD, 1), lambda i: (0, 0)),
+            pl.BlockSpec((1, tile), lambda i: (0, i)),
+            pl.BlockSpec((tile, width), lambda i: (i, 0)),
+        ],
+        out_specs=pl.BlockSpec((8, tile), lambda i: (0, i)),
+        out_shape=jax.ShapeDtypeStruct((8, count), jnp.float32),
+        cost_estimate=pl.CostEstimate(
+            flops=2 * VOCAB_PAD * width * count,
+            transcendentals=VOCAB_PAD * count,
+            bytes_accessed=count * width * 2 + VOCAB_PAD * width * 2 + count * 36,
+        ),
+    )(head, vocab, ids[None, :], rows)
+    return out[0], out[1], out[2], out[3]
 
 
 def shards(hidden, norm_gain, head_weight, targets, lengths, padding_mask, owner_map):

time: 161 us -> 161 us (level)
  Pallas kernels: 0 us -> 9.47 us
  matrix products: 7.73 us -> 0 us
  local copies, waits for them, and re-layouts: 7.19 us -> 11.8 us
  other arithmetic: 12.3 us -> 8.77 us
  waiting for transfers between devices: 106 us -> 103 us
    pallas_call x0 -> x1, Pallas kernels: none -> 9.47 us  [slice_stats(): pl.pallas_call(stats_kernel, grid=(count // tile,), in_specs=[pl.BlockSpe...]
    dot_general x1 -> x0, matrix products: 7.73 us -> none  [slice_stats(): lax.dot_general(head_weight, rows, (((1,), (1,)), ((), ())), preferred_el...]
    reduce_sum x1 -> x0, other arithmetic: 3.51 us -> none  [slice_stats(): row_total = jnp.sum(weights, axis=0)]
    all_gather x1, waiting for transfers between devices: 91.2 us -> 88.5 us  [shards(): gathered = lax.all_gather(packet, 'tok', axis=0)]
    concatenate x0 -> x2, local copies, waits for them, and re-layouts: none -> 1.93 us  [the longest x1 1.93 us: slice_stats(): jnp.concatenate([head_weight, jnp.zeros((VOCAB_PAD - slice_width, width),...]
  transfers between devices with their start and end apart: 3 -> 3, of which waited for: 3 -> 3; matrix products, arithmetic and copies ran while one was open for 3% -> 4% of each run, Pallas kernels for 0% -> 0%
where the time goes in v4:
time: 161 us
  waiting for transfers between devices  103 us (64%)
  between operations  14.2 us (9%)
  starting transfers between devices  13.3 us (8%)
  local copies, waits for them, and re-layouts  11.8 us (7%)
  Pallas kernels  9.47 us (6%)
  other arithmetic  8.77 us (5%)
    all_gather x1, waiting for transfers between devices, shards(): gathered = lax.all_gather(packet, 'tok', axis=0)  88.5 us
    all_to_all x1, waiting for transfers between devices, shards(): incoming = lax.all_to_all(outgoing, 'tok', 0, 0, tiled=True)  11.1 us
    pallas_call x1, Pallas kernels, slice_stats(): pl.pallas_call(stats_kernel, grid=(count // tile,), in_specs=[pl.BlockSpe...  9.47 us
    all_to_all x1, starting transfers between devices, shards(): incoming = lax.all_to_all(outgoing, 'tok', 0, 0, tiled=True)  9.27 us
    all_to_all x1, starting transfers between devices, shards(): got = lax.all_to_all(rep_pair, 'rep', 0, 0, tiled=True)  3.96 us
    all_to_all x1, waiting for transfers between devices, shards(): got = lax.all_to_all(rep_pair, 'rep', 0, 0, tiled=True)  3.3 us
  transfers between devices with their start and end apart: 3, of which 3 were waited for; matrix products, arithmetic and copies ran while one was open for 4% of the time, Pallas kernels for 0%

profile of v4, /device:TPU:1, one launch (start us, length us, event | category | flops | bytes accessed | tf_op | source)
XLA Modules:
  0.0 160.5 jit_solution(16653876056621558177)
XLA Ops:
  7.2 0.9 fusion.2
  8.1 0.7 convert_convert_fusion
  8.8 0.7 convert_convert_fusion.1
  9.6 0.7 convert_element_type.35
  10.2 0.9 fusion.4
  11.1 0.6 fusion.5
  11.8 0.7 copy.59
  12.8 0.8 copy.57.vocab_ref
  13.6 1.9 %concatenate.29.head_ref = bf16[256,1024]{1,0:T(8,128)(2,1)} pad(bf16[251,1024]{1,0:T(8,128)(2,1)} %param.9, bf16[]{:T(256)} %constant.25.clone.1), padding=0_5x0_0 | pad | bytes 1038338 | tf_op jit(solution)/shard_map/concatenate | solution.py:39
  15.5 0.9 convert_reduce_fusion.1
  16.5 0.2 convert_reduce_fusion
  16.7 0.7 iota_compare_fusion.2
  17.5 88.5 %all-gather.3.cloned.1.call-done.rows_ref = bf16[4096,1024]{1,0:T(8,128)(2,1)} async-done(((bf16[32,1024]{1,0:T(8,128)(2,1)}), bf16[4096,1024]{1,0:T(8,128)(2,1)}) %all-gather.3.cloned.1.call-update) | async-done | bytes 8388624 | tf_op jit(solution)/shard_map/all_gather | solution.py:94
  106.0 2.0 %slice.88 = bf16[128,1,1024]{2,1,0:T(2,128)(2,1)S(1)} slice(bf16[128,32,1024]{2,1,0:T(8,128)(2,1)} %bitcast.31), slice={[0:128], [24:25], [0:1024]} | slice | bytes 524288 | tf_op jit(solution)/shard_map/slice | solution.py:96
  107.9 0.4 copy.72
  108.6 0.7 broadcast_in_dim_reshape.3.ids_ref
  109.3 9.5 %shard_map.94 = f32[8,4096]{1,0:T(8,128)} custom-call(bf16[256,1024]{1,0:T(8,128)(2,1)} %concatenate.29.head_ref, s32[256,1]{1,0:T(8,128)} %copy.57.vocab_ref, s32[1,4096]{1,0:T(1,128)} %broadcast_in_dim_reshape.3.ids_ref, bf16[4096,1024]{1,0:T(8,128)(2,1)} %all-gather.3.cloned.1.call-done.rows_ref), custom_call_target="tpu_custom_call" | custom-call | flops 2147483648 | bytes 9060352 | tf_op jit(solution)/shard_map/pallas_call | solution.py:45
  118.7 1.3 slice_reduce_fusion.2
  120.6 0.3 select_reduce_fusion
  121.1 0.3 copy.61
  121.4 0.7 reshape.198
  122.1 0.7 copy.63
  122.8 9.3 %all-to-all-start = ((f32[128,1,112]{2,1,0:T(1,128)}), f32[128,1,112]{2,1,0:T(1,128)S(1)}, u32[]{:S(2)}, u32[]{:S(2)}) async-start(f32[128,1,112]{2,1,0:T(1,128)} %copy.63), calls=%async_computation | async-start | bytes 131072 | tf_op jit(solution)/shard_map/all_to_all | solution.py:133
  132.2 0.2 dynamic-slice_reduce_fusion
  132.4 11.1 %all-to-all-done = f32[128,1,112]{2,1,0:T(1,128)S(1)} async-done(((f32[128,1,112]{2,1,0:T(1,128)}), f32[128,1,112]{2,1,0:T(1,128)S(1)}, u32[]{:S(2)}, u32[]{:S(2)}) %all-to-all-start) | async-done | bytes 57376 | tf_op jit(solution)/shard_map/all_to_all | solution.py:133
  143.6 0.3 fusion.10
  144.2 0.7 copy.69
  144.9 4.0 %all-to-all-start.1 = ((f32[4,2,2]{1,2,0:T(2,128)}), f32[4,2,2]{1,2,0:T(2,128)S(1)}, u32[]{:S(2)}, u32[]{:S(2)}) async-start(f32[4,2,2]{1,2,0:T(2,128)} %copy.69), calls=%async_computation.1 | async-start | bytes 8192 | tf_op jit(solution)/shard_map/all_to_all | solution.py:150
  149.0 0.2 multiply_reduce_fusion
  149.2 0.5 subtract_select_fusion
  149.7 3.3 %all-to-all-done.1 = f32[4,2,2]{1,2,0:T(2,128)S(1)} async-done(((f32[4,2,2]{1,2,0:T(2,128)}), f32[4,2,2]{1,2,0:T(2,128)S(1)}, u32[]{:S(2)}, u32[]{:S(2)}) %all-to-all-start.1) | async-done | bytes 96 | tf_op jit(solution)/shard_map/all_to_all | solution.py:150
  153.0 0.6 copy.70
  (48 shorter events, 2.0 us)
Async XLA Ops:
  7.2 98.8 %all-gather.3.cloned.1.call-start = ((), (), s32[]{:S(2)}) async-start(), calls=%async_computation.2 | async-start | bytes 8454144 | tf_op jit(solution)/shard_map/all_gather | solution.py:94
  15.5 133.7 %copy-start = (s32[24]{0:T(128)S(1)}, s32[24]{0:T(128)}, u32[]{:S(2)}) copy-start(s32[24]{0:T(128)} %param.12) | copy-start | bytes 292
  122.8 20.7 %all-to-all-start = ((f32[128,1,112]{2,1,0:T(1,128)}), f32[128,1,112]{2,1,0:T(1,128)S(1)}, u32[]{:S(2)}, u32[]{:S(2)}) async-start(f32[128,1,112]{2,1,0:T(1,128)} %copy.63), calls=%async_computation | async-start | bytes 131072 | tf_op jit(solution)/shard_map/all_to_all | solution.py:133
  144.9 8.1 %all-to-all-start.1 = ((f32[4,2,2]{1,2,0:T(2,128)}), f32[4,2,2]{1,2,0:T(2,128)S(1)}, u32[]{:S(2)}, u32[]{:S(2)}) async-start(f32[4,2,2]{1,2,0:T(2,128)} %copy.69), calls=%async_computation.1 | async-start | bytes 8192 | tf_op jit(solution)/shard_map/all_to_all | solution.py:150
Sparse Core Ops, SparseCore 0:
  11.9 94.0 all-gather.2

commit v5 on v4

--- a/solution.py
+++ b/solution.py
@@ -79,31 +79,13 @@
     state_norm = jnp.sqrt(mean_square)
     live_row = padding_mask == 1
 
-    pad_rows = 8
-    meta = jnp.concatenate(
-        [
-            (targets // 256).astype(jnp.float32),
-            (targets % 256).astype(jnp.float32),
-            live_row.astype(jnp.float32),
-            jnp.zeros((width - 3 * local_rows,), jnp.float32),
-        ]
-    )
-    meta_rows = jnp.concatenate([meta[None, :], jnp.zeros((pad_rows - 1, width), jnp.float32)], axis=0)
-    packet = jnp.concatenate([normed, meta_rows.astype(jnp.bfloat16)], axis=0)
-    block_rows = local_rows + pad_rows
-    gathered = lax.all_gather(packet, "tok", axis=0)
-
-    meta_all = gathered[:, local_rows, :].astype(jnp.float32)
-    piece_ids = (meta_all[:, 0:local_rows] * 256.0 + meta_all[:, local_rows:2 * local_rows]).astype(jnp.int32)
-    piece_live = meta_all[:, 2 * local_rows:3 * local_rows] > 0.5
+    gathered = lax.all_gather(normed, "tok", axis=0, tiled=True)
+    meta = lax.all_gather(jnp.stack([targets, padding_mask]), "tok", axis=0)
+    piece_ids = meta[:, 0, :]
+    piece_live = meta[:, 1, :] == 1
     vocab_ids = tok_place * slice_width + jnp.arange(slice_width, dtype=jnp.int32)
-    ids_full = jnp.concatenate([piece_ids, jnp.zeros((tok_count, pad_rows), jnp.int32)], axis=1)
-    flat_stats = slice_stats(
-        gathered.reshape(tok_count * block_rows, width), ids_full.reshape(-1), head_weight, vocab_ids
-    )
-    top_p, total_p, moment_p, chosen_p = (
-        part.reshape(tok_count, block_rows)[:, :local_rows] for part in flat_stats
-    )
+    flat_stats = slice_stats(gathered, piece_ids.reshape(-1), head_weight, vocab_ids)
+    top_p, total_p, moment_p, chosen_p = (part.reshape(tok_count, local_rows) for part in flat_stats)
 
     seq_ends = jnp.cumsum(lengths)
     seq_ids = jnp.arange(seq_count, dtype=jnp.int32)

time: 161 us -> 154 us (0.957)
  waiting for transfers between devices: 103 us -> 41.9 us
  blocking collectives: 0 us -> 58.5 us
  local copies, waits for them, and re-layouts: 11.8 us -> 9.56 us
  Pallas kernels: 9.47 us -> 7.45 us
    all_gather x1, waiting for transfers between devices: 88.5 us -> 27.4 us  [shards(): gathered = lax.all_gather(normed, 'tok', axis=0, tiled=True)]
    all_gather x0 -> x1, blocking collectives: none -> 58.5 us  [shards(): meta = lax.all_gather(jnp.stack([targets, padding_mask]), 'tok', axis=0)]
    pallas_call x1, Pallas kernels: 9.47 us -> 7.45 us  [slice_stats(): pl.pallas_call(stats_kernel, grid=(count // tile,), in_specs=[pl.BlockSpe...]
    slice x2 -> x1, local copies, waits for them, and re-layouts: 2.02 us -> 0.23 us  [shards(): piece_live = meta[:, 1, :] == 1]
  transfers between devices with their start and end apart: 3 -> 3, of which waited for: 3 -> 3; matrix products, arithmetic and copies ran while one was open for 4% -> 6% of each run, Pallas kernels for 0% -> 0%
where the time goes in v5:
time: 154 us; the launch traced here: 153 us
  blocking collectives  58.5 us (38%)
  waiting for transfers between devices  41.9 us (27%)
  between operations  14.2 us (9%)
  starting transfers between devices  13.4 us (9%)
  local copies, waits for them, and re-layouts  9.56 us (6%)
  other arithmetic  8 us (5%)
  Pallas kernels  7.45 us (5%)
    all_gather x1, blocking collectives, shards(): meta = lax.all_gather(jnp.stack([targets, padding_mask]), 'tok', axis=0)  58.5 us
    all_gather x1, waiting for transfers between devices, shards(): gathered = lax.all_gather(normed, 'tok', axis=0, tiled=True)  27.4 us
    all_to_all x1, waiting for transfers between devices, shards(): incoming = lax.all_to_all(outgoing, 'tok', 0, 0, tiled=True)  11.1 us
    all_to_all x1, starting transfers between devices, shards(): incoming = lax.all_to_all(outgoing, 'tok', 0, 0, tiled=True)  9.43 us
    pallas_call x1, Pallas kernels, slice_stats(): pl.pallas_call(stats_kernel, grid=(count // tile,), in_specs=[pl.BlockSpe...  7.45 us
    all_to_all x1, starting transfers between devices, shards(): got = lax.all_to_all(rep_pair, 'rep', 0, 0, tiled=True)  3.96 us
    all_to_all x1, waiting for transfers between devices, shards(): got = lax.all_to_all(rep_pair, 'rep', 0, 0, tiled=True)  3.3 us
  transfers between devices with their start and end apart: 3, of which 3 were waited for; matrix products, arithmetic and copies ran while one was open for 6% of the time, Pallas kernels for 0%

profile of v5, /device:TPU:1, one launch (start us, length us, event | category | flops | bytes accessed | tf_op | source)
XLA Modules:
  0.0 153.0 jit_solution(8517710667390036948)
XLA Ops:
  7.2 0.9 fusion.1
  8.1 0.7 convert_element_type.16
  8.8 1.5 fusion.3
  10.4 0.7 copy.43
  11.3 0.7 add_bitcast_fusion
  12.0 58.5 %all-gather.1 = s32[128,2,24]{2,1,0:T(2,128)S(1)} all-gather(s32[1,2,24]{2,1,0:T(2,128)S(1)} %add_bitcast_fusion), channel_id=2, replica_groups=mesh['tok'=128,'rep'=4] {'tok'}, dimensions={0}, use_global_device_ids=true | all-gather | bytes 24768 | tf_op jit(solution)/shard_map/all_gather | solution.py:83
  70.5 0.2 fusion.5
  70.7 0.7 broadcast_in_dim_reshape_squeeze.4.ids_ref
  71.5 0.8 copy.41.vocab_ref
  72.3 1.9 %concatenate.16.head_ref = bf16[256,1024]{1,0:T(8,128)(2,1)} pad(bf16[251,1024]{1,0:T(8,128)(2,1)} %param.9, bf16[]{:T(256)} %constant.18.clone.1), padding=0_5x0_0 | pad | bytes 1038338 | tf_op jit(solution)/shard_map/concatenate | solution.py:39
  74.2 0.9 convert_reduce_fusion.1
  75.2 0.2 convert_reduce_fusion
  75.4 0.7 iota_compare_fusion.1
  76.1 27.4 %all-gather.4.cloned.1.call-done.rows_ref = bf16[3072,1024]{1,0:T(8,128)(2,1)} async-done(((bf16[24,1024]{1,0:T(8,128)(2,1)}), bf16[3072,1024]{1,0:T(8,128)(2,1)}) %all-gather.4.cloned.1.call-update) | async-done | bytes 6291472 | tf_op jit(solution)/shard_map/all_gather | solution.py:82
  103.6 7.4 %shard_map.94 = f32[8,3072]{1,0:T(8,128)} custom-call(bf16[256,1024]{1,0:T(8,128)(2,1)} %concatenate.16.head_ref, s32[256,1]{1,0:T(8,128)} %copy.41.vocab_ref, s32[1,3072]{1,0:T(1,128)} %broadcast_in_dim_reshape_squeeze.4.ids_ref, bf16[3072,1024]{1,0:T(8,128)(2,1)} %all-gather.4.cloned.1.call-done.rows_ref), custom_call_target="tpu_custom_call" | custom-call | flops 1610612736 | bytes 6926336 | tf_op jit(solution)/shard_map/pallas_call | solution.py:45
  111.0 1.2 slice_reduce_fusion.9
  112.9 0.3 select_reduce_fusion
  113.2 0.1 select_reduce_fusion.2
  113.4 0.3 copy.46
  113.6 0.7 reshape.198
  114.3 0.7 copy.48
  115.1 9.4 %all-to-all-start = ((f32[128,1,112]{2,1,0:T(1,128)}), f32[128,1,112]{2,1,0:T(1,128)S(1)}, u32[]{:S(2)}, u32[]{:S(2)}) async-start(f32[128,1,112]{2,1,0:T(1,128)} %copy.48), calls=%async_computation | async-start | bytes 131072 | tf_op jit(solution)/shard_map/all_to_all | solution.py:115
  124.6 0.2 dynamic-slice_reduce_fusion
  124.8 11.1 %all-to-all-done = f32[128,1,112]{2,1,0:T(1,128)S(1)} async-done(((f32[128,1,112]{2,1,0:T(1,128)}), f32[128,1,112]{2,1,0:T(1,128)S(1)}, u32[]{:S(2)}, u32[]{:S(2)}) %all-to-all-start) | async-done | bytes 57376 | tf_op jit(solution)/shard_map/all_to_all | solution.py:115
  136.1 0.3 fusion.6
  136.6 0.7 copy.54
  137.3 4.0 %all-to-all-start.1 = ((f32[4,2,2]{1,2,0:T(2,128)}), f32[4,2,2]{1,2,0:T(2,128)S(1)}, u32[]{:S(2)}, u32[]{:S(2)}) async-start(f32[4,2,2]{1,2,0:T(2,128)} %copy.54), calls=%async_computation.1 | async-start | bytes 8192 | tf_op jit(solution)/shard_map/all_to_all | solution.py:132
  141.3 0.1 reduce_max.47
  141.4 0.2 multiply_reduce_fusion
  141.6 0.5 compare_select_fusion
  142.1 3.3 %all-to-all-done.1 = f32[4,2,2]{1,2,0:T(2,128)S(1)} async-done(((f32[4,2,2]{1,2,0:T(2,128)}), f32[4,2,2]{1,2,0:T(2,128)S(1)}, u32[]{:S(2)}, u32[]{:S(2)}) %all-to-all-start.1) | async-done | bytes 96 | tf_op jit(solution)/shard_map/all_to_all | solution.py:132
  145.5 0.6 copy.55
  (38 shorter events, 1.6 us)
Async XLA Ops:
  7.2 96.4 %all-gather.4.cloned.1.call-start = ((), (), s32[]{:S(2)}) async-start(), calls=%async_computation.2 | async-start | bytes 6340608 | tf_op jit(solution)/shard_map/all_gather | solution.py:82
  11.2 130.4 %copy-start = (s32[24]{0:T(128)S(1)}, s32[24]{0:T(128)}, u32[]{:S(2)}) copy-start(s32[24]{0:T(128)} %param.12) | copy-start | bytes 292
  115.1 20.9 %all-to-all-start = ((f32[128,1,112]{2,1,0:T(1,128)}), f32[128,1,112]{2,1,0:T(1,128)S(1)}, u32[]{:S(2)}, u32[]{:S(2)}) async-start(f32[128,1,112]{2,1,0:T(1,128)} %copy.48), calls=%async_computation | async-start | bytes 131072 | tf_op jit(solution)/shard_map/all_to_all | solution.py:115
  137.3 8.1 %all-to-all-start.1 = ((f32[4,2,2]{1,2,0:T(2,128)}), f32[4,2,2]{1,2,0:T(2,128)S(1)}, u32[]{:S(2)}, u32[]{:S(2)}) async-start(f32[4,2,2]{1,2,0:T(2,128)} %copy.54), calls=%async_computation.1 | async-start | bytes 8192 | tf_op jit(solution)/shard_map/all_to_all | solution.py:132
Sparse Core Ops, SparseCore 0:
  11.1 92.3 all-gather.3

commit v6 on v5

--- a/solution.py
+++ b/solution.py
@@ -129,7 +129,13 @@
     rep_max = jnp.max(in_req[..., 0], axis=0)
     rep_norm = jnp.sum(in_req[..., 1], axis=0)
     rep_pair = jnp.stack([rep_max, rep_norm], axis=2)
-    got = lax.all_to_all(rep_pair, "rep", 0, 0, tiled=True)
+    rep_count_static = rep_pair.shape[0]
+    shares = [lax.dynamic_index_in_dim(rep_pair, rep_place, 0, keepdims=False)]
+    for shift in range(1, rep_count_static):
+        share = lax.dynamic_index_in_dim(rep_pair, (rep_place + shift) % rep_count, 0, keepdims=False)
+        pairs = [(i, (i + shift) % rep_count_static) for i in range(rep_count_static)]
+        shares.append(lax.ppermute(share, "rep", pairs))
+    got = jnp.stack(shares)
     final_max = jnp.max(got[..., 0], axis=0)
     final_norm = jnp.sum(got[..., 1], axis=0)
     has_slot = jnp.any(slot_hot[:, device_place, :], axis=0)

time: 154 us -> 158 us (1.026)
  starting transfers between devices: 13.4 us -> 18.7 us
    ppermute x0 -> x3, starting transfers between devices: none -> 9.25 us  [shards(): shares.append(lax.ppermute(share, 'rep', pairs))]
    all_to_all x1 -> x0, starting transfers between devices: 3.96 us -> none  [shards(): got = lax.all_to_all(rep_pair, 'rep', 0, 0, tiled=True)]
    all_to_all x1 -> x0, waiting for transfers between devices: 3.3 us -> none  [shards(): got = lax.all_to_all(rep_pair, 'rep', 0, 0, tiled=True)]
    ppermute x0 -> x3, waiting for transfers between devices: none -> 2.02 us  [shards(): shares.append(lax.ppermute(share, 'rep', pairs))]
  transfers between devices with their start and end apart: 3 -> 5, of which waited for: 3 -> 3; matrix products, arithmetic and copies ran while one was open for 6% -> 5% of each run, Pallas kernels for 0% -> 0%
where the time goes in v6:
time: 158 us; the launch traced here: 157 us
  blocking collectives  58.5 us (37%)
  waiting for transfers between devices  40.5 us (26%)
  starting transfers between devices  18.7 us (12%)
  between operations  14.3 us (9%)
  local copies, waits for them, and re-layouts  9.47 us (6%)
  other arithmetic  8.28 us (5%)
  Pallas kernels  7.44 us (5%)
    all_gather x1, blocking collectives, shards(): meta = lax.all_gather(jnp.stack([targets, padding_mask]), 'tok', axis=0)  58.5 us
    all_gather x1, waiting for transfers between devices, shards(): gathered = lax.all_gather(normed, 'tok', axis=0, tiled=True)  27.4 us
    all_to_all x1, waiting for transfers between devices, shards(): incoming = lax.all_to_all(outgoing, 'tok', 0, 0, tiled=True)  11.1 us
    all_to_all x1, starting transfers between devices, shards(): incoming = lax.all_to_all(outgoing, 'tok', 0, 0, tiled=True)  9.45 us
    ppermute x3, starting transfers between devices, shards(): shares.append(lax.ppermute(share, 'rep', pairs))  9.25 us
    pallas_call x1, Pallas kernels, slice_stats(): pl.pallas_call(stats_kernel, grid=(count // tile,), in_specs=[pl.BlockSpe...  7.44 us
  transfers between devices with their start and end apart: 5, of which 3 were waited for; matrix products, arithmetic and copies ran while one was open for 5% of the time, Pallas kernels for 0%

profile of v6, /device:TPU:1, one launch (start us, length us, event | category | flops | bytes accessed | tf_op | source)
XLA Modules:
  0.0 157.2 jit_solution(1749741021756818591)
XLA Ops:
  7.2 0.9 fusion.1
  8.1 0.7 convert_element_type.16
  8.8 1.5 fusion.3
  10.4 0.7 copy.60
  11.3 0.7 add_bitcast_fusion
  12.0 58.5 %all-gather.1 = s32[128,2,24]{2,1,0:T(2,128)S(1)} all-gather(s32[1,2,24]{2,1,0:T(2,128)S(1)} %add_bitcast_fusion), channel_id=2, replica_groups=mesh['tok'=128,'rep'=4] {'tok'}, dimensions={0}, use_global_device_ids=true | all-gather | bytes 24768 | tf_op jit(solution)/shard_map/all_gather | solution.py:83
  70.5 0.2 fusion.9
  70.7 0.7 broadcast_in_dim_reshape_squeeze.4.ids_ref
  71.5 0.8 copy.58.vocab_ref
  72.3 1.9 %concatenate.16.head_ref = bf16[256,1024]{1,0:T(8,128)(2,1)} pad(bf16[251,1024]{1,0:T(8,128)(2,1)} %param.9, bf16[]{:T(256)} %constant.60.clone.1), padding=0_5x0_0 | pad | bytes 1038338 | tf_op jit(solution)/shard_map/concatenate | solution.py:39
  74.2 0.9 convert_reduce_fusion.1
  75.2 0.2 convert_reduce_fusion
  75.4 0.7 iota_compare_fusion.1
  76.1 27.4 %all-gather.4.cloned.1.call-done.rows_ref = bf16[3072,1024]{1,0:T(8,128)(2,1)} async-done(((bf16[24,1024]{1,0:T(8,128)(2,1)}), bf16[3072,1024]{1,0:T(8,128)(2,1)}) %all-gather.4.cloned.1.call-update) | async-done | bytes 6291472 | tf_op jit(solution)/shard_map/all_gather | solution.py:82
  103.6 7.4 %shard_map.94 = f32[8,3072]{1,0:T(8,128)} custom-call(bf16[256,1024]{1,0:T(8,128)(2,1)} %concatenate.16.head_ref, s32[256,1]{1,0:T(8,128)} %copy.58.vocab_ref, s32[1,3072]{1,0:T(1,128)} %broadcast_in_dim_reshape_squeeze.4.ids_ref, bf16[3072,1024]{1,0:T(8,128)(2,1)} %all-gather.4.cloned.1.call-done.rows_ref), custom_call_target="tpu_custom_call" | custom-call | flops 1610612736 | bytes 6926336 | tf_op jit(solution)/shard_map/pallas_call | solution.py:45
  111.0 1.2 slice_reduce_fusion.9
  112.9 0.3 select_reduce_fusion
  113.2 0.1 select_reduce_fusion.2
  113.4 0.3 copy.63
  113.6 0.7 reshape.198
  114.3 0.7 copy.65
  115.1 9.4 %all-to-all-start = ((f32[128,1,112]{2,1,0:T(1,128)}), f32[128,1,112]{2,1,0:T(1,128)S(1)}, u32[]{:S(2)}, u32[]{:S(2)}) async-start(f32[128,1,112]{2,1,0:T(1,128)} %copy.65), calls=%async_computation | async-start | bytes 131072 | tf_op jit(solution)/shard_map/all_to_all | solution.py:115
  124.7 0.2 dynamic-slice_reduce_fusion
  124.9 11.1 %all-to-all-done = f32[128,1,112]{2,1,0:T(1,128)S(1)} async-done(((f32[128,1,112]{2,1,0:T(1,128)}), f32[128,1,112]{2,1,0:T(1,128)S(1)}, u32[]{:S(2)}, u32[]{:S(2)}) %all-to-all-start) | async-done | bytes 57376 | tf_op jit(solution)/shard_map/all_to_all | solution.py:115
  136.1 0.3 fusion.10
  137.0 4.3 %collective-permute-start.2 = (f32[2,2]{1,0:T(2,128)S(1)}, f32[2,2]{1,0:T(2,128)S(1)}, u32[]{:S(2)}, u32[]{:S(2)}) collective-permute-start(f32[2,2]{1,0:T(2,128)S(1)} %bitcast.54), channel_id=1, source_target_pairs={{0,3},{1,0},{2,1},{3,2},{4,7},{5,4},{6,5},{7,6},{8,11},{9,8},{10,9... | collective-permute-start | bytes 56 | tf_op jit(solution)/shard_map/ppermute | solution.py:137
  141.3 2.5 %collective-permute-start.1 = (f32[2,2]{1,0:T(2,128)S(1)}, f32[2,2]{1,0:T(2,128)S(1)}, u32[]{:S(2)}, u32[]{:S(2)}) collective-permute-start(f32[2,2]{1,0:T(2,128)S(1)} %bitcast.51), channel_id=1, source_target_pairs={{0,2},{1,3},{2,0},{3,1},{4,6},{5,7},{6,4},{7,5},{8,10},{9,11},{10,... | collective-permute-start | bytes 56 | tf_op jit(solution)/shard_map/ppermute | solution.py:137
  143.8 2.5 %collective-permute-start = (f32[2,2]{1,0:T(2,128)S(1)}, f32[2,2]{1,0:T(2,128)S(1)}, u32[]{:S(2)}, u32[]{:S(2)}) collective-permute-start(f32[2,2]{1,0:T(2,128)S(1)} %bitcast.50), channel_id=1, source_target_pairs={{0,1},{1,2},{2,3},{3,0},{4,5},{5,6},{6,7},{7,4},{8,9},{9,10},{10,1... | collective-permute-start | bytes 56 | tf_op jit(solution)/shard_map/ppermute | solution.py:137
  146.4 0.2 multiply_reduce_fusion
  146.6 0.5 compare_select_fusion
  147.3 2.0 %collective-permute-done = f32[2,2]{1,0:T(2,128)S(1)} collective-permute-done((f32[2,2]{1,0:T(2,128)S(1)}, f32[2,2]{1,0:T(2,128)S(1)}, u32[]{:S(2)}, u32[]{:S(2)}) %collective-permute-start) | collective-permute-done | bytes 48 | tf_op jit(solution)/shard_map/ppermute | solution.py:137
  149.7 0.7 copy.77
  (48 shorter events, 2.6 us)
Async XLA Ops:
  7.2 96.4 %all-gather.4.cloned.1.call-start = ((), (), s32[]{:S(2)}) async-start(), calls=%async_computation.1 | async-start | bytes 6340608 | tf_op jit(solution)/shard_map/all_gather | solution.py:82
  70.5 76.1 %copy-start = (s32[24]{0:T(128)S(1)}, s32[24]{0:T(128)}, u32[]{:S(2)}) copy-start(s32[24]{0:T(128)} %param.12) | copy-start | bytes 292
  115.1 20.9 %all-to-all-start = ((f32[128,1,112]{2,1,0:T(1,128)}), f32[128,1,112]{2,1,0:T(1,128)S(1)}, u32[]{:S(2)}, u32[]{:S(2)}) async-start(f32[128,1,112]{2,1,0:T(1,128)} %copy.65), calls=%async_computation | async-start | bytes 131072 | tf_op jit(solution)/shard_map/all_to_all | solution.py:115
  137.0 10.1 %collective-permute-start.2 = (f32[2,2]{1,0:T(2,128)S(1)}, f32[2,2]{1,0:T(2,128)S(1)}, u32[]{:S(2)}, u32[]{:S(2)}) collective-permute-start(f32[2,2]{1,0:T(2,128)S(1)} %bitcast.54), channel_id=1, source_target_pairs={{0,3},{1,0},{2,1},{3,2},{4,7},{5,4},{6,5},{7,6},{8,11},{9,8},{10,9... | collective-permute-start | bytes 56 | tf_op jit(solution)/shard_map/ppermute | solution.py:137
  141.3 5.9 %collective-permute-start.1 = (f32[2,2]{1,0:T(2,128)S(1)}, f32[2,2]{1,0:T(2,128)S(1)}, u32[]{:S(2)}, u32[]{:S(2)}) collective-permute-start(f32[2,2]{1,0:T(2,128)S(1)} %bitcast.51), channel_id=1, source_target_pairs={{0,2},{1,3},{2,0},{3,1},{4,6},{5,7},{6,4},{7,5},{8,10},{9,11},{10,... | collective-permute-start | bytes 56 | tf_op jit(solution)/shard_map/ppermute | solution.py:137
  143.8 5.5 %collective-permute-start = (f32[2,2]{1,0:T(2,128)S(1)}, f32[2,2]{1,0:T(2,128)S(1)}, u32[]{:S(2)}, u32[]{:S(2)}) collective-permute-start(f32[2,2]{1,0:T(2,128)S(1)} %bitcast.50), channel_id=1, source_target_pairs={{0,1},{1,2},{2,3},{3,0},{4,5},{5,6},{6,7},{7,4},{8,9},{9,10},{10,1... | collective-permute-start | bytes 56 | tf_op jit(solution)/shard_map/ppermute | solution.py:137
Sparse Core Ops, SparseCore 0:
  11.1 92.3 all-gather.3

commit v7 on v5

--- a/solution.py
+++ b/solution.py
@@ -17,18 +17,17 @@
 
 
 def stats_kernel(head_ref, vocab_ref, ids_ref, rows_ref, out_ref):
-    logits = lax.dot_general(
-        head_ref[...], rows_ref[...], (((1,), (1,)), ((), ())), preferred_element_type=jnp.float32
-    )
+    logits = jnp.dot(rows_ref[...], head_ref[...], preferred_element_type=jnp.float32)
     real = vocab_ref[...] >= 0
     logits = jnp.where(real, logits, -jnp.inf)
-    row_top = jnp.max(logits, axis=0, keepdims=True)
+    row_top = jnp.max(logits, axis=1, keepdims=True)
     weights = jnp.where(real, jnp.exp(logits - row_top), 0.0)
-    row_total = jnp.sum(weights, axis=0, keepdims=True)
-    moment = jnp.sum(jnp.where(real, weights * logits, 0.0), axis=0, keepdims=True)
-    chosen = jnp.sum(jnp.where(vocab_ref[...] == ids_ref[...], logits, 0.0), axis=0, keepdims=True)
-    out_ref[...] = jnp.concatenate(
-        [row_top, row_total, moment, chosen, jnp.zeros((4, row_top.shape[1]), jnp.float32)], axis=0
+    row_total = jnp.sum(weights, axis=1, keepdims=True)
+    moment = jnp.sum(jnp.where(real, weights * logits, 0.0), axis=1, keepdims=True)
+    chosen = jnp.sum(jnp.where(vocab_ref[...] == ids_ref[...], logits, 0.0), axis=1, keepdims=True)
+    lane = lax.broadcasted_iota(jnp.int32, out_ref.shape, 1)
+    out_ref[...] = jnp.where(
+        lane == 0, row_top, jnp.where(lane == 1, row_total, jnp.where(lane == 2, moment, jnp.where(lane == 3, chosen, 0.0)))
     )
 
 
@@ -38,28 +37,28 @@
     slice_width = head_weight.shape[0]
     head = jnp.concatenate(
         [head_weight, jnp.zeros((VOCAB_PAD - slice_width, width), head_weight.dtype)], axis=0
-    )
+    ).T
     vocab = jnp.concatenate(
         [vocab_ids, jnp.full((VOCAB_PAD - slice_width,), -1, jnp.int32)]
-    )[:, None]
+    )[None, :]
     out = pl.pallas_call(
         stats_kernel,
         grid=(count // tile,),
         in_specs=[
-            pl.BlockSpec((VOCAB_PAD, width), lambda i: (0, 0)),
-            pl.BlockSpec((VOCAB_PAD, 1), lambda i: (0, 0)),
-            pl.BlockSpec((1, tile), lambda i: (0, i)),
+            pl.BlockSpec((width, VOCAB_PAD), lambda i: (0, 0)),
+            pl.BlockSpec((1, VOCAB_PAD), lambda i: (0, 0)),
+            pl.BlockSpec((tile, 1), lambda i: (i, 0)),
             pl.BlockSpec((tile, width), lambda i: (i, 0)),
         ],
-        out_specs=pl.BlockSpec((8, tile), lambda i: (0, i)),
-        out_shape=jax.ShapeDtypeStruct((8, count), jnp.float32),
+        out_specs=pl.BlockSpec((tile, 128), lambda i: (i, 0)),
+        out_shape=jax.ShapeDtypeStruct((count, 128), jnp.float32),
         cost_estimate=pl.CostEstimate(
             flops=2 * VOCAB_PAD * width * count,
             transcendentals=VOCAB_PAD * count,
-            bytes_accessed=count * width * 2 + VOCAB_PAD * width * 2 + count * 36,
+            bytes_accessed=count * width * 2 + VOCAB_PAD * width * 2 + count * 516,
         ),
-    )(head, vocab, ids[None, :], rows)
-    return out[0], out[1], out[2], out[3]
+    )(head, vocab, ids[:, None], rows)
+    return out[:, 0], out[:, 1], out[:, 2], out[:, 3]
 
 
 def shards(hidden, norm_gain, head_weight, targets, lengths, padding_mask, owner_map):

time: 154 us -> 159 us (1.032)
  local copies, waits for them, and re-layouts: 9.56 us -> 15.7 us
    slice x1, local copies, waits for them, and re-layouts: 1.21 us -> 6.45 us  [slice_stats(): return (out[:, 0], out[:, 1], out[:, 2], out[:, 3])]
    concatenate x1 -> x0, local copies, waits for them, and re-layouts: 1.89 us -> none  [slice_stats(): jnp.concatenate([head_weight, jnp.zeros((VOCAB_PAD - slice_width, width),...]
  transfers between devices with their start and end apart: 3 -> 3, of which waited for: 3 -> 3; matrix products, arithmetic and copies ran while one was open for 6% -> 5% of each run, Pallas kernels for 0% -> 0%
where the time goes in v7:
time: 159 us
  blocking collectives  58.5 us (37%)
  waiting for transfers between devices  42.3 us (27%)
  local copies, waits for them, and re-layouts  15.7 us (10%)
  between operations  14.2 us (9%)
  starting transfers between devices  13.4 us (8%)
  Pallas kernels  7.89 us (5%)
  other arithmetic  6.62 us (4%)
    all_gather x1, blocking collectives, shards(): meta = lax.all_gather(jnp.stack([targets, padding_mask]), 'tok', axis=0)  58.5 us
    all_gather x1, waiting for transfers between devices, shards(): gathered = lax.all_gather(normed, 'tok', axis=0, tiled=True)  27.8 us
    all_to_all x1, waiting for transfers between devices, shards(): incoming = lax.all_to_all(outgoing, 'tok', 0, 0, tiled=True)  11.1 us
    all_to_all x1, starting transfers between devices, shards(): incoming = lax.all_to_all(outgoing, 'tok', 0, 0, tiled=True)  9.44 us
    pallas_call x1, Pallas kernels, slice_stats(): pl.pallas_call(stats_kernel, grid=(count // tile,), in_specs=[pl.BlockSpe...  7.89 us
    slice x1, local copies, waits for them, and re-layouts, slice_stats(): return (out[:, 0], out[:, 1], out[:, 2], out[:, 3])  6.45 us
    all_to_all x1, starting transfers between devices, shards(): got = lax.all_to_all(rep_pair, 'rep', 0, 0, tiled=True)  3.94 us
    all_to_all x1, waiting for transfers between devices, shards(): got = lax.all_to_all(rep_pair, 'rep', 0, 0, tiled=True)  3.3 us
  transfers between devices with their start and end apart: 3, of which 3 were waited for; matrix products, arithmetic and copies ran while one was open for 5% of the time, Pallas kernels for 0%

profile of v7, /device:TPU:1, one launch (start us, length us, event | category | flops | bytes accessed | tf_op | source)
XLA Modules:
  0.0 158.6 jit_solution(14045364353945452588)
XLA Ops:
  7.2 0.9 fusion.1
  8.1 0.7 convert_element_type.16
  8.8 1.5 fusion.3
  10.4 0.7 copy.47
  11.3 0.7 add_bitcast_fusion
  12.0 58.5 %all-gather.1 = s32[128,2,24]{2,1,0:T(2,128)S(1)} all-gather(s32[1,2,24]{2,1,0:T(2,128)S(1)} %add_bitcast_fusion), channel_id=2, replica_groups=mesh['tok'=128,'rep'=4] {'tok'}, dimensions={0}, use_global_device_ids=true | all-gather | bytes 24768 | tf_op jit(solution)/shard_map/all_gather | solution.py:82
  70.5 0.2 fusion.5
  70.8 1.3 copy.44
  72.1 1.6 %broadcast_in_dim_reshape_squeeze.5.ids_ref = s32[3072,1]{1,0:T(8,128)} reshape(s32[128,24]{1,0:T(8,128)S(1)} %get-tuple-element.28) | data formatting | bytes 24576 | tf_op jit(solution)/shard_map/broadcast_in_dim;reshape;squeeze | solution.py:60
  73.7 0.6 concatenate.17
  74.3 0.2 convert_reduce_fusion.1
  74.6 0.2 convert_reduce_fusion
  74.8 0.9 pad_bitcast_fusion.head_ref
  75.7 27.8 %all-gather.4.cloned.1.call-done.rows_ref = bf16[3072,1024]{1,0:T(8,128)(2,1)} async-done(((bf16[24,1024]{1,0:T(8,128)(2,1)}), bf16[3072,1024]{1,0:T(8,128)(2,1)}) %all-gather.4.cloned.1.call-update) | async-done | bytes 6291472 | tf_op jit(solution)/shard_map/all_gather | solution.py:81
  103.6 7.9 %shard_map.94 = f32[3072,128]{1,0:T(8,128)} custom-call(bf16[1024,256]{1,0:T(8,128)(2,1)} %pad_bitcast_fusion.head_ref, s32[1,256]{1,0:T(1,128)} %bitcast.38, s32[3072,1]{1,0:T(8,128)} %broadcast_in_dim_reshape_squeeze.5.ids_ref, bf16[3072,1024]{1,0:T(8,128)(2,1)} %all-gather.4.cloned.1.call-done.rows_ref), custom_call_target="tpu_custom_call" | custom-call | flops 1610612736 | bytes 8400896 | tf_op jit(solution)/shard_map/pallas_call | solution.py:44
  111.5 6.4 %slice_reduce_fusion.2 = (f32[3072]{0:T(1024)S(1)}, f32[3072]{0:T(1024)S(1)}, f32[3072]{0:T(1024)S(1)}, f32[3072]{0:T(1024)S(1)}) fusion(f32[3072,128]{1,0:T(8,128)} %shard_map.94), kind=kLoop, calls=%fused_computation.2 | loop fusion | bytes 98304 | tf_op jit(solution)/shard_map/slice | solution.py:61
  118.6 0.3 select_reduce_fusion
  118.9 0.1 select_reduce_fusion.2
  119.0 0.3 copy.50
  119.3 0.7 reshape.198
  120.0 0.7 copy.52
  120.8 9.4 %all-to-all-start = ((f32[128,1,112]{2,1,0:T(1,128)}), f32[128,1,112]{2,1,0:T(1,128)S(1)}, u32[]{:S(2)}, u32[]{:S(2)}) async-start(f32[128,1,112]{2,1,0:T(1,128)} %copy.52), calls=%async_computation | async-start | bytes 131072 | tf_op jit(solution)/shard_map/all_to_all | solution.py:114
  130.3 0.2 dynamic-slice_reduce_fusion
  130.5 11.1 %all-to-all-done = f32[128,1,112]{2,1,0:T(1,128)S(1)} async-done(((f32[128,1,112]{2,1,0:T(1,128)}), f32[128,1,112]{2,1,0:T(1,128)S(1)}, u32[]{:S(2)}, u32[]{:S(2)}) %all-to-all-start) | async-done | bytes 57376 | tf_op jit(solution)/shard_map/all_to_all | solution.py:114
  141.8 0.3 fusion.6
  142.3 0.7 copy.58
  143.0 3.9 %all-to-all-start.1 = ((f32[4,2,2]{1,2,0:T(2,128)}), f32[4,2,2]{1,2,0:T(2,128)S(1)}, u32[]{:S(2)}, u32[]{:S(2)}) async-start(f32[4,2,2]{1,2,0:T(2,128)} %copy.58), calls=%async_computation.1 | async-start | bytes 8192 | tf_op jit(solution)/shard_map/all_to_all | solution.py:131
  147.0 0.1 reduce_max.47
  147.1 0.2 multiply_reduce_fusion
  147.3 0.5 compare_select_fusion
  147.8 3.3 %all-to-all-done.1 = f32[4,2,2]{1,2,0:T(2,128)S(1)} async-done(((f32[4,2,2]{1,2,0:T(2,128)}), f32[4,2,2]{1,2,0:T(2,128)S(1)}, u32[]{:S(2)}, u32[]{:S(2)}) %all-to-all-start.1) | async-done | bytes 96 | tf_op jit(solution)/shard_map/all_to_all | solution.py:131
  151.1 0.6 copy.59
  (40 shorter events, 1.7 us)
Async XLA Ops:
  7.2 96.4 %all-gather.4.cloned.1.call-start = ((), (), s32[]{:S(2)}) async-start(), calls=%async_computation.2 | async-start | bytes 6340608 | tf_op jit(solution)/shard_map/all_gather | solution.py:81
  12.0 62.3 %copy-start.1 = (s32[64]{0:T(128)S(1)}, s32[64]{0:T(128)}, u32[]{:S(2)}) copy-start(s32[64]{0:T(128)} %param.13) | copy-start | bytes 772
  118.4 28.9 %copy-start = (s32[24]{0:T(128)S(1)}, s32[24]{0:T(128)}, u32[]{:S(2)}) copy-start(s32[24]{0:T(128)} %param.12) | copy-start | bytes 292
  120.8 20.9 %all-to-all-start = ((f32[128,1,112]{2,1,0:T(1,128)}), f32[128,1,112]{2,1,0:T(1,128)S(1)}, u32[]{:S(2)}, u32[]{:S(2)}) async-start(f32[128,1,112]{2,1,0:T(1,128)} %copy.52), calls=%async_computation | async-start | bytes 131072 | tf_op jit(solution)/shard_map/all_to_all | solution.py:114
  143.0 8.1 %all-to-all-start.1 = ((f32[4,2,2]{1,2,0:T(2,128)}), f32[4,2,2]{1,2,0:T(2,128)S(1)}, u32[]{:S(2)}, u32[]{:S(2)}) async-start(f32[4,2,2]{1,2,0:T(2,128)} %copy.58), calls=%async_computation.1 | async-start | bytes 8192 | tf_op jit(solution)/shard_map/all_to_all | solution.py:131
Sparse Core Ops, SparseCore 0:
  11.1 92.3 all-gather.3

commit v8 on v5

--- a/solution.py
+++ b/solution.py
@@ -108,13 +108,16 @@
     )
     req_max = jnp.max(jnp.where(slot_hot, part_max[:, None, None], NEG_FILL), axis=0)
     req_norm = jnp.sum(jnp.where(slot_hot, part_norm[:, None, None], 0.0), axis=0)
-    req = jnp.stack([req_max, req_norm], axis=2).reshape(tok_count, rep_count * SLOTS * 2)
+    req = jnp.stack([req_max, req_norm], axis=2).reshape(tok_count * rep_count, SLOTS * 2)
 
     stats = jnp.stack([top_p, total_p, moment_p, chosen_p], axis=2).reshape(tok_count, local_rows * 4)
-    outgoing = jnp.concatenate([stats, req], axis=1)
-    incoming = lax.all_to_all(outgoing, "tok", 0, 0, tiled=True)
+    same_rep = jnp.arange(rep_count, dtype=jnp.int32)[None, :, None] == rep_place
+    spread = jnp.where(same_rep, stats[:, None, :], 0.0).reshape(tok_count * rep_count, local_rows * 4)
+    outgoing = jnp.concatenate([spread, req], axis=1)
+    incoming = lax.all_to_all(outgoing, ("tok", "rep"), 0, 0, tiled=True)
 
-    in_stats = incoming[:, : local_rows * 4].reshape(tok_count, local_rows, 4)
+    by_rep = incoming[:, : local_rows * 4].reshape(tok_count, rep_count, local_rows * 4)
+    in_stats = lax.dynamic_index_in_dim(by_rep, rep_place, 1, keepdims=False).reshape(tok_count, local_rows, 4)
     tops = in_stats[:, :, 0]
     row_top = jnp.max(tops, axis=0)
     scale = jnp.exp(tops - row_top[None, :])
@@ -125,13 +128,9 @@
     logprob = jnp.where(live_row, row_chosen - row_top - log_total, 0.0)
     entropy = jnp.where(live_row, row_top + log_total - row_moment / row_total, 0.0)
 
-    in_req = incoming[:, local_rows * 4:].reshape(tok_count, rep_count, SLOTS, 2)
-    rep_max = jnp.max(in_req[..., 0], axis=0)
-    rep_norm = jnp.sum(in_req[..., 1], axis=0)
-    rep_pair = jnp.stack([rep_max, rep_norm], axis=2)
-    got = lax.all_to_all(rep_pair, "rep", 0, 0, tiled=True)
-    final_max = jnp.max(got[..., 0], axis=0)
-    final_norm = jnp.sum(got[..., 1], axis=0)
+    in_req = incoming[:, local_rows * 4:].reshape(tok_count * rep_count, SLOTS, 2)
+    final_max = jnp.max(in_req[..., 0], axis=0)
+    final_norm = jnp.sum(in_req[..., 1], axis=0)
     has_slot = jnp.any(slot_hot[:, device_place, :], axis=0)
     request_table = jnp.where(
         has_slot[:, None], jnp.stack([final_max, final_norm], axis=1), 0.0

time: 154 us -> 154 us (level)
  local copies, waits for them, and re-layouts: 9.56 us -> 7.73 us
    all_to_all x2 -> x1, waiting for transfers between devices: 14.4 us -> 16.1 us  [shards(): incoming = lax.all_to_all(outgoing, ('tok', 'rep'), 0, 0, tiled=True)]
    all_to_all x2 -> x1, starting transfers between devices: 13.4 us -> 13.1 us  [shards(): incoming = lax.all_to_all(outgoing, ('tok', 'rep'), 0, 0, tiled=True)]
  transfers between devices with their start and end apart: 3 -> 2, of which waited for: 3 -> 2; matrix products, arithmetic and copies ran while one was open for 6% -> 5% of each run, Pallas kernels for 0% -> 0%
where the time goes in v8:
time: 154 us; the launch traced here: 153 us
  blocking collectives  58.5 us (38%)
  waiting for transfers between devices  43.3 us (28%)
  between operations  14.3 us (9%)
  starting transfers between devices  13.2 us (9%)
  other arithmetic  8.94 us (6%)
  local copies, waits for them, and re-layouts  7.73 us (5%)
  Pallas kernels  7.44 us (5%)
    all_gather x1, blocking collectives, shards(): meta = lax.all_gather(jnp.stack([targets, padding_mask]), 'tok', axis=0)  58.5 us
    all_gather x1, waiting for transfers between devices, shards(): gathered = lax.all_gather(normed, 'tok', axis=0, tiled=True)  27.2 us
    all_to_all x1, waiting for transfers between devices, shards(): incoming = lax.all_to_all(outgoing, ('tok', 'rep'), 0, 0, tiled=True)  16.1 us
    all_to_all x1, starting transfers between devices, shards(): incoming = lax.all_to_all(outgoing, ('tok', 'rep'), 0, 0, tiled=True)  13.1 us
    pallas_call x1, Pallas kernels, slice_stats(): pl.pallas_call(stats_kernel, grid=(count // tile,), in_specs=[pl.BlockSpe...  7.44 us
  transfers between devices with their start and end apart: 2, of which 2 were waited for; matrix products, arithmetic and copies ran while one was open for 5% of the time, Pallas kernels for 0%

profile of v8, /device:TPU:1, one launch (start us, length us, event | category | flops | bytes accessed | tf_op | source)
XLA Modules:
  0.0 153.4 jit_solution(16166820567618526484)
XLA Ops:
  7.2 0.9 fusion.1
  8.1 0.7 convert_element_type.16
  8.8 1.5 fusion.3
  10.4 0.1 broadcast_in_dim.122
  10.5 0.7 copy.54
  11.5 0.7 add_bitcast_fusion
  12.1 58.5 %all-gather.1 = s32[128,2,24]{2,1,0:T(2,128)S(1)} all-gather(s32[1,2,24]{2,1,0:T(2,128)S(1)} %add_bitcast_fusion), channel_id=2, replica_groups=mesh['tok'=128,'rep'=4] {'tok'}, dimensions={0}, use_global_device_ids=true | all-gather | bytes 24768 | tf_op jit(solution)/shard_map/all_gather | solution.py:83
  70.6 0.2 fusion.5
  70.9 0.7 broadcast_in_dim_reshape_squeeze.4.ids_ref
  71.6 0.8 copy.51.vocab_ref
  72.4 1.9 %concatenate.16.head_ref = bf16[256,1024]{1,0:T(8,128)(2,1)} pad(bf16[251,1024]{1,0:T(8,128)(2,1)} %param.9, bf16[]{:T(256)} %constant.19.clone.1), padding=0_5x0_0 | pad | bytes 1038338 | tf_op jit(solution)/shard_map/concatenate | solution.py:39
  74.3 0.9 convert_reduce_fusion.1
  75.3 0.2 convert_reduce_fusion
  75.6 0.7 iota_compare_fusion.1
  76.3 27.2 %all-gather.4.cloned.1.call-done.rows_ref = bf16[3072,1024]{1,0:T(8,128)(2,1)} async-done(((bf16[24,1024]{1,0:T(8,128)(2,1)}), bf16[3072,1024]{1,0:T(8,128)(2,1)}) %all-gather.4.cloned.1.call-update) | async-done | bytes 6291472 | tf_op jit(solution)/shard_map/all_gather | solution.py:82
  103.5 7.4 %shard_map.94 = f32[8,3072]{1,0:T(8,128)} custom-call(bf16[256,1024]{1,0:T(8,128)(2,1)} %concatenate.16.head_ref, s32[256,1]{1,0:T(8,128)} %copy.51.vocab_ref, s32[1,3072]{1,0:T(1,128)} %broadcast_in_dim_reshape_squeeze.4.ids_ref, bf16[3072,1024]{1,0:T(8,128)(2,1)} %all-gather.4.cloned.1.call-done.rows_ref), custom_call_target="tpu_custom_call" | custom-call | flops 1610612736 | bytes 6926336 | tf_op jit(solution)/shard_map/pallas_call | solution.py:45
  111.0 1.2 slice_reduce_fusion.7
  113.0 0.3 select_reduce_fusion
  113.3 0.1 select_reduce_fusion.2
  113.5 0.1 copy.58
  113.7 0.1 broadcast_select_fusion
  113.8 0.8 pad_maximum_fusion.1
  114.6 13.1 %all-to-all-start = ((f32[512,1,100]{2,1,0:T(1,128)}), f32[512,1,100]{2,1,0:T(1,128)S(1)}, u32[]{:S(2)}, u32[]{:S(2)}) async-start(f32[512,1,100]{2,1,0:T(1,128)} %bitcast.11), calls=%async_computation | async-start | bytes 524288 | tf_op jit(solution)/shard_map/all_to_all | solution.py:117
  127.9 0.2 dynamic-slice_reduce_fusion
  128.1 16.1 %all-to-all-done = f32[512,1,100]{2,1,0:T(1,128)S(1)} async-done(((f32[512,1,100]{2,1,0:T(1,128)}), f32[512,1,100]{2,1,0:T(1,128)S(1)}, u32[]{:S(2)}, u32[]{:S(2)}) %all-to-all-start) | async-done | bytes 204832 | tf_op jit(solution)/shard_map/all_to_all | solution.py:117
  144.2 0.1 slice.67
  144.5 0.3 fusion.6
  144.9 0.1 slice_reduce_fusion.6
  145.0 0.7 copy.64
  145.7 0.1 reduce_max.38
  145.8 0.2 multiply_reduce_fusion
  146.0 0.5 compare_select_fusion
  (38 shorter events, 1.6 us)
Async XLA Ops:
  7.2 96.4 %all-gather.4.cloned.1.call-start = ((), (), s32[]{:S(2)}) async-start(), calls=%async_computation.1 | async-start | bytes 6340608 | tf_op jit(solution)/shard_map/all_gather | solution.py:82
  75.5 70.5 %copy-start = (s32[24]{0:T(128)S(1)}, s32[24]{0:T(128)}, u32[]{:S(2)}) copy-start(s32[24]{0:T(128)} %param.12) | copy-start | bytes 292
  114.6 29.6 %all-to-all-start = ((f32[512,1,100]{2,1,0:T(1,128)}), f32[512,1,100]{2,1,0:T(1,128)S(1)}, u32[]{:S(2)}, u32[]{:S(2)}) async-start(f32[512,1,100]{2,1,0:T(1,128)} %bitcast.11), calls=%async_computation | async-start | bytes 524288 | tf_op jit(solution)/shard_map/all_to_all | solution.py:117
Sparse Core Ops, SparseCore 0:
  11.1 92.3 all-gather.3

commit v9 on v5

--- a/solution.py
+++ b/solution.py
@@ -12,7 +12,7 @@
 NEG_FILL = -1e30
 
 
-TILE = 512
+TILE = 1024
 VOCAB_PAD = 256
 
 
@@ -62,6 +62,27 @@
     return out[0], out[1], out[2], out[3]
 
 
+def norm_kernel(hidden_ref, gain_ref, normed_ref, square_ref):
+    widened = hidden_ref[...].astype(jnp.float32)
+    mean_square = jnp.mean(widened * widened, axis=1, keepdims=True)
+    normed_ref[...] = (
+        widened * lax.rsqrt(mean_square + EPSILON) * gain_ref[...].astype(jnp.float32)
+    ).astype(normed_ref.dtype)
+    square_ref[...] = jnp.broadcast_to(mean_square, square_ref.shape)
+
+
+def rms_norm(hidden, norm_gain):
+    rows, width = hidden.shape
+    normed, square = pl.pallas_call(
+        norm_kernel,
+        out_shape=(
+            jax.ShapeDtypeStruct((rows, width), jnp.bfloat16),
+            jax.ShapeDtypeStruct((rows, 128), jnp.float32),
+        ),
+    )(hidden, norm_gain[None, :])
+    return normed, square[:, 0]
+
+
 def shards(hidden, norm_gain, head_weight, targets, lengths, padding_mask, owner_map):
     tok_count = lax.axis_size("tok")
     rep_count = lax.axis_size("rep")
@@ -71,11 +92,7 @@
     slice_width = head_weight.shape[0]
     seq_count = lengths.shape[0]
 
-    widened = hidden.astype(jnp.float32)
-    mean_square = jnp.mean(widened * widened, axis=1)
-    normed = (
-        widened * lax.rsqrt(mean_square + EPSILON)[:, None] * norm_gain.astype(jnp.float32)[None, :]
-    ).astype(jnp.bfloat16)
+    normed, mean_square = rms_norm(hidden, norm_gain)
     state_norm = jnp.sqrt(mean_square)
     live_row = padding_mask == 1
 

time: 154 us -> 152 us (0.987)
  other arithmetic: 8 us -> 4.94 us
  local copies, waits for them, and re-layouts: 9.56 us -> 11.7 us
    convert_element_type x2 -> x0, other arithmetic: 2.18 us -> none  [the longest x1 1.49 us: shards(): normed = (widened * lax.rsqrt(mean_square + EPSILON)[:, None] * norm_gain...]
where the time goes in v9:
time: 152 us
  blocking collectives  58.4 us (38%)
  waiting for transfers between devices  41.3 us (27%)
  between operations  14.2 us (9%)
  starting transfers between devices  13.5 us (9%)
  local copies, waits for them, and re-layouts  11.7 us (8%)
  Pallas kernels  7.83 us (5%)
  other arithmetic  4.94 us (3%)
    all_gather x1, blocking collectives, shards(): meta = lax.all_gather(jnp.stack([targets, padding_mask]), 'tok', axis=0)  58.4 us
    all_gather x1, waiting for transfers between devices, shards(): gathered = lax.all_gather(normed, 'tok', axis=0, tiled=True)  26.8 us
    all_to_all x1, waiting for transfers between devices, shards(): incoming = lax.all_to_all(outgoing, 'tok', 0, 0, tiled=True)  11.1 us
    all_to_all x1, starting transfers between devices, shards(): incoming = lax.all_to_all(outgoing, 'tok', 0, 0, tiled=True)  9.44 us
    pallas_call x1, Pallas kernels, slice_stats(): pl.pallas_call(stats_kernel, grid=(count // tile,), in_specs=[pl.BlockSpe...  6.31 us
    all_to_all x1, starting transfers between devices, shards(): got = lax.all_to_all(rep_pair, 'rep', 0, 0, tiled=True)  3.99 us
    all_to_all x1, waiting for transfers between devices, shards(): got = lax.all_to_all(rep_pair, 'rep', 0, 0, tiled=True)  3.3 us
  transfers between devices with their start and end apart: 3, of which 3 were waited for; matrix products, arithmetic and copies ran while one was open for 6% of the time, Pallas kernels for 0%

profile of v9, /device:TPU:1, one launch (start us, length us, event | category | flops | bytes accessed | tf_op | source)
XLA Modules:
  0.0 151.8 jit_solution(13436216681764477583)
XLA Ops:
  7.2 1.3 broadcast_in_dim.96.gain_ref
  8.5 1.5 %shard_map.94 = (bf16[24,1024]{1,0:T(8,128)(2,1)}, f32[24,128]{1,0:T(8,128)}) custom-call(bf16[24,1024]{1,0:T(8,128)(2,1)} %hidden_ref.1, bf16[1,1024]{1,0:T(2,128)(2,1)} %broadcast_in_dim.96.gain_ref), custom_call_target="tpu_custom_call" | custom-call | tf_op jit(solution)/shard_map/pallas_call | solution.py:76
  10.0 0.7 copy.43
  11.0 0.7 add_bitcast_fusion
  11.7 58.4 %all-gather.1 = s32[128,2,24]{2,1,0:T(2,128)S(1)} all-gather(s32[1,2,24]{2,1,0:T(2,128)S(1)} %add_bitcast_fusion), channel_id=2, replica_groups=mesh['tok'=128,'rep'=4] {'tok'}, dimensions={0}, use_global_device_ids=true | all-gather | bytes 24768 | tf_op jit(solution)/shard_map/all_gather | solution.py:100
  70.2 0.2 fusion.2
  70.5 0.7 broadcast_in_dim_reshape_squeeze.4.ids_ref
  71.2 0.8 copy.41.vocab_ref
  72.0 1.9 %concatenate.16.head_ref = bf16[256,1024]{1,0:T(8,128)(2,1)} pad(bf16[251,1024]{1,0:T(8,128)(2,1)} %param.9, bf16[]{:T(256)} %constant.16.clone.1), padding=0_5x0_0 | pad | bytes 1038338 | tf_op jit(solution)/shard_map/concatenate | solution.py:39
  73.9 0.8 sqrt_reduce_fusion
  74.7 0.9 convert_reduce_fusion.1
  75.8 0.2 convert_reduce_fusion
  76.0 0.7 iota_compare_fusion.1
  76.7 26.8 %all-gather.4.cloned.1.call-done.rows_ref = bf16[3072,1024]{1,0:T(8,128)(2,1)} async-done(((bf16[24,1024]{1,0:T(8,128)(2,1)}), bf16[3072,1024]{1,0:T(8,128)(2,1)}) %all-gather.4.cloned.1.call-update) | async-done | bytes 6291472 | tf_op jit(solution)/shard_map/all_gather | solution.py:99
  103.5 6.3 %shard_map.95 = f32[8,3072]{1,0:T(8,128)} custom-call(bf16[256,1024]{1,0:T(8,128)(2,1)} %concatenate.16.head_ref, s32[256,1]{1,0:T(8,128)} %copy.41.vocab_ref, s32[1,3072]{1,0:T(1,128)} %broadcast_in_dim_reshape_squeeze.4.ids_ref, bf16[3072,1024]{1,0:T(8,128)(2,1)} %all-gather.4.cloned.1.call-done.rows_ref), custom_call_target="tpu_custom_call" | custom-call | flops 1610612736 | bytes 6926336 | tf_op jit(solution)/shard_map/pallas_call | solution.py:45
  109.8 1.2 slice_reduce_fusion.9
  111.7 0.3 select_reduce_fusion
  112.0 0.1 select_reduce_fusion.2
  112.2 0.3 copy.46
  112.5 0.7 reshape.189
  113.2 0.7 copy.48
  113.9 9.4 %all-to-all-start = ((f32[128,1,112]{2,1,0:T(1,128)}), f32[128,1,112]{2,1,0:T(1,128)S(1)}, u32[]{:S(2)}, u32[]{:S(2)}) async-start(f32[128,1,112]{2,1,0:T(1,128)} %copy.48), calls=%async_computation | async-start | bytes 131072 | tf_op jit(solution)/shard_map/all_to_all | solution.py:132
  123.5 0.2 dynamic-slice_reduce_fusion
  123.7 11.1 %all-to-all-done = f32[128,1,112]{2,1,0:T(1,128)S(1)} async-done(((f32[128,1,112]{2,1,0:T(1,128)}), f32[128,1,112]{2,1,0:T(1,128)S(1)}, u32[]{:S(2)}, u32[]{:S(2)}) %all-to-all-start) | async-done | bytes 57376 | tf_op jit(solution)/shard_map/all_to_all | solution.py:132
  134.9 0.3 fusion.3
  135.5 0.7 copy.54
  136.2 4.0 %all-to-all-start.1 = ((f32[4,2,2]{1,2,0:T(2,128)}), f32[4,2,2]{1,2,0:T(2,128)S(1)}, u32[]{:S(2)}, u32[]{:S(2)}) async-start(f32[4,2,2]{1,2,0:T(2,128)} %copy.54), calls=%async_computation.1 | async-start | bytes 8192 | tf_op jit(solution)/shard_map/all_to_all | solution.py:149
  140.2 0.1 reduce_max.47
  140.3 0.2 multiply_reduce_fusion
  140.5 0.5 compare_select_fusion
  141.0 3.3 %all-to-all-done.1 = f32[4,2,2]{1,2,0:T(2,128)S(1)} async-done(((f32[4,2,2]{1,2,0:T(2,128)}), f32[4,2,2]{1,2,0:T(2,128)S(1)}, u32[]{:S(2)}, u32[]{:S(2)}) %all-to-all-start.1) | async-done | bytes 96 | tf_op jit(solution)/shard_map/all_to_all | solution.py:149
  144.3 0.6 copy.55
  (37 shorter events, 1.6 us)
Async XLA Ops:
  7.2 96.4 %all-gather.4.cloned.1.call-start = ((), (), s32[]{:S(2)}) async-start(), calls=%async_computation.2 | async-start | bytes 6340608 | tf_op jit(solution)/shard_map/all_gather | solution.py:99
  11.0 129.5 %copy-start = (s32[24]{0:T(128)S(1)}, s32[24]{0:T(128)}, u32[]{:S(2)}) copy-start(s32[24]{0:T(128)} %param.12) | copy-start | bytes 292
  113.9 20.9 %all-to-all-start = ((f32[128,1,112]{2,1,0:T(1,128)}), f32[128,1,112]{2,1,0:T(1,128)S(1)}, u32[]{:S(2)}, u32[]{:S(2)}) async-start(f32[128,1,112]{2,1,0:T(1,128)} %copy.48), calls=%async_computation | async-start | bytes 131072 | tf_op jit(solution)/shard_map/all_to_all | solution.py:132
  136.2 8.1 %all-to-all-start.1 = ((f32[4,2,2]{1,2,0:T(2,128)}), f32[4,2,2]{1,2,0:T(2,128)S(1)}, u32[]{:S(2)}, u32[]{:S(2)}) async-start(f32[4,2,2]{1,2,0:T(2,128)} %copy.54), calls=%async_computation.1 | async-start | bytes 8192 | tf_op jit(solution)/shard_map/all_to_all | solution.py:149
Sparse Core Ops, SparseCore 0:
  11.1 92.3 all-gather.3

commit v10 on v9

--- a/solution.py
+++ b/solution.py
@@ -66,7 +66,7 @@
     widened = hidden_ref[...].astype(jnp.float32)
     mean_square = jnp.mean(widened * widened, axis=1, keepdims=True)
     normed_ref[...] = (
-        widened * lax.rsqrt(mean_square + EPSILON) * gain_ref[...].astype(jnp.float32)
+        widened * lax.rsqrt(mean_square + EPSILON) * gain_ref[...].astype(jnp.float32)[None, :]
     ).astype(normed_ref.dtype)
     square_ref[...] = jnp.broadcast_to(mean_square, square_ref.shape)
 
@@ -79,7 +79,7 @@
             jax.ShapeDtypeStruct((rows, width), jnp.bfloat16),
             jax.ShapeDtypeStruct((rows, 128), jnp.float32),
         ),
-    )(hidden, norm_gain[None, :])
+    )(hidden, norm_gain)
     return normed, square[:, 0]
 
 

time: 152 us -> 152 us (level)
  no operation moved by 1% of the time
where the time goes in v10:
time: 152 us
  blocking collectives  58.5 us (38%)
  waiting for transfers between devices  42.5 us (28%)
  between operations  14.2 us (9%)
  starting transfers between devices  13.5 us (9%)
  local copies, waits for them, and re-layouts  10.4 us (7%)
  Pallas kernels  7.83 us (5%)
  other arithmetic  4.95 us (3%)
    all_gather x1, blocking collectives, shards(): meta = lax.all_gather(jnp.stack([targets, padding_mask]), 'tok', axis=0)  58.5 us
    all_gather x1, waiting for transfers between devices, shards(): gathered = lax.all_gather(normed, 'tok', axis=0, tiled=True)  28.1 us
    all_to_all x1, waiting for transfers between devices, shards(): incoming = lax.all_to_all(outgoing, 'tok', 0, 0, tiled=True)  11.1 us
    all_to_all x1, starting transfers between devices, shards(): incoming = lax.all_to_all(outgoing, 'tok', 0, 0, tiled=True)  9.46 us
    pallas_call x1, Pallas kernels, slice_stats(): pl.pallas_call(stats_kernel, grid=(count // tile,), in_specs=[pl.BlockSpe...  6.31 us
    all_to_all x1, starting transfers between devices, shards(): got = lax.all_to_all(rep_pair, 'rep', 0, 0, tiled=True)  3.97 us
    all_to_all x1, waiting for transfers between devices, shards(): got = lax.all_to_all(rep_pair, 'rep', 0, 0, tiled=True)  3.3 us
  transfers between devices with their start and end apart: 3, of which 3 were waited for; matrix products, arithmetic and copies ran while one was open for 6% of the time, Pallas kernels for 0%

profile of v10, /device:TPU:1, one launch (start us, length us, event | category | flops | bytes accessed | tf_op | source)
XLA Modules:
  0.0 151.8 jit_solution(10741887302232994123)
XLA Ops:
  7.2 1.5 %shard_map.94 = (bf16[24,1024]{1,0:T(8,128)(2,1)}, f32[24,128]{1,0:T(8,128)}) custom-call(bf16[24,1024]{1,0:T(8,128)(2,1)} %hidden_ref.1, bf16[1024]{0:T(1024)(128)(2,1)} %gain_ref.1), custom_call_target="tpu_custom_call" | custom-call | tf_op jit(solution)/shard_map/pallas_call | solution.py:76
  8.8 0.7 copy.43
  9.7 0.7 add_bitcast_fusion
  10.5 58.5 %all-gather.1 = s32[128,2,24]{2,1,0:T(2,128)S(1)} all-gather(s32[1,2,24]{2,1,0:T(2,128)S(1)} %add_bitcast_fusion), channel_id=2, replica_groups=mesh['tok'=128,'rep'=4] {'tok'}, dimensions={0}, use_global_device_ids=true | all-gather | bytes 24768 | tf_op jit(solution)/shard_map/all_gather | solution.py:100
  68.9 0.2 fusion.2
  69.2 0.7 broadcast_in_dim_reshape_squeeze.4.ids_ref
  69.9 0.8 copy.41.vocab_ref
  70.7 1.9 %concatenate.16.head_ref = bf16[256,1024]{1,0:T(8,128)(2,1)} pad(bf16[251,1024]{1,0:T(8,128)(2,1)} %param.9, bf16[]{:T(256)} %constant.16.clone.1), padding=0_5x0_0 | pad | bytes 1038338 | tf_op jit(solution)/shard_map/concatenate | solution.py:39
  72.6 0.8 sqrt_reduce_fusion
  73.5 0.9 convert_reduce_fusion.1
  74.5 0.2 convert_reduce_fusion
  74.7 0.7 iota_compare_fusion.1
  75.4 28.1 %all-gather.4.cloned.1.call-done.rows_ref = bf16[3072,1024]{1,0:T(8,128)(2,1)} async-done(((bf16[24,1024]{1,0:T(8,128)(2,1)}), bf16[3072,1024]{1,0:T(8,128)(2,1)}) %all-gather.4.cloned.1.call-update) | async-done | bytes 6291472 | tf_op jit(solution)/shard_map/all_gather | solution.py:99
  103.5 6.3 %shard_map.95 = f32[8,3072]{1,0:T(8,128)} custom-call(bf16[256,1024]{1,0:T(8,128)(2,1)} %concatenate.16.head_ref, s32[256,1]{1,0:T(8,128)} %copy.41.vocab_ref, s32[1,3072]{1,0:T(1,128)} %broadcast_in_dim_reshape_squeeze.4.ids_ref, bf16[3072,1024]{1,0:T(8,128)(2,1)} %all-gather.4.cloned.1.call-done.rows_ref), custom_call_target="tpu_custom_call" | custom-call | flops 1610612736 | bytes 6926336 | tf_op jit(solution)/shard_map/pallas_call | solution.py:45
  109.8 1.2 slice_reduce_fusion.9
  111.7 0.3 select_reduce_fusion
  112.0 0.1 select_reduce_fusion.2
  112.2 0.3 copy.46
  112.4 0.7 reshape.189
  113.1 0.7 copy.48
  113.9 9.5 %all-to-all-start = ((f32[128,1,112]{2,1,0:T(1,128)}), f32[128,1,112]{2,1,0:T(1,128)S(1)}, u32[]{:S(2)}, u32[]{:S(2)}) async-start(f32[128,1,112]{2,1,0:T(1,128)} %copy.48), calls=%async_computation | async-start | bytes 131072 | tf_op jit(solution)/shard_map/all_to_all | solution.py:132
  123.5 0.2 dynamic-slice_reduce_fusion
  123.7 11.1 %all-to-all-done = f32[128,1,112]{2,1,0:T(1,128)S(1)} async-done(((f32[128,1,112]{2,1,0:T(1,128)}), f32[128,1,112]{2,1,0:T(1,128)S(1)}, u32[]{:S(2)}, u32[]{:S(2)}) %all-to-all-start) | async-done | bytes 57376 | tf_op jit(solution)/shard_map/all_to_all | solution.py:132
  134.9 0.3 fusion.3
  135.2 0.1 slice_reduce_fusion.6
  135.5 0.7 copy.54
  136.2 4.0 %all-to-all-start.1 = ((f32[4,2,2]{1,2,0:T(2,128)}), f32[4,2,2]{1,2,0:T(2,128)S(1)}, u32[]{:S(2)}, u32[]{:S(2)}) async-start(f32[4,2,2]{1,2,0:T(2,128)} %copy.54), calls=%async_computation.1 | async-start | bytes 8192 | tf_op jit(solution)/shard_map/all_to_all | solution.py:149
  140.1 0.1 reduce_max.47
  140.2 0.2 multiply_reduce_fusion
  140.4 0.5 compare_select_fusion
  141.0 3.3 %all-to-all-done.1 = f32[4,2,2]{1,2,0:T(2,128)S(1)} async-done(((f32[4,2,2]{1,2,0:T(2,128)}), f32[4,2,2]{1,2,0:T(2,128)S(1)}, u32[]{:S(2)}, u32[]{:S(2)}) %all-to-all-start.1) | async-done | bytes 96 | tf_op jit(solution)/shard_map/all_to_all | solution.py:149
  144.3 0.6 copy.55
  (36 shorter events, 1.5 us)
Async XLA Ops:
  7.2 96.3 %all-gather.4.cloned.1.call-start = ((), (), s32[]{:S(2)}) async-start(), calls=%async_computation.2 | async-start | bytes 6340608 | tf_op jit(solution)/shard_map/all_gather | solution.py:99
  9.7 130.7 %copy-start = (s32[24]{0:T(128)S(1)}, s32[24]{0:T(128)}, u32[]{:S(2)}) copy-start(s32[24]{0:T(128)} %param.12) | copy-start | bytes 292
  113.9 20.9 %all-to-all-start = ((f32[128,1,112]{2,1,0:T(1,128)}), f32[128,1,112]{2,1,0:T(1,128)S(1)}, u32[]{:S(2)}, u32[]{:S(2)}) async-start(f32[128,1,112]{2,1,0:T(1,128)} %copy.48), calls=%async_computation | async-start | bytes 131072 | tf_op jit(solution)/shard_map/all_to_all | solution.py:132
  136.2 8.1 %all-to-all-start.1 = ((f32[4,2,2]{1,2,0:T(2,128)}), f32[4,2,2]{1,2,0:T(2,128)S(1)}, u32[]{:S(2)}, u32[]{:S(2)}) async-start(f32[4,2,2]{1,2,0:T(2,128)} %copy.54), calls=%async_computation.1 | async-start | bytes 8192 | tf_op jit(solution)/shard_map/all_to_all | solution.py:149
Sparse Core Ops, SparseCore 0:
  11.1 92.3 all-gather.3

commit v11 on v9

--- a/solution.py
+++ b/solution.py
@@ -12,7 +12,7 @@
 NEG_FILL = -1e30
 
 
-TILE = 1024
+TILE = 1536
 VOCAB_PAD = 256
 
 
@@ -20,12 +20,11 @@
     logits = lax.dot_general(
         head_ref[...], rows_ref[...], (((1,), (1,)), ((), ())), preferred_element_type=jnp.float32
     )
-    real = vocab_ref[...] >= 0
-    logits = jnp.where(real, logits, -jnp.inf)
+    logits = jnp.where(vocab_ref[...] >= 0, logits, NEG_FILL)
     row_top = jnp.max(logits, axis=0, keepdims=True)
-    weights = jnp.where(real, jnp.exp(logits - row_top), 0.0)
+    weights = jnp.exp(logits - row_top)
     row_total = jnp.sum(weights, axis=0, keepdims=True)
-    moment = jnp.sum(jnp.where(real, weights * logits, 0.0), axis=0, keepdims=True)
+    moment = jnp.sum(weights * logits, axis=0, keepdims=True)
     chosen = jnp.sum(jnp.where(vocab_ref[...] == ids_ref[...], logits, 0.0), axis=0, keepdims=True)
     out_ref[...] = jnp.concatenate(
         [row_top, row_total, moment, chosen, jnp.zeros((4, row_top.shape[1]), jnp.float32)], axis=0

time: 152 us -> 152 us (level)
  no operation moved by 1% of the time
where the time goes in v11:
time: 152 us; the launch traced here: 151 us
  blocking collectives  58.4 us (38%)
  waiting for transfers between devices  41.3 us (27%)
  between operations  14.2 us (9%)
  starting transfers between devices  13.5 us (9%)
  local copies, waits for them, and re-layouts  11.7 us (8%)
  Pallas kernels  7.14 us (5%)
  other arithmetic  4.94 us (3%)
    all_gather x1, blocking collectives, shards(): meta = lax.all_gather(jnp.stack([targets, padding_mask]), 'tok', axis=0)  58.4 us
    all_gather x1, waiting for transfers between devices, shards(): gathered = lax.all_gather(normed, 'tok', axis=0, tiled=True)  26.8 us
    all_to_all x1, waiting for transfers between devices, shards(): incoming = lax.all_to_all(outgoing, 'tok', 0, 0, tiled=True)  11.1 us
    all_to_all x1, starting transfers between devices, shards(): incoming = lax.all_to_all(outgoing, 'tok', 0, 0, tiled=True)  9.44 us
    pallas_call x1, Pallas kernels, slice_stats(): pl.pallas_call(stats_kernel, grid=(count // tile,), in_specs=[pl.BlockSpe...  5.62 us
    all_to_all x1, starting transfers between devices, shards(): got = lax.all_to_all(rep_pair, 'rep', 0, 0, tiled=True)  4 us
    all_to_all x1, waiting for transfers between devices, shards(): got = lax.all_to_all(rep_pair, 'rep', 0, 0, tiled=True)  3.3 us
  transfers between devices with their start and end apart: 3, of which 3 were waited for; matrix products, arithmetic and copies ran while one was open for 6% of the time, Pallas kernels for 0%

profile of v11, /device:TPU:1, one launch (start us, length us, event | category | flops | bytes accessed | tf_op | source)
XLA Modules:
  0.0 151.2 jit_solution(973495305601847770)
XLA Ops:
  7.2 1.3 broadcast_in_dim.96.gain_ref
  8.5 1.5 %shard_map.94 = (bf16[24,1024]{1,0:T(8,128)(2,1)}, f32[24,128]{1,0:T(8,128)}) custom-call(bf16[24,1024]{1,0:T(8,128)(2,1)} %hidden_ref.1, bf16[1,1024]{1,0:T(2,128)(2,1)} %broadcast_in_dim.96.gain_ref), custom_call_target="tpu_custom_call" | custom-call | tf_op jit(solution)/shard_map/pallas_call | solution.py:75
  10.0 0.7 copy.43
  11.0 0.7 add_bitcast_fusion
  11.7 58.4 %all-gather.1 = s32[128,2,24]{2,1,0:T(2,128)S(1)} all-gather(s32[1,2,24]{2,1,0:T(2,128)S(1)} %add_bitcast_fusion), channel_id=2, replica_groups=mesh['tok'=128,'rep'=4] {'tok'}, dimensions={0}, use_global_device_ids=true | all-gather | bytes 24768 | tf_op jit(solution)/shard_map/all_gather | solution.py:99
  70.2 0.2 fusion.2
  70.5 0.7 broadcast_in_dim_reshape_squeeze.4.ids_ref
  71.2 0.8 copy.41.vocab_ref
  72.0 1.9 %concatenate.16.head_ref = bf16[256,1024]{1,0:T(8,128)(2,1)} pad(bf16[251,1024]{1,0:T(8,128)(2,1)} %param.9, bf16[]{:T(256)} %constant.16.clone.1), padding=0_5x0_0 | pad | bytes 1038338 | tf_op jit(solution)/shard_map/concatenate | solution.py:38
  73.9 0.8 sqrt_reduce_fusion
  74.7 0.9 convert_reduce_fusion.1
  75.8 0.2 convert_reduce_fusion
  76.0 0.7 iota_compare_fusion.1
  76.7 26.8 %all-gather.4.cloned.1.call-done.rows_ref = bf16[3072,1024]{1,0:T(8,128)(2,1)} async-done(((bf16[24,1024]{1,0:T(8,128)(2,1)}), bf16[3072,1024]{1,0:T(8,128)(2,1)}) %all-gather.4.cloned.1.call-update) | async-done | bytes 6291472 | tf_op jit(solution)/shard_map/all_gather | solution.py:98
  103.5 5.6 %shard_map.95 = f32[8,3072]{1,0:T(8,128)} custom-call(bf16[256,1024]{1,0:T(8,128)(2,1)} %concatenate.16.head_ref, s32[256,1]{1,0:T(8,128)} %copy.41.vocab_ref, s32[1,3072]{1,0:T(1,128)} %broadcast_in_dim_reshape_squeeze.4.ids_ref, bf16[3072,1024]{1,0:T(8,128)(2,1)} %all-gather.4.cloned.1.call-done.rows_ref), custom_call_target="tpu_custom_call" | custom-call | flops 1610612736 | bytes 6926336 | tf_op jit(solution)/shard_map/pallas_call | solution.py:44
  109.2 1.2 slice_reduce_fusion.9
  111.0 0.3 select_reduce_fusion
  111.3 0.1 select_reduce_fusion.2
  111.5 0.3 copy.46
  111.8 0.7 reshape.189
  112.5 0.7 copy.48
  113.2 9.4 %all-to-all-start = ((f32[128,1,112]{2,1,0:T(1,128)}), f32[128,1,112]{2,1,0:T(1,128)S(1)}, u32[]{:S(2)}, u32[]{:S(2)}) async-start(f32[128,1,112]{2,1,0:T(1,128)} %copy.48), calls=%async_computation | async-start | bytes 131072 | tf_op jit(solution)/shard_map/all_to_all | solution.py:131
  122.8 0.2 dynamic-slice_reduce_fusion
  123.0 11.1 %all-to-all-done = f32[128,1,112]{2,1,0:T(1,128)S(1)} async-done(((f32[128,1,112]{2,1,0:T(1,128)}), f32[128,1,112]{2,1,0:T(1,128)S(1)}, u32[]{:S(2)}, u32[]{:S(2)}) %all-to-all-start) | async-done | bytes 57376 | tf_op jit(solution)/shard_map/all_to_all | solution.py:131
  134.2 0.3 fusion.3
  134.8 0.7 copy.54
  135.5 4.0 %all-to-all-start.1 = ((f32[4,2,2]{1,2,0:T(2,128)}), f32[4,2,2]{1,2,0:T(2,128)S(1)}, u32[]{:S(2)}, u32[]{:S(2)}) async-start(f32[4,2,2]{1,2,0:T(2,128)} %copy.54), calls=%async_computation.1 | async-start | bytes 8192 | tf_op jit(solution)/shard_map/all_to_all | solution.py:148
  139.5 0.1 reduce_max.47
  139.6 0.2 multiply_reduce_fusion
  139.8 0.5 compare_select_fusion
  140.3 3.3 %all-to-all-done.1 = f32[4,2,2]{1,2,0:T(2,128)S(1)} async-done(((f32[4,2,2]{1,2,0:T(2,128)}), f32[4,2,2]{1,2,0:T(2,128)S(1)}, u32[]{:S(2)}, u32[]{:S(2)}) %all-to-all-start.1) | async-done | bytes 96 | tf_op jit(solution)/shard_map/all_to_all | solution.py:148
  143.7 0.6 copy.55
  (37 shorter events, 1.6 us)
Async XLA Ops:
  7.2 96.4 %all-gather.4.cloned.1.call-start = ((), (), s32[]{:S(2)}) async-start(), calls=%async_computation.2 | async-start | bytes 6340608 | tf_op jit(solution)/shard_map/all_gather | solution.py:98
  11.0 128.8 %copy-start = (s32[24]{0:T(128)S(1)}, s32[24]{0:T(128)}, u32[]{:S(2)}) copy-start(s32[24]{0:T(128)} %param.12) | copy-start | bytes 292
  113.2 20.9 %all-to-all-start = ((f32[128,1,112]{2,1,0:T(1,128)}), f32[128,1,112]{2,1,0:T(1,128)S(1)}, u32[]{:S(2)}, u32[]{:S(2)}) async-start(f32[128,1,112]{2,1,0:T(1,128)} %copy.48), calls=%async_computation | async-start | bytes 131072 | tf_op jit(solution)/shard_map/all_to_all | solution.py:131
  135.5 8.1 %all-to-all-start.1 = ((f32[4,2,2]{1,2,0:T(2,128)}), f32[4,2,2]{1,2,0:T(2,128)S(1)}, u32[]{:S(2)}, u32[]{:S(2)}) async-start(f32[4,2,2]{1,2,0:T(2,128)} %copy.54), calls=%async_computation.1 | async-start | bytes 8192 | tf_op jit(solution)/shard_map/all_to_all | solution.py:148
Sparse Core Ops, SparseCore 0:
  11.1 92.3 all-gather.3

commit v12 on v11

--- a/solution.py
+++ b/solution.py
@@ -126,17 +126,17 @@
     req_norm = jnp.sum(jnp.where(slot_hot, part_norm[:, None, None], 0.0), axis=0)
     req = jnp.stack([req_max, req_norm], axis=2).reshape(tok_count, rep_count * SLOTS * 2)
 
-    stats = jnp.stack([top_p, total_p, moment_p, chosen_p], axis=2).reshape(tok_count, local_rows * 4)
+    stats = jnp.stack([top_p, total_p, moment_p, chosen_p], axis=1).reshape(tok_count, local_rows * 4)
     outgoing = jnp.concatenate([stats, req], axis=1)
     incoming = lax.all_to_all(outgoing, "tok", 0, 0, tiled=True)
 
-    in_stats = incoming[:, : local_rows * 4].reshape(tok_count, local_rows, 4)
-    tops = in_stats[:, :, 0]
+    in_stats = incoming[:, : local_rows * 4].reshape(tok_count, 4, local_rows)
+    tops = in_stats[:, 0, :]
     row_top = jnp.max(tops, axis=0)
     scale = jnp.exp(tops - row_top[None, :])
-    row_total = jnp.sum(in_stats[:, :, 1] * scale, axis=0)
-    row_moment = jnp.sum(in_stats[:, :, 2] * scale, axis=0)
-    row_chosen = jnp.sum(in_stats[:, :, 3], axis=0)
+    row_total = jnp.sum(in_stats[:, 1, :] * scale, axis=0)
+    row_moment = jnp.sum(in_stats[:, 2, :] * scale, axis=0)
+    row_chosen = jnp.sum(in_stats[:, 3, :], axis=0)
     log_total = jnp.log(row_total)
     logprob = jnp.where(live_row, row_chosen - row_top - log_total, 0.0)
     entropy = jnp.where(live_row, row_top + log_total - row_moment / row_total, 0.0)

time: 152 us -> 152 us (level)
  no operation moved by 1% of the time
where the time goes in v12:
time: 152 us; the launch traced here: 151 us
  blocking collectives  58.5 us (38%)
  waiting for transfers between devices  41.6 us (27%)
  between operations  14.2 us (9%)
  starting transfers between devices  13.5 us (9%)
  local copies, waits for them, and re-layouts  11.8 us (8%)
  Pallas kernels  7.14 us (5%)
  other arithmetic  4.63 us (3%)
    all_gather x1, blocking collectives, shards(): meta = lax.all_gather(jnp.stack([targets, padding_mask]), 'tok', axis=0)  58.5 us
    all_gather x1, waiting for transfers between devices, shards(): gathered = lax.all_gather(normed, 'tok', axis=0, tiled=True)  26.9 us
    all_to_all x1, waiting for transfers between devices, shards(): incoming = lax.all_to_all(outgoing, 'tok', 0, 0, tiled=True)  11.1 us
    all_to_all x1, starting transfers between devices, shards(): incoming = lax.all_to_all(outgoing, 'tok', 0, 0, tiled=True)  9.42 us
    pallas_call x1, Pallas kernels, slice_stats(): pl.pallas_call(stats_kernel, grid=(count // tile,), in_specs=[pl.BlockSpe...  5.62 us
    all_to_all x1, starting transfers between devices, shards(): got = lax.all_to_all(rep_pair, 'rep', 0, 0, tiled=True)  4 us
    all_to_all x1, waiting for transfers between devices, shards(): got = lax.all_to_all(rep_pair, 'rep', 0, 0, tiled=True)  3.61 us
  transfers between devices with their start and end apart: 3, of which 3 were waited for; matrix products, arithmetic and copies ran while one was open for 6% of the time, Pallas kernels for 0%

profile of v12, /device:TPU:1, one launch (start us, length us, event | category | flops | bytes accessed | tf_op | source)
XLA Modules:
  0.0 151.4 jit_solution(4028495775443936174)
XLA Ops:
  7.2 1.3 broadcast_in_dim.96.gain_ref
  8.5 1.5 %shard_map.94 = (bf16[24,1024]{1,0:T(8,128)(2,1)}, f32[24,128]{1,0:T(8,128)}) custom-call(bf16[24,1024]{1,0:T(8,128)(2,1)} %hidden_ref.1, bf16[1,1024]{1,0:T(2,128)(2,1)} %broadcast_in_dim.96.gain_ref), custom_call_target="tpu_custom_call" | custom-call | tf_op jit(solution)/shard_map/pallas_call | solution.py:75
  10.1 0.7 copy.43
  11.0 0.7 add_bitcast_fusion
  11.7 58.5 %all-gather.1 = s32[128,2,24]{2,1,0:T(2,128)S(1)} all-gather(s32[1,2,24]{2,1,0:T(2,128)S(1)} %add_bitcast_fusion), channel_id=2, replica_groups=mesh['tok'=128,'rep'=4] {'tok'}, dimensions={0}, use_global_device_ids=true | all-gather | bytes 24768 | tf_op jit(solution)/shard_map/all_gather | solution.py:99
  70.2 0.2 fusion.7
  70.5 0.7 broadcast_in_dim_reshape_squeeze.4.ids_ref
  71.2 0.8 copy.38.vocab_ref
  72.0 1.9 %concatenate.16.head_ref = bf16[256,1024]{1,0:T(8,128)(2,1)} pad(bf16[251,1024]{1,0:T(8,128)(2,1)} %param.9, bf16[]{:T(256)} %constant.16.clone.1), padding=0_5x0_0 | pad | bytes 1038338 | tf_op jit(solution)/shard_map/concatenate | solution.py:38
  73.9 0.8 sqrt_reduce_fusion
  74.7 0.9 convert_reduce_fusion.1
  75.8 0.2 convert_reduce_fusion
  76.0 0.7 iota_compare_fusion.1
  76.7 26.9 %all-gather.4.cloned.1.call-done.rows_ref = bf16[3072,1024]{1,0:T(8,128)(2,1)} async-done(((bf16[24,1024]{1,0:T(8,128)(2,1)}), bf16[3072,1024]{1,0:T(8,128)(2,1)}) %all-gather.4.cloned.1.call-update) | async-done | bytes 6291472 | tf_op jit(solution)/shard_map/all_gather | solution.py:98
  103.6 5.6 %shard_map.95 = f32[8,3072]{1,0:T(8,128)} custom-call(bf16[256,1024]{1,0:T(8,128)(2,1)} %concatenate.16.head_ref, s32[256,1]{1,0:T(8,128)} %copy.38.vocab_ref, s32[1,3072]{1,0:T(1,128)} %broadcast_in_dim_reshape_squeeze.4.ids_ref, bf16[3072,1024]{1,0:T(8,128)(2,1)} %all-gather.4.cloned.1.call-done.rows_ref), custom_call_target="tpu_custom_call" | custom-call | flops 1610612736 | bytes 6926336 | tf_op jit(solution)/shard_map/pallas_call | solution.py:44
  109.2 1.2 slice_reduce_fusion.10
  111.2 0.3 select_reduce_fusion
  111.5 0.1 select_reduce_fusion.2
  111.7 0.3 copy.46
  111.9 0.7 reshape.189
  112.7 0.7 copy.48
  113.4 9.4 %all-to-all-start = ((f32[128,1,112]{2,1,0:T(1,128)}), f32[128,1,112]{2,1,0:T(1,128)S(1)}, u32[]{:S(2)}, u32[]{:S(2)}) async-start(f32[128,1,112]{2,1,0:T(1,128)} %copy.48), calls=%async_computation | async-start | bytes 131072 | tf_op jit(solution)/shard_map/all_to_all | solution.py:131
  122.9 0.2 dynamic-slice_reduce_fusion
  123.2 11.1 %all-to-all-done = f32[128,1,112]{2,1,0:T(1,128)S(1)} async-done(((f32[128,1,112]{2,1,0:T(1,128)}), f32[128,1,112]{2,1,0:T(1,128)S(1)}, u32[]{:S(2)}, u32[]{:S(2)}) %all-to-all-start) | async-done | bytes 57376 | tf_op jit(solution)/shard_map/all_to_all | solution.py:131
  134.4 0.1 slice_reduce_fusion.7
  134.7 0.1 slice_reduce_fusion.5
  134.8 0.2 fusion.3
  135.0 0.7 copy.53
  135.7 4.0 %all-to-all-start.1 = ((f32[4,2,2]{1,2,0:T(2,128)}), f32[4,2,2]{1,2,0:T(2,128)S(1)}, u32[]{:S(2)}, u32[]{:S(2)}) async-start(f32[4,2,2]{1,2,0:T(2,128)} %copy.53), calls=%async_computation.1 | async-start | bytes 8192 | tf_op jit(solution)/shard_map/all_to_all | solution.py:148
  139.7 0.5 compare_select_fusion
  140.2 3.6 %all-to-all-done.1 = f32[4,2,2]{1,2,0:T(2,128)S(1)} async-done(((f32[4,2,2]{1,2,0:T(2,128)}), f32[4,2,2]{1,2,0:T(2,128)S(1)}, u32[]{:S(2)}, u32[]{:S(2)}) %all-to-all-start.1) | async-done | bytes 96 | tf_op jit(solution)/shard_map/all_to_all | solution.py:148
  143.9 0.6 copy.54
  (39 shorter events, 1.7 us)
Async XLA Ops:
  7.2 132.5 %copy-start = (s32[24]{0:T(128)S(1)}, s32[24]{0:T(128)}, u32[]{:S(2)}) copy-start(s32[24]{0:T(128)} %param.12) | copy-start | bytes 292
  7.2 96.4 %all-gather.4.cloned.1.call-start = ((), (), s32[]{:S(2)}) async-start(), calls=%async_computation.2 | async-start | bytes 6340608 | tf_op jit(solution)/shard_map/all_gather | solution.py:98
  113.4 20.9 %all-to-all-start = ((f32[128,1,112]{2,1,0:T(1,128)}), f32[128,1,112]{2,1,0:T(1,128)S(1)}, u32[]{:S(2)}, u32[]{:S(2)}) async-start(f32[128,1,112]{2,1,0:T(1,128)} %copy.48), calls=%async_computation | async-start | bytes 131072 | tf_op jit(solution)/shard_map/all_to_all | solution.py:131
  135.7 8.1 %all-to-all-start.1 = ((f32[4,2,2]{1,2,0:T(2,128)}), f32[4,2,2]{1,2,0:T(2,128)S(1)}, u32[]{:S(2)}, u32[]{:S(2)}) async-start(f32[4,2,2]{1,2,0:T(2,128)} %copy.53), calls=%async_computation.1 | async-start | bytes 8192 | tf_op jit(solution)/shard_map/all_to_all | solution.py:148
Sparse Core Ops, SparseCore 0:
  11.1 92.3 all-gather.3

commit v13 on v11

--- a/solution.py
+++ b/solution.py
@@ -3,6 +3,7 @@
 from jax import lax
 from jax.experimental import pallas as pl
 from jax.experimental.pallas import tpu as pltpu
+from jax.experimental.layout import Layout, with_layout_constraint
 from jax.sharding import PartitionSpec as P
 
 SLOTS = 2
@@ -127,7 +128,7 @@
     req = jnp.stack([req_max, req_norm], axis=2).reshape(tok_count, rep_count * SLOTS * 2)
 
     stats = jnp.stack([top_p, total_p, moment_p, chosen_p], axis=2).reshape(tok_count, local_rows * 4)
-    outgoing = jnp.concatenate([stats, req], axis=1)
+    outgoing = with_layout_constraint(jnp.concatenate([stats, req], axis=1), Layout((0, 1)))
     incoming = lax.all_to_all(outgoing, "tok", 0, 0, tiled=True)
 
     in_stats = incoming[:, : local_rows * 4].reshape(tok_count, local_rows, 4)

time: 152 us -> 152 us (level)
  no operation moved by 1% of the time
where the time goes in v13:
time: 152 us; the launch traced here: 151 us
  blocking collectives  58.4 us (38%)
  waiting for transfers between devices  41.3 us (27%)
  between operations  14.2 us (9%)
  starting transfers between devices  13.5 us (9%)
  local copies, waits for them, and re-layouts  11 us (7%)
  Pallas kernels  7.14 us (5%)
  other arithmetic  5.65 us (4%)
    all_gather x1, blocking collectives, shards(): meta = lax.all_gather(jnp.stack([targets, padding_mask]), 'tok', axis=0)  58.4 us
    all_gather x1, waiting for transfers between devices, shards(): gathered = lax.all_gather(normed, 'tok', axis=0, tiled=True)  26.8 us
    all_to_all x1, waiting for transfers between devices, shards(): incoming = lax.all_to_all(outgoing, 'tok', 0, 0, tiled=True)  11.1 us
    all_to_all x1, starting transfers between devices, shards(): incoming = lax.all_to_all(outgoing, 'tok', 0, 0, tiled=True)  9.44 us
    pallas_call x1, Pallas kernels, slice_stats(): pl.pallas_call(stats_kernel, grid=(count // tile,), in_specs=[pl.BlockSpe...  5.62 us
    all_to_all x1, starting transfers between devices, shards(): got = lax.all_to_all(rep_pair, 'rep', 0, 0, tiled=True)  4 us
    all_to_all x1, waiting for transfers between devices, shards(): got = lax.all_to_all(rep_pair, 'rep', 0, 0, tiled=True)  3.3 us
  transfers between devices with their start and end apart: 3, of which 3 were waited for; matrix products, arithmetic and copies ran while one was open for 6% of the time, Pallas kernels for 0%

profile of v13, /device:TPU:1, one launch (start us, length us, event | category | flops | bytes accessed | tf_op | source)
XLA Modules:
  0.0 151.2 jit_solution(3338442825178999086)
XLA Ops:
  7.2 1.3 broadcast_in_dim.96.gain_ref
  8.5 1.5 %shard_map.94 = (bf16[24,1024]{1,0:T(8,128)(2,1)}, f32[24,128]{1,0:T(8,128)}) custom-call(bf16[24,1024]{1,0:T(8,128)(2,1)} %hidden_ref.1, bf16[1,1024]{1,0:T(2,128)(2,1)} %broadcast_in_dim.96.gain_ref), custom_call_target="tpu_custom_call" | custom-call | tf_op jit(solution)/shard_map/pallas_call | solution.py:76
  10.0 0.7 copy.49
  11.0 0.7 add_bitcast_fusion
  11.7 58.4 %all-gather.1 = s32[128,2,24]{2,1,0:T(2,128)S(1)} all-gather(s32[1,2,24]{2,1,0:T(2,128)S(1)} %add_bitcast_fusion), channel_id=2, replica_groups=mesh['tok'=128,'rep'=4] {'tok'}, dimensions={0}, use_global_device_ids=true | all-gather | bytes 24768 | tf_op jit(solution)/shard_map/all_gather | solution.py:100
  70.2 0.2 fusion.2
  70.5 0.7 broadcast_in_dim_reshape_squeeze.4.ids_ref
  71.2 0.8 copy.47.vocab_ref
  72.0 1.9 %concatenate.16.head_ref = bf16[256,1024]{1,0:T(8,128)(2,1)} pad(bf16[251,1024]{1,0:T(8,128)(2,1)} %param.9, bf16[]{:T(256)} %constant.16.clone.1), padding=0_5x0_0 | pad | bytes 1038338 | tf_op jit(solution)/shard_map/concatenate | solution.py:39
  73.9 0.8 sqrt_reduce_fusion
  74.7 0.9 convert_reduce_fusion.1
  75.8 0.2 convert_reduce_fusion
  76.0 0.7 iota_compare_fusion.1
  76.7 26.8 %all-gather.4.cloned.1.call-done.rows_ref = bf16[3072,1024]{1,0:T(8,128)(2,1)} async-done(((bf16[24,1024]{1,0:T(8,128)(2,1)}), bf16[3072,1024]{1,0:T(8,128)(2,1)}) %all-gather.4.cloned.1.call-update) | async-done | bytes 6291472 | tf_op jit(solution)/shard_map/all_gather | solution.py:99
  103.5 5.6 %shard_map.95 = f32[8,3072]{1,0:T(8,128)} custom-call(bf16[256,1024]{1,0:T(8,128)(2,1)} %concatenate.16.head_ref, s32[256,1]{1,0:T(8,128)} %copy.47.vocab_ref, s32[1,3072]{1,0:T(1,128)} %broadcast_in_dim_reshape_squeeze.4.ids_ref, bf16[3072,1024]{1,0:T(8,128)(2,1)} %all-gather.4.cloned.1.call-done.rows_ref), custom_call_target="tpu_custom_call" | custom-call | flops 1610612736 | bytes 6926336 | tf_op jit(solution)/shard_map/pallas_call | solution.py:45
  109.2 1.2 slice_reduce_fusion.9
  111.1 0.3 select_reduce_fusion
  111.4 0.1 select_reduce_fusion.2
  111.6 0.3 copy.52
  111.9 0.7 reshape.189
  112.5 0.7 pad_maximum_fusion.1
  113.2 9.4 %all-to-all-start = ((f32[128,1,112]{2,1,0:T(1,128)}), f32[128,1,112]{2,1,0:T(1,128)S(1)}, u32[]{:S(2)}, u32[]{:S(2)}) async-start(f32[128,1,112]{2,1,0:T(1,128)} %bitcast.10), calls=%async_computation | async-start | bytes 131072 | tf_op jit(solution)/shard_map/all_to_all | solution.py:132
  122.8 0.2 dynamic-slice_reduce_fusion
  123.0 11.1 %all-to-all-done = f32[128,1,112]{2,1,0:T(1,128)S(1)} async-done(((f32[128,1,112]{2,1,0:T(1,128)}), f32[128,1,112]{2,1,0:T(1,128)S(1)}, u32[]{:S(2)}, u32[]{:S(2)}) %all-to-all-start) | async-done | bytes 57376 | tf_op jit(solution)/shard_map/all_to_all | solution.py:132
  134.2 0.3 fusion.3
  134.8 0.7 copy.60
  135.5 4.0 %all-to-all-start.1 = ((f32[4,2,2]{1,2,0:T(2,128)}), f32[4,2,2]{1,2,0:T(2,128)S(1)}, u32[]{:S(2)}, u32[]{:S(2)}) async-start(f32[4,2,2]{1,2,0:T(2,128)} %copy.60), calls=%async_computation.1 | async-start | bytes 8192 | tf_op jit(solution)/shard_map/all_to_all | solution.py:149
  139.5 0.1 reduce_max.47
  139.6 0.2 multiply_reduce_fusion
  139.8 0.5 compare_select_fusion
  140.3 3.3 %all-to-all-done.1 = f32[4,2,2]{1,2,0:T(2,128)S(1)} async-done(((f32[4,2,2]{1,2,0:T(2,128)}), f32[4,2,2]{1,2,0:T(2,128)S(1)}, u32[]{:S(2)}, u32[]{:S(2)}) %all-to-all-start.1) | async-done | bytes 96 | tf_op jit(solution)/shard_map/all_to_all | solution.py:149
  143.7 0.6 copy.61
  (36 shorter events, 1.7 us)
Async XLA Ops:
  7.2 96.4 %all-gather.4.cloned.1.call-start = ((), (), s32[]{:S(2)}) async-start(), calls=%async_computation.2 | async-start | bytes 6340608 | tf_op jit(solution)/shard_map/all_gather | solution.py:99
  11.0 128.8 %copy-start = (s32[24]{0:T(128)S(1)}, s32[24]{0:T(128)}, u32[]{:S(2)}) copy-start(s32[24]{0:T(128)} %param.12) | copy-start | bytes 292
  113.2 20.9 %all-to-all-start = ((f32[128,1,112]{2,1,0:T(1,128)}), f32[128,1,112]{2,1,0:T(1,128)S(1)}, u32[]{:S(2)}, u32[]{:S(2)}) async-start(f32[128,1,112]{2,1,0:T(1,128)} %bitcast.10), calls=%async_computation | async-start | bytes 131072 | tf_op jit(solution)/shard_map/all_to_all | solution.py:132
  135.5 8.1 %all-to-all-start.1 = ((f32[4,2,2]{1,2,0:T(2,128)}), f32[4,2,2]{1,2,0:T(2,128)S(1)}, u32[]{:S(2)}, u32[]{:S(2)}) async-start(f32[4,2,2]{1,2,0:T(2,128)} %copy.60), calls=%async_computation.1 | async-start | bytes 8192 | tf_op jit(solution)/shard_map/all_to_all | solution.py:149
Sparse Core Ops, SparseCore 0:
  11.1 92.3 all-gather.3

commit v14 on v13

--- a/solution.py
+++ b/solution.py
@@ -145,7 +145,7 @@
     in_req = incoming[:, local_rows * 4:].reshape(tok_count, rep_count, SLOTS, 2)
     rep_max = jnp.max(in_req[..., 0], axis=0)
     rep_norm = jnp.sum(in_req[..., 1], axis=0)
-    rep_pair = jnp.stack([rep_max, rep_norm], axis=2)
+    rep_pair = with_layout_constraint(jnp.stack([rep_max, rep_norm], axis=2), Layout((0, 1, 2)))
     got = lax.all_to_all(rep_pair, "rep", 0, 0, tiled=True)
     final_max = jnp.max(got[..., 0], axis=0)
     final_norm = jnp.sum(got[..., 1], axis=0)

time: 152 us -> 152 us (level)
  no operation moved by 1% of the time
where the time goes in v14:
time: 152 us; the launch traced here: 151 us
  blocking collectives  58.4 us (38%)
  waiting for transfers between devices  41.3 us (27%)
  between operations  14.2 us (9%)
  starting transfers between devices  13.5 us (9%)
  local copies, waits for them, and re-layouts  10.3 us (7%)
  Pallas kernels  7.14 us (5%)
  other arithmetic  6.46 us (4%)
    all_gather x1, blocking collectives, shards(): meta = lax.all_gather(jnp.stack([targets, padding_mask]), 'tok', axis=0)  58.4 us
    all_gather x1, waiting for transfers between devices, shards(): gathered = lax.all_gather(normed, 'tok', axis=0, tiled=True)  26.8 us
    all_to_all x1, waiting for transfers between devices, shards(): incoming = lax.all_to_all(outgoing, 'tok', 0, 0, tiled=True)  11.1 us
    all_to_all x1, starting transfers between devices, shards(): incoming = lax.all_to_all(outgoing, 'tok', 0, 0, tiled=True)  9.44 us
    pallas_call x1, Pallas kernels, slice_stats(): pl.pallas_call(stats_kernel, grid=(count // tile,), in_specs=[pl.BlockSpe...  5.62 us
    all_to_all x1, starting transfers between devices, shards(): got = lax.all_to_all(rep_pair, 'rep', 0, 0, tiled=True)  4 us
    all_to_all x1, waiting for transfers between devices, shards(): got = lax.all_to_all(rep_pair, 'rep', 0, 0, tiled=True)  3.3 us
  transfers between devices with their start and end apart: 3, of which 3 were waited for; matrix products, arithmetic and copies ran while one was open for 6% of the time, Pallas kernels for 0%

profile of v14, /device:TPU:1, one launch (start us, length us, event | category | flops | bytes accessed | tf_op | source)
XLA Modules:
  0.0 151.3 jit_solution(4142226113069190971)
XLA Ops:
  7.2 1.3 broadcast_in_dim.96.gain_ref
  8.5 1.5 %shard_map.94 = (bf16[24,1024]{1,0:T(8,128)(2,1)}, f32[24,128]{1,0:T(8,128)}) custom-call(bf16[24,1024]{1,0:T(8,128)(2,1)} %hidden_ref.1, bf16[1,1024]{1,0:T(2,128)(2,1)} %broadcast_in_dim.96.gain_ref), custom_call_target="tpu_custom_call" | custom-call | tf_op jit(solution)/shard_map/pallas_call | solution.py:76
  10.0 0.7 copy.54
  11.0 0.7 add_bitcast_fusion
  11.7 58.4 %all-gather.1 = s32[128,2,24]{2,1,0:T(2,128)S(1)} all-gather(s32[1,2,24]{2,1,0:T(2,128)S(1)} %add_bitcast_fusion), channel_id=2, replica_groups=mesh['tok'=128,'rep'=4] {'tok'}, dimensions={0}, use_global_device_ids=true | all-gather | bytes 24768 | tf_op jit(solution)/shard_map/all_gather | solution.py:100
  70.2 0.2 fusion.2
  70.5 0.7 broadcast_in_dim_reshape_squeeze.4.ids_ref
  71.2 0.8 copy.52.vocab_ref
  72.0 1.9 %concatenate.16.head_ref = bf16[256,1024]{1,0:T(8,128)(2,1)} pad(bf16[251,1024]{1,0:T(8,128)(2,1)} %param.9, bf16[]{:T(256)} %constant.16.clone.1), padding=0_5x0_0 | pad | bytes 1038338 | tf_op jit(solution)/shard_map/concatenate | solution.py:39
  73.9 0.8 sqrt_reduce_fusion
  74.7 0.9 convert_reduce_fusion.1
  75.8 0.2 convert_reduce_fusion
  76.0 0.7 iota_compare_fusion.1
  76.7 26.8 %all-gather.4.cloned.1.call-done.rows_ref = bf16[3072,1024]{1,0:T(8,128)(2,1)} async-done(((bf16[24,1024]{1,0:T(8,128)(2,1)}), bf16[3072,1024]{1,0:T(8,128)(2,1)}) %all-gather.4.cloned.1.call-update) | async-done | bytes 6291472 | tf_op jit(solution)/shard_map/all_gather | solution.py:99
  103.5 5.6 %shard_map.95 = f32[8,3072]{1,0:T(8,128)} custom-call(bf16[256,1024]{1,0:T(8,128)(2,1)} %concatenate.16.head_ref, s32[256,1]{1,0:T(8,128)} %copy.52.vocab_ref, s32[1,3072]{1,0:T(1,128)} %broadcast_in_dim_reshape_squeeze.4.ids_ref, bf16[3072,1024]{1,0:T(8,128)(2,1)} %all-gather.4.cloned.1.call-done.rows_ref), custom_call_target="tpu_custom_call" | custom-call | flops 1610612736 | bytes 6926336 | tf_op jit(solution)/shard_map/pallas_call | solution.py:45
  109.2 1.2 slice_reduce_fusion.9
  111.1 0.3 select_reduce_fusion
  111.4 0.1 select_reduce_fusion.2
  111.6 0.3 copy.57
  111.9 0.7 reshape.189
  112.5 0.7 pad_maximum_fusion.1
  113.2 9.4 %all-to-all-start = ((f32[128,1,112]{2,1,0:T(1,128)}), f32[128,1,112]{2,1,0:T(1,128)S(1)}, u32[]{:S(2)}, u32[]{:S(2)}) async-start(f32[128,1,112]{2,1,0:T(1,128)} %bitcast.10), calls=%async_computation | async-start | bytes 131072 | tf_op jit(solution)/shard_map/all_to_all | solution.py:132
  122.8 0.2 dynamic-slice_reduce_fusion
  123.0 11.1 %all-to-all-done = f32[128,1,112]{2,1,0:T(1,128)S(1)} async-done(((f32[128,1,112]{2,1,0:T(1,128)}), f32[128,1,112]{2,1,0:T(1,128)S(1)}, u32[]{:S(2)}, u32[]{:S(2)}) %all-to-all-start) | async-done | bytes 57376 | tf_op jit(solution)/shard_map/all_to_all | solution.py:132
  134.2 0.3 fusion.3
  134.8 0.7 pad_maximum_fusion.3
  135.5 4.0 %all-to-all-start.1 = ((f32[4,2,2]{2,1,0:T(2,128)}), f32[4,2,2]{2,1,0:T(2,128)S(1)}, u32[]{:S(2)}, u32[]{:S(2)}) async-start(f32[4,2,2]{2,1,0:T(2,128)} %pad_maximum_fusion.3), calls=%async_computation.1 | async-start | bytes 8192 | tf_op jit(solution)/shard_map/all_to_all | solution.py:149
  139.6 0.2 multiply_reduce_fusion
  139.8 0.5 compare_select_fusion
  140.3 3.3 %all-to-all-done.1 = f32[4,2,2]{2,1,0:T(2,128)S(1)} async-done(((f32[4,2,2]{2,1,0:T(2,128)}), f32[4,2,2]{2,1,0:T(2,128)S(1)}, u32[]{:S(2)}, u32[]{:S(2)}) %all-to-all-start.1) | async-done | bytes 96 | tf_op jit(solution)/shard_map/all_to_all | solution.py:149
  143.6 0.2 slice_reduce_fusion.6
  143.8 0.7 copy.67
  (35 shorter events, 1.8 us)
Async XLA Ops:
  7.2 96.4 %all-gather.4.cloned.1.call-start = ((), (), s32[]{:S(2)}) async-start(), calls=%async_computation.2 | async-start | bytes 6340608 | tf_op jit(solution)/shard_map/all_gather | solution.py:99
  11.0 128.8 %copy-start = (s32[24]{0:T(128)S(1)}, s32[24]{0:T(128)}, u32[]{:S(2)}) copy-start(s32[24]{0:T(128)} %param.12) | copy-start | bytes 292
  113.2 20.9 %all-to-all-start = ((f32[128,1,112]{2,1,0:T(1,128)}), f32[128,1,112]{2,1,0:T(1,128)S(1)}, u32[]{:S(2)}, u32[]{:S(2)}) async-start(f32[128,1,112]{2,1,0:T(1,128)} %bitcast.10), calls=%async_computation | async-start | bytes 131072 | tf_op jit(solution)/shard_map/all_to_all | solution.py:132
  135.5 8.1 %all-to-all-start.1 = ((f32[4,2,2]{2,1,0:T(2,128)}), f32[4,2,2]{2,1,0:T(2,128)S(1)}, u32[]{:S(2)}, u32[]{:S(2)}) async-start(f32[4,2,2]{2,1,0:T(2,128)} %pad_maximum_fusion.3), calls=%async_computation.1 | async-start | bytes 8192 | tf_op jit(solution)/shard_map/all_to_all | solution.py:149
Sparse Core Ops, SparseCore 0:
  11.1 92.3 all-gather.3

commit v15 on v13

--- a/solution.py
+++ b/solution.py
@@ -13,7 +13,7 @@
 NEG_FILL = -1e30
 
 
-TILE = 1536
+TILE = 3072
 VOCAB_PAD = 256
 
 

time: 152 us -> 152 us (level)
  no operation moved by 1% of the time
where the time goes in v15:
time: 152 us
  blocking collectives  58.4 us (38%)
  waiting for transfers between devices  41.3 us (27%)
  between operations  14.2 us (9%)
  starting transfers between devices  13.5 us (9%)
  local copies, waits for them, and re-layouts  11 us (7%)
  Pallas kernels  7.97 us (5%)
  other arithmetic  5.65 us (4%)
    all_gather x1, blocking collectives, shards(): meta = lax.all_gather(jnp.stack([targets, padding_mask]), 'tok', axis=0)  58.4 us
    all_gather x1, waiting for transfers between devices, shards(): gathered = lax.all_gather(normed, 'tok', axis=0, tiled=True)  26.8 us
    all_to_all x1, waiting for transfers between devices, shards(): incoming = lax.all_to_all(outgoing, 'tok', 0, 0, tiled=True)  11.1 us
    all_to_all x1, starting transfers between devices, shards(): incoming = lax.all_to_all(outgoing, 'tok', 0, 0, tiled=True)  9.44 us
    pallas_call x1, Pallas kernels, slice_stats(): pl.pallas_call(stats_kernel, grid=(count // tile,), in_specs=[pl.BlockSpe...  6.45 us
    all_to_all x1, starting transfers between devices, shards(): got = lax.all_to_all(rep_pair, 'rep', 0, 0, tiled=True)  4 us
    all_to_all x1, waiting for transfers between devices, shards(): got = lax.all_to_all(rep_pair, 'rep', 0, 0, tiled=True)  3.3 us
  transfers between devices with their start and end apart: 3, of which 3 were waited for; matrix products, arithmetic and copies ran while one was open for 6% of the time, Pallas kernels for 0%

profile of v15, /device:TPU:1, one launch (start us, length us, event | category | flops | bytes accessed | tf_op | source)
XLA Modules:
  0.0 152.0 jit_solution(17385380680975561628)
XLA Ops:
  7.2 1.3 broadcast_in_dim.96.gain_ref
  8.5 1.5 shard_map.94
  10.0 0.7 copy.49
  11.0 0.7 add_bitcast_fusion
  11.7 58.4 %all-gather.1 = s32[128,2,24]{2,1,0:T(2,128)S(1)} all-gather(s32[1,2,24]{2,1,0:T(2,128)S(1)} %add_bitcast_fusion), channel_id=2, replica_groups=mesh['tok'=128,'rep'=4] {'tok'}, dimensions={0}, use_global_device_ids=true | all-gather | bytes 24768 | tf_op jit(solution)/shard_map/all_gather | solution.py:100
  70.2 0.2 fusion.2
  70.5 0.7 broadcast_in_dim_reshape_squeeze.4.ids_ref
  71.2 0.8 copy.47.vocab_ref
  72.0 1.9 %concatenate.16.head_ref = bf16[256,1024]{1,0:T(8,128)(2,1)} pad(bf16[251,1024]{1,0:T(8,128)(2,1)} %param.9, bf16[]{:T(256)} %constant.16.clone.1), padding=0_5x0_0 | pad | bytes 1038338 | tf_op jit(solution)/shard_map/concatenate | solution.py:39
  73.9 0.8 sqrt_reduce_fusion
  74.7 0.9 convert_reduce_fusion.1
  75.8 0.2 convert_reduce_fusion
  76.0 0.7 iota_compare_fusion.1
  76.7 26.8 %all-gather.4.cloned.1.call-done.rows_ref = bf16[3072,1024]{1,0:T(8,128)(2,1)} async-done(((bf16[24,1024]{1,0:T(8,128)(2,1)}), bf16[3072,1024]{1,0:T(8,128)(2,1)}) %all-gather.4.cloned.1.call-update) | async-done | bytes 6291472 | tf_op jit(solution)/shard_map/all_gather | solution.py:99
  103.5 6.4 %shard_map.95 = f32[8,3072]{1,0:T(8,128)} custom-call(bf16[256,1024]{1,0:T(8,128)(2,1)} %concatenate.16.head_ref, s32[256,1]{1,0:T(8,128)} %copy.47.vocab_ref, s32[1,3072]{1,0:T(1,128)} %broadcast_in_dim_reshape_squeeze.4.ids_ref, bf16[3072,1024]{1,0:T(8,128)(2,1)} %all-gather.4.cloned.1.call-done.rows_ref), custom_call_target="tpu_custom_call" | custom-call | flops 1610612736 | bytes 6926336 | tf_op jit(solution)/shard_map/pallas_call | solution.py:45
  110.0 1.2 slice_reduce_fusion.9
  112.0 0.3 select_reduce_fusion
  112.3 0.1 select_reduce_fusion.2
  112.4 0.3 copy.52
  112.7 0.7 reshape.189
  113.3 0.7 pad_maximum_fusion.1
  114.1 9.4 %all-to-all-start = ((f32[128,1,112]{2,1,0:T(1,128)}), f32[128,1,112]{2,1,0:T(1,128)S(1)}, u32[]{:S(2)}, u32[]{:S(2)}) async-start(f32[128,1,112]{2,1,0:T(1,128)} %bitcast.10), calls=%async_computation | async-start | bytes 131072 | tf_op jit(solution)/shard_map/all_to_all | solution.py:132
  123.6 0.2 dynamic-slice_reduce_fusion
  123.8 11.1 %all-to-all-done = f32[128,1,112]{2,1,0:T(1,128)S(1)} async-done(((f32[128,1,112]{2,1,0:T(1,128)}), f32[128,1,112]{2,1,0:T(1,128)S(1)}, u32[]{:S(2)}, u32[]{:S(2)}) %all-to-all-start) | async-done | bytes 57376 | tf_op jit(solution)/shard_map/all_to_all | solution.py:132
  135.1 0.3 fusion.3
  135.6 0.7 copy.60
  136.3 4.0 %all-to-all-start.1 = ((f32[4,2,2]{1,2,0:T(2,128)}), f32[4,2,2]{1,2,0:T(2,128)S(1)}, u32[]{:S(2)}, u32[]{:S(2)}) async-start(f32[4,2,2]{1,2,0:T(2,128)} %copy.60), calls=%async_computation.1 | async-start | bytes 8192 | tf_op jit(solution)/shard_map/all_to_all | solution.py:149
  140.3 0.1 reduce_max.47
  140.4 0.2 multiply_reduce_fusion
  140.6 0.5 compare_select_fusion
  141.1 3.3 %all-to-all-done.1 = f32[4,2,2]{1,2,0:T(2,128)S(1)} async-done(((f32[4,2,2]{1,2,0:T(2,128)}), f32[4,2,2]{1,2,0:T(2,128)S(1)}, u32[]{:S(2)}, u32[]{:S(2)}) %all-to-all-start.1) | async-done | bytes 96 | tf_op jit(solution)/shard_map/all_to_all | solution.py:149
  144.5 0.6 copy.61
  (36 shorter events, 1.7 us)
Async XLA Ops:
  7.2 96.4 %all-gather.4.cloned.1.call-start = ((), (), s32[]{:S(2)}) async-start(), calls=%async_computation.2 | async-start | bytes 6340608 | tf_op jit(solution)/shard_map/all_gather | solution.py:99
  11.0 129.6 %copy-start = (s32[24]{0:T(128)S(1)}, s32[24]{0:T(128)}, u32[]{:S(2)}) copy-start(s32[24]{0:T(128)} %param.12) | copy-start | bytes 292
  114.1 20.9 %all-to-all-start = ((f32[128,1,112]{2,1,0:T(1,128)}), f32[128,1,112]{2,1,0:T(1,128)S(1)}, u32[]{:S(2)}, u32[]{:S(2)}) async-start(f32[128,1,112]{2,1,0:T(1,128)} %bitcast.10), calls=%async_computation | async-start | bytes 131072 | tf_op jit(solution)/shard_map/all_to_all | solution.py:132
  136.3 8.1 %all-to-all-start.1 = ((f32[4,2,2]{1,2,0:T(2,128)}), f32[4,2,2]{1,2,0:T(2,128)S(1)}, u32[]{:S(2)}, u32[]{:S(2)}) async-start(f32[4,2,2]{1,2,0:T(2,128)} %copy.60), calls=%async_computation.1 | async-start | bytes 8192 | tf_op jit(solution)/shard_map/all_to_all | solution.py:149
Sparse Core Ops, SparseCore 0:
  11.1 92.3 all-gather.3

commit v16 on v15

--- a/solution.py
+++ b/solution.py
@@ -13,7 +13,7 @@
 NEG_FILL = -1e30
 
 
-TILE = 3072
+TILE = 1024
 VOCAB_PAD = 256
 
 

time: 152 us -> 152 us (level)
  no operation moved by 1% of the time
where the time goes in v16:
time: 152 us
  blocking collectives  58.4 us (38%)
  waiting for transfers between devices  41.3 us (27%)
  between operations  14.2 us (9%)
  starting transfers between devices  13.5 us (9%)
  local copies, waits for them, and re-layouts  11 us (7%)
  Pallas kernels  7.54 us (5%)
  other arithmetic  5.65 us (4%)
    all_gather x1, blocking collectives, shards(): meta = lax.all_gather(jnp.stack([targets, padding_mask]), 'tok', axis=0)  58.4 us
    all_gather x1, waiting for transfers between devices, shards(): gathered = lax.all_gather(normed, 'tok', axis=0, tiled=True)  26.8 us
    all_to_all x1, waiting for transfers between devices, shards(): incoming = lax.all_to_all(outgoing, 'tok', 0, 0, tiled=True)  11.1 us
    all_to_all x1, starting transfers between devices, shards(): incoming = lax.all_to_all(outgoing, 'tok', 0, 0, tiled=True)  9.44 us
    pallas_call x1, Pallas kernels, slice_stats(): pl.pallas_call(stats_kernel, grid=(count // tile,), in_specs=[pl.BlockSpe...  6.02 us
    all_to_all x1, starting transfers between devices, shards(): got = lax.all_to_all(rep_pair, 'rep', 0, 0, tiled=True)  3.99 us
    all_to_all x1, waiting for transfers between devices, shards(): got = lax.all_to_all(rep_pair, 'rep', 0, 0, tiled=True)  3.3 us
  transfers between devices with their start and end apart: 3, of which 3 were waited for; matrix products, arithmetic and copies ran while one was open for 6% of the time, Pallas kernels for 0%

profile of v16, /device:TPU:1, one launch (start us, length us, event | category | flops | bytes accessed | tf_op | source)
XLA Modules:
  0.0 151.6 jit_solution(5618113428849550937)
XLA Ops:
  7.2 1.3 broadcast_in_dim.96.gain_ref
  8.5 1.5 %shard_map.94 = (bf16[24,1024]{1,0:T(8,128)(2,1)}, f32[24,128]{1,0:T(8,128)}) custom-call(bf16[24,1024]{1,0:T(8,128)(2,1)} %hidden_ref.1, bf16[1,1024]{1,0:T(2,128)(2,1)} %broadcast_in_dim.96.gain_ref), custom_call_target="tpu_custom_call" | custom-call | tf_op jit(solution)/shard_map/pallas_call | solution.py:76
  10.0 0.7 copy.49
  11.0 0.7 add_bitcast_fusion
  11.7 58.4 %all-gather.1 = s32[128,2,24]{2,1,0:T(2,128)S(1)} all-gather(s32[1,2,24]{2,1,0:T(2,128)S(1)} %add_bitcast_fusion), channel_id=2, replica_groups=mesh['tok'=128,'rep'=4] {'tok'}, dimensions={0}, use_global_device_ids=true | all-gather | bytes 24768 | tf_op jit(solution)/shard_map/all_gather | solution.py:100
  70.2 0.2 fusion.2
  70.5 0.7 broadcast_in_dim_reshape_squeeze.4.ids_ref
  71.2 0.8 copy.47.vocab_ref
  72.0 1.9 %concatenate.16.head_ref = bf16[256,1024]{1,0:T(8,128)(2,1)} pad(bf16[251,1024]{1,0:T(8,128)(2,1)} %param.9, bf16[]{:T(256)} %constant.16.clone.1), padding=0_5x0_0 | pad | bytes 1038338 | tf_op jit(solution)/shard_map/concatenate | solution.py:39
  73.9 0.8 sqrt_reduce_fusion
  74.7 0.9 convert_reduce_fusion.1
  75.8 0.2 convert_reduce_fusion
  76.0 0.7 iota_compare_fusion.1
  76.7 26.8 %all-gather.4.cloned.1.call-done.rows_ref = bf16[3072,1024]{1,0:T(8,128)(2,1)} async-done(((bf16[24,1024]{1,0:T(8,128)(2,1)}), bf16[3072,1024]{1,0:T(8,128)(2,1)}) %all-gather.4.cloned.1.call-update) | async-done | bytes 6291472 | tf_op jit(solution)/shard_map/all_gather | solution.py:99
  103.5 6.0 %shard_map.95 = f32[8,3072]{1,0:T(8,128)} custom-call(bf16[256,1024]{1,0:T(8,128)(2,1)} %concatenate.16.head_ref, s32[256,1]{1,0:T(8,128)} %copy.47.vocab_ref, s32[1,3072]{1,0:T(1,128)} %broadcast_in_dim_reshape_squeeze.4.ids_ref, bf16[3072,1024]{1,0:T(8,128)(2,1)} %all-gather.4.cloned.1.call-done.rows_ref), custom_call_target="tpu_custom_call" | custom-call | flops 1610612736 | bytes 6926336 | tf_op jit(solution)/shard_map/pallas_call | solution.py:45
  109.5 1.2 slice_reduce_fusion.9
  111.5 0.3 select_reduce_fusion
  111.8 0.1 select_reduce_fusion.2
  112.0 0.3 copy.52
  112.3 0.7 reshape.189
  112.9 0.7 pad_maximum_fusion.1
  113.6 9.4 %all-to-all-start = ((f32[128,1,112]{2,1,0:T(1,128)}), f32[128,1,112]{2,1,0:T(1,128)S(1)}, u32[]{:S(2)}, u32[]{:S(2)}) async-start(f32[128,1,112]{2,1,0:T(1,128)} %bitcast.10), calls=%async_computation | async-start | bytes 131072 | tf_op jit(solution)/shard_map/all_to_all | solution.py:132
  123.2 0.2 dynamic-slice_reduce_fusion
  123.4 11.1 %all-to-all-done = f32[128,1,112]{2,1,0:T(1,128)S(1)} async-done(((f32[128,1,112]{2,1,0:T(1,128)}), f32[128,1,112]{2,1,0:T(1,128)S(1)}, u32[]{:S(2)}, u32[]{:S(2)}) %all-to-all-start) | async-done | bytes 57376 | tf_op jit(solution)/shard_map/all_to_all | solution.py:132
  134.6 0.3 fusion.3
  135.2 0.7 copy.60
  135.9 4.0 %all-to-all-start.1 = ((f32[4,2,2]{1,2,0:T(2,128)}), f32[4,2,2]{1,2,0:T(2,128)S(1)}, u32[]{:S(2)}, u32[]{:S(2)}) async-start(f32[4,2,2]{1,2,0:T(2,128)} %copy.60), calls=%async_computation.1 | async-start | bytes 8192 | tf_op jit(solution)/shard_map/all_to_all | solution.py:149
  139.9 0.1 reduce_max.47
  140.0 0.2 multiply_reduce_fusion
  140.2 0.5 compare_select_fusion
  140.7 3.3 %all-to-all-done.1 = f32[4,2,2]{1,2,0:T(2,128)S(1)} async-done(((f32[4,2,2]{1,2,0:T(2,128)}), f32[4,2,2]{1,2,0:T(2,128)S(1)}, u32[]{:S(2)}, u32[]{:S(2)}) %all-to-all-start.1) | async-done | bytes 96 | tf_op jit(solution)/shard_map/all_to_all | solution.py:149
  144.1 0.6 copy.61
  (36 shorter events, 1.7 us)
Async XLA Ops:
  7.2 96.4 %all-gather.4.cloned.1.call-start = ((), (), s32[]{:S(2)}) async-start(), calls=%async_computation.2 | async-start | bytes 6340608 | tf_op jit(solution)/shard_map/all_gather | solution.py:99
  11.0 129.2 %copy-start = (s32[24]{0:T(128)S(1)}, s32[24]{0:T(128)}, u32[]{:S(2)}) copy-start(s32[24]{0:T(128)} %param.12) | copy-start | bytes 292
  113.6 20.9 %all-to-all-start = ((f32[128,1,112]{2,1,0:T(1,128)}), f32[128,1,112]{2,1,0:T(1,128)S(1)}, u32[]{:S(2)}, u32[]{:S(2)}) async-start(f32[128,1,112]{2,1,0:T(1,128)} %bitcast.10), calls=%async_computation | async-start | bytes 131072 | tf_op jit(solution)/shard_map/all_to_all | solution.py:132
  135.9 8.1 %all-to-all-start.1 = ((f32[4,2,2]{1,2,0:T(2,128)}), f32[4,2,2]{1,2,0:T(2,128)S(1)}, u32[]{:S(2)}, u32[]{:S(2)}) async-start(f32[4,2,2]{1,2,0:T(2,128)} %copy.60), calls=%async_computation.1 | async-start | bytes 8192 | tf_op jit(solution)/shard_map/all_to_all | solution.py:149
Sparse Core Ops, SparseCore 0:
  11.1 92.3 all-gather.3
